TPU v7x, 1024 devices: a whole 4x4x32 slice. The times are simulated.
1024 devices in a mesh: gx: 32 (over y, x, core), gy: 32 (over z).
Axes of the slice: x: 4, y: 4, z: 32, core: 2. Of those that a mesh axis runs over, the one named last changes fastest.
Arguments:
- velocity: float32 [3, 256, 256, 128], P(None, 'gx', 'gy'), may hold values from -6 to 6
- stress: float32 [6, 256, 256, 128], P(None, 'gx', 'gy'), may hold values from -6 to 6
- buoyancy: float32 [256, 256, 128], P('gx', 'gy'), may hold values from 0.25 to 0.5
- lame_lambda: float32 [256, 256, 128], P('gx', 'gy'), may hold values from 0.05 to 0.2
- lame_mu: float32 [256, 256, 128], P('gx', 'gy'), may hold values from 0.1 to 0.25
- rate_exponent: int32 [32, 32], P('gx', 'gy'), may hold values from 0 to 2
Outputs:
- velocity_out: float32 [3, 256, 256, 128], P(None, 'gx', 'gy')
- stress_out: float32 [6, 256, 256, 128], P(None, 'gx', 'gy')
All inputs are finite; a program needn't handle non-finite values.
Results may differ from a plain program's by a relative error of at most 0.00002.
Values sent between devices are 32-bit elements; how exact they have to be, the bound alone decides.
No kernel may reach another device: no remote copies, remote signals or barrier semaphores. Data moves between devices by JAX's collectives and lax.ppermute only.
A program may use at most 32 MiB of HBM per device.

v0:
```python
import jax
import jax.numpy as jnp
from jax import lax
from jax.sharding import PartitionSpec as P

TILE = 8
COARSE = 2


def with_halo(cells, sides, width):
    for axis, dim in sides:
        count = lax.axis_size(axis)
        ends = count - 1
        head = lax.slice_in_dim(cells, 0, width, axis=dim)
        tail = lax.slice_in_dim(cells, cells.shape[dim] - width, cells.shape[dim], axis=dim)
        cells = jnp.concatenate(
            [
                lax.ppermute(tail, axis, [(i, (i + 1) % count) for i in range(ends)]),
                cells,
                lax.ppermute(head, axis, [((i + 1) % count, i) for i in range(ends)]),
            ],
            axis=dim,
        )
    return cells


def expand_levels(rate_exponent):
    cells = jnp.repeat(jnp.repeat(rate_exponent, TILE, axis=0), TILE, axis=1)
    return cells[:, :, None]


def level_scale(exponent):
    return jnp.where(exponent == 2, 0.25, jnp.where(exponent == 1, 0.5, 1.0)).astype(jnp.float32)


def substep_active(exponent, sub):
    odd_sub = sub % 2 == 1
    last_sub = sub == 3
    return (exponent == 2) | (exponent == 1) & odd_sub | (exponent >= 0) & last_sub


def centre(field):
    return field[1:-1, 1:-1]


def plus_x(field):
    return field[2:, 1:-1]


def minus_x(field):
    return field[:-2, 1:-1]


def plus_y(field):
    return field[1:-1, 2:]


def minus_y(field):
    return field[1:-1, :-2]


def z_forward(field):
    return jnp.concatenate([field[..., 1:], jnp.zeros_like(field[..., :1])], axis=-1) - field


def z_backward(field):
    return field - jnp.concatenate([jnp.zeros_like(field[..., :1]), field[..., :-1]], axis=-1)


def velocity_forces(padded, stress_zz):
    stress_xx, stress_yy, stress_xy, stress_xz, stress_yz = (
        padded[0],
        padded[1],
        padded[2],
        padded[3],
        padded[4],
    )
    force_x = (
        plus_x(stress_xx)
        - centre(stress_xx)
        + (centre(stress_xy) - minus_y(stress_xy))
        + z_backward(centre(stress_xz))
    )
    force_y = (
        centre(stress_xy)
        - minus_x(stress_xy)
        + (plus_y(stress_yy) - centre(stress_yy))
        + z_backward(centre(stress_yz))
    )
    force_z = (
        centre(stress_xz)
        - minus_x(stress_xz)
        + (centre(stress_yz) - minus_y(stress_yz))
        + z_forward(stress_zz)
    )
    return jnp.stack([force_x, force_y, force_z])


def advance_velocity(velocity, forces, push_coef, active):
    return jnp.where(active, velocity + push_coef * forces, velocity)


def advance_stress(stress, vel_padded, lam_coef, shear_coef, active):
    vel_x, vel_y, vel_z = (vel_padded[0], vel_padded[1], vel_padded[2])
    strain_x = centre(vel_x) - minus_x(vel_x)
    strain_y = centre(vel_y) - minus_y(vel_y)
    strain_z = z_backward(centre(vel_z))
    shear_xy = plus_y(vel_x) - centre(vel_x) + (plus_x(vel_y) - centre(vel_y))
    shear_xz = z_forward(centre(vel_x)) + (plus_x(vel_z) - centre(vel_z))
    shear_yz = z_forward(centre(vel_y)) + (plus_y(vel_z) - centre(vel_z))
    trace_sum = strain_x + strain_y + strain_z
    two_shear = 2.0 * shear_coef
    fresh = jnp.stack(
        [
            stress[0] + (lam_coef * trace_sum + two_shear * strain_x),
            stress[1] + (lam_coef * trace_sum + two_shear * strain_y),
            stress[2] + shear_coef * shear_xy,
            stress[3] + shear_coef * shear_xz,
            stress[4] + shear_coef * shear_yz,
            stress[5] + (lam_coef * trace_sum + two_shear * strain_z),
        ]
    )
    return jnp.where(active, fresh, stress)


def stress_faces(fields):
    return with_halo(fields, (("gx", 1), ("gy", 2)), 1)


def velocity_faces(fields):
    return with_halo(fields, (("gx", 1), ("gy", 2)), 1)


def per_device(velocity, stress, buoyancy, lame_lambda, lame_mu, rate_exponent):
    exponent = expand_levels(rate_exponent)
    scale = level_scale(exponent)
    push_coef = buoyancy * scale
    lam_coef = lame_lambda * scale
    shear_coef = lame_mu * scale
    for step in range(COARSE):
        for sub in range(4):
            active = substep_active(exponent, sub)
            padded = stress_faces(stress[:5])
            previous = velocity
            stress_now = stress
            velocity = advance_velocity(
                previous, velocity_forces(padded, stress_now[5]), push_coef, active
            )
            vel_padded = velocity_faces(velocity)
            stress = advance_stress(stress_now, vel_padded, lam_coef, shear_coef, active)
    return (velocity, stress)


def solution(mesh):
    in_specs = (
        P(None, "gx", "gy", None),
        P(None, "gx", "gy", None),
        P("gx", "gy", None),
        P("gx", "gy", None),
        P("gx", "gy", None),
        P("gx", "gy"),
    )
    out_specs = (P(None, "gx", "gy", None), P(None, "gx", "gy", None))
    return jax.shard_map(
        per_device, mesh=mesh, in_specs=in_specs, out_specs=out_specs, check_vma=False
    )
```

profile of v0, /device:TPU:7, one launch (start us, length us, event | category | flops | bytes accessed | tf_op | source)
XLA Modules:
  0.0 321.0 jit_solution(12617312344620317958)
XLA Ops:
  1.4 3.7 %collective-permute-start = (f32[5,1,8,128]{3,2,1,0:T(8,128)S(1)}, f32[5,1,8,128]{3,2,1,0:T(8,128)S(1)}, u32[]{:S(2)}, u32[]{:S(2)}) collective-permute-start(f32[5,1,8,128]{3,2,1,0:T(8,128)S(1)} %get-tuple-element.112), channel_id=1, source_target_pairs={{0,32},{32,64},{64,96},{96,128},{128,160},{160,192},{192,224},{224... | collective-permute-start | bytes 61448 | tf_op jit(solution)/shard_map/ppermute | solution.py:18
  9.4 2.9 collective-permute-done.1
  12.3 3.5 %collective-permute-start.2 = (f32[5,10,1,128]{3,2,1,0:T(1,128)S(1)}, f32[5,10,1,128]{3,2,1,0:T(1,128)S(1)}, u32[]{:S(2)}, u32[]{:S(2)}) collective-permute-start(f32[5,10,1,128]{3,2,1,0:T(1,128)S(1)} %get-tuple-element.96), channel_id=1, source_target_pairs={{0,1},{1,2},{2,3},{3,4},{4,5},{5,6},{6,7},{7,8},{8,9},{9,10},{10,1... | collective-permute-start | bytes 76808 | tf_op jit(solution)/shard_map/ppermute | solution.py:18
  17.3 3.4 %collective-permute-done.3 = f32[5,10,1,128]{3,2,1,0:T(1,128)S(1)} collective-permute-done((f32[5,10,1,128]{3,2,1,0:T(1,128)S(1)}, f32[5,10,1,128]{3,2,1,0:T(1,128)S(1)}, u32[]{:S(2)}, u32[]{:S(2)}) %collective-permute-start.3) | collective-permute-done | bytes 25632 | tf_op jit(solution)/shard_map/ppermute | solution.py:20
  22.6 4.1 %collective-permute-start.4 = (f32[3,1,8,128]{3,2,1,0:T(8,128)S(1)}, f32[3,1,8,128]{3,2,1,0:T(8,128)S(1)}, u32[]{:S(2)}, u32[]{:S(2)}) collective-permute-start(f32[3,1,8,128]{3,2,1,0:T(8,128)S(1)} %get-tuple-element.144), channel_id=1, source_target_pairs={{0,32},{32,64},{64,96},{96,128},{128,160},{160,192},{192,224},{224... | collective-permute-start | bytes 36872 | tf_op jit(solution)/shard_map/ppermute | solution.py:18
  28.6 5.2 %collective-permute-done.5 = f32[3,1,8,128]{3,2,1,0:T(8,128)S(1)} collective-permute-done((f32[3,1,8,128]{3,2,1,0:T(8,128)S(1)}, f32[3,1,8,128]{3,2,1,0:T(8,128)S(1)}, u32[]{:S(2)}, u32[]{:S(2)}) %collective-permute-start.5) | collective-permute-done | bytes 12320 | tf_op jit(solution)/shard_map/ppermute | solution.py:20
  33.8 3.5 %collective-permute-start.6 = (f32[3,10,1,128]{3,2,1,0:T(1,128)S(1)}, f32[3,10,1,128]{3,2,1,0:T(1,128)S(1)}, u32[]{:S(2)}, u32[]{:S(2)}) collective-permute-start(f32[3,10,1,128]{3,2,1,0:T(1,128)S(1)} %get-tuple-element.128), channel_id=1, source_target_pairs={{0,1},{1,2},{2,3},{3,4},{4,5},{5,6},{6,7},{7,8},{8,9},{9,10},{10,1... | collective-permute-start | bytes 46088 | tf_op jit(solution)/shard_map/ppermute | solution.py:18
  38.7 4.5 %collective-permute-done.7 = f32[3,10,1,128]{3,2,1,0:T(1,128)S(1)} collective-permute-done((f32[3,10,1,128]{3,2,1,0:T(1,128)S(1)}, f32[3,10,1,128]{3,2,1,0:T(1,128)S(1)}, u32[]{:S(2)}, u32[]{:S(2)}) %collective-permute-start.7) | collective-permute-done | bytes 15392 | tf_op jit(solution)/shard_map/ppermute | solution.py:20
  44.4 3.1 collective-permute-start.8
  49.5 5.2 %collective-permute-done.9 = f32[5,1,8,128]{3,2,1,0:T(8,128)S(1)} collective-permute-done((f32[5,1,8,128]{3,2,1,0:T(8,128)S(1)}, f32[5,1,8,128]{3,2,1,0:T(8,128)S(1)}, u32[]{:S(2)}, u32[]{:S(2)}) %collective-permute-start.9) | collective-permute-done | bytes 20512 | tf_op jit(solution)/shard_map/ppermute | solution.py:20
  54.8 4.8 %collective-permute-start.10 = (f32[5,10,1,128]{3,2,1,0:T(1,128)S(1)}, f32[5,10,1,128]{3,2,1,0:T(1,128)S(1)}, u32[]{:S(2)}, u32[]{:S(2)}) collective-permute-start(f32[5,10,1,128]{3,2,1,0:T(1,128)S(1)} %get-tuple-element.94), channel_id=1, source_target_pairs={{0,1},{1,2},{2,3},{3,4},{4,5},{5,6},{6,7},{7,8},{8,9},{9,10},{10,1... | collective-permute-start | bytes 76808 | tf_op jit(solution)/shard_map/ppermute | solution.py:18
  61.0 3.5 %collective-permute-done.11 = f32[5,10,1,128]{3,2,1,0:T(1,128)S(1)} collective-permute-done((f32[5,10,1,128]{3,2,1,0:T(1,128)S(1)}, f32[5,10,1,128]{3,2,1,0:T(1,128)S(1)}, u32[]{:S(2)}, u32[]{:S(2)}) %collective-permute-start.11) | collective-permute-done | bytes 25632 | tf_op jit(solution)/shard_map/ppermute | solution.py:20
  64.8 3.1 collective-permute-start.12
  69.8 5.2 %collective-permute-done.13 = f32[3,1,8,128]{3,2,1,0:T(8,128)S(1)} collective-permute-done((f32[3,1,8,128]{3,2,1,0:T(8,128)S(1)}, f32[3,1,8,128]{3,2,1,0:T(8,128)S(1)}, u32[]{:S(2)}, u32[]{:S(2)}) %collective-permute-start.13) | collective-permute-done | bytes 12320 | tf_op jit(solution)/shard_map/ppermute | solution.py:20
  75.0 3.6 %collective-permute-start.14 = (f32[3,10,1,128]{3,2,1,0:T(1,128)S(1)}, f32[3,10,1,128]{3,2,1,0:T(1,128)S(1)}, u32[]{:S(2)}, u32[]{:S(2)}) collective-permute-start(f32[3,10,1,128]{3,2,1,0:T(1,128)S(1)} %get-tuple-element.126), channel_id=1, source_target_pairs={{0,1},{1,2},{2,3},{3,4},{4,5},{5,6},{6,7},{7,8},{8,9},{9,10},{10,1... | collective-permute-start | bytes 46088 | tf_op jit(solution)/shard_map/ppermute | solution.py:18
  80.0 3.3 %collective-permute-done.15 = f32[3,10,1,128]{3,2,1,0:T(1,128)S(1)} collective-permute-done((f32[3,10,1,128]{3,2,1,0:T(1,128)S(1)}, f32[3,10,1,128]{3,2,1,0:T(1,128)S(1)}, u32[]{:S(2)}, u32[]{:S(2)}) %collective-permute-start.15) | collective-permute-done | bytes 15392 | tf_op jit(solution)/shard_map/ppermute | solution.py:20
  83.9 3.2 collective-permute-start.16
  89.1 5.3 %collective-permute-done.17 = f32[5,1,8,128]{3,2,1,0:T(8,128)S(1)} collective-permute-done((f32[5,1,8,128]{3,2,1,0:T(8,128)S(1)}, f32[5,1,8,128]{3,2,1,0:T(8,128)S(1)}, u32[]{:S(2)}, u32[]{:S(2)}) %collective-permute-start.17) | collective-permute-done | bytes 20512 | tf_op jit(solution)/shard_map/ppermute | solution.py:20
  94.3 4.5 %collective-permute-start.18 = (f32[5,10,1,128]{3,2,1,0:T(1,128)S(1)}, f32[5,10,1,128]{3,2,1,0:T(1,128)S(1)}, u32[]{:S(2)}, u32[]{:S(2)}) collective-permute-start(f32[5,10,1,128]{3,2,1,0:T(1,128)S(1)} %get-tuple-element.92), channel_id=1, source_target_pairs={{0,1},{1,2},{2,3},{3,4},{4,5},{5,6},{6,7},{7,8},{8,9},{9,10},{10,1... | collective-permute-start | bytes 76808 | tf_op jit(solution)/shard_map/ppermute | solution.py:18
  100.2 3.5 %collective-permute-done.19 = f32[5,10,1,128]{3,2,1,0:T(1,128)S(1)} collective-permute-done((f32[5,10,1,128]{3,2,1,0:T(1,128)S(1)}, f32[5,10,1,128]{3,2,1,0:T(1,128)S(1)}, u32[]{:S(2)}, u32[]{:S(2)}) %collective-permute-start.19) | collective-permute-done | bytes 25632 | tf_op jit(solution)/shard_map/ppermute | solution.py:20
  104.0 3.1 collective-permute-start.20
  109.0 5.2 %collective-permute-done.21 = f32[3,1,8,128]{3,2,1,0:T(8,128)S(1)} collective-permute-done((f32[3,1,8,128]{3,2,1,0:T(8,128)S(1)}, f32[3,1,8,128]{3,2,1,0:T(8,128)S(1)}, u32[]{:S(2)}, u32[]{:S(2)}) %collective-permute-start.21) | collective-permute-done | bytes 12320 | tf_op jit(solution)/shard_map/ppermute | solution.py:20
  114.2 4.8 %collective-permute-start.22 = (f32[3,10,1,128]{3,2,1,0:T(1,128)S(1)}, f32[3,10,1,128]{3,2,1,0:T(1,128)S(1)}, u32[]{:S(2)}, u32[]{:S(2)}) collective-permute-start(f32[3,10,1,128]{3,2,1,0:T(1,128)S(1)} %get-tuple-element.124), channel_id=1, source_target_pairs={{0,1},{1,2},{2,3},{3,4},{4,5},{5,6},{6,7},{7,8},{8,9},{9,10},{10,1... | collective-permute-start | bytes 46088 | tf_op jit(solution)/shard_map/ppermute | solution.py:18
  120.4 3.4 %collective-permute-done.23 = f32[3,10,1,128]{3,2,1,0:T(1,128)S(1)} collective-permute-done((f32[3,10,1,128]{3,2,1,0:T(1,128)S(1)}, f32[3,10,1,128]{3,2,1,0:T(1,128)S(1)}, u32[]{:S(2)}, u32[]{:S(2)}) %collective-permute-start.23) | collective-permute-done | bytes 15392 | tf_op jit(solution)/shard_map/ppermute | solution.py:20
  124.4 3.1 collective-permute-start.24
  129.5 5.2 %collective-permute-done.25 = f32[5,1,8,128]{3,2,1,0:T(8,128)S(1)} collective-permute-done((f32[5,1,8,128]{3,2,1,0:T(8,128)S(1)}, f32[5,1,8,128]{3,2,1,0:T(8,128)S(1)}, u32[]{:S(2)}, u32[]{:S(2)}) %collective-permute-start.25) | collective-permute-done | bytes 20512 | tf_op jit(solution)/shard_map/ppermute | solution.py:20
  134.8 3.6 %collective-permute-start.26 = (f32[5,10,1,128]{3,2,1,0:T(1,128)S(1)}, f32[5,10,1,128]{3,2,1,0:T(1,128)S(1)}, u32[]{:S(2)}, u32[]{:S(2)}) collective-permute-start(f32[5,10,1,128]{3,2,1,0:T(1,128)S(1)} %get-tuple-element.90), channel_id=1, source_target_pairs={{0,1},{1,2},{2,3},{3,4},{4,5},{5,6},{6,7},{7,8},{8,9},{9,10},{10,1... | collective-permute-start | bytes 76808 | tf_op jit(solution)/shard_map/ppermute | solution.py:18
  139.8 3.5 %collective-permute-done.27 = f32[5,10,1,128]{3,2,1,0:T(1,128)S(1)} collective-permute-done((f32[5,10,1,128]{3,2,1,0:T(1,128)S(1)}, f32[5,10,1,128]{3,2,1,0:T(1,128)S(1)}, u32[]{:S(2)}, u32[]{:S(2)}) %collective-permute-start.27) | collective-permute-done | bytes 25632 | tf_op jit(solution)/shard_map/ppermute | solution.py:20
  143.6 3.1 collective-permute-start.28
  148.6 5.2 %collective-permute-done.29 = f32[3,1,8,128]{3,2,1,0:T(8,128)S(1)} collective-permute-done((f32[3,1,8,128]{3,2,1,0:T(8,128)S(1)}, f32[3,1,8,128]{3,2,1,0:T(8,128)S(1)}, u32[]{:S(2)}, u32[]{:S(2)}) %collective-permute-start.29) | collective-permute-done | bytes 12320 | tf_op jit(solution)/shard_map/ppermute | solution.py:20
  153.8 4.5 %collective-permute-start.30 = (f32[3,10,1,128]{3,2,1,0:T(1,128)S(1)}, f32[3,10,1,128]{3,2,1,0:T(1,128)S(1)}, u32[]{:S(2)}, u32[]{:S(2)}) collective-permute-start(f32[3,10,1,128]{3,2,1,0:T(1,128)S(1)} %get-tuple-element.122), channel_id=1, source_target_pairs={{0,1},{1,2},{2,3},{3,4},{4,5},{5,6},{6,7},{7,8},{8,9},{9,10},{10,1... | collective-permute-start | bytes 46088 | tf_op jit(solution)/shard_map/ppermute | solution.py:18
  159.6 3.4 %collective-permute-done.31 = f32[3,10,1,128]{3,2,1,0:T(1,128)S(1)} collective-permute-done((f32[3,10,1,128]{3,2,1,0:T(1,128)S(1)}, f32[3,10,1,128]{3,2,1,0:T(1,128)S(1)}, u32[]{:S(2)}, u32[]{:S(2)}) %collective-permute-start.31) | collective-permute-done | bytes 15392 | tf_op jit(solution)/shard_map/ppermute | solution.py:20
  163.6 3.1 collective-permute-start.32
  168.7 5.3 %collective-permute-done.33 = f32[5,1,8,128]{3,2,1,0:T(8,128)S(1)} collective-permute-done((f32[5,1,8,128]{3,2,1,0:T(8,128)S(1)}, f32[5,1,8,128]{3,2,1,0:T(8,128)S(1)}, u32[]{:S(2)}, u32[]{:S(2)}) %collective-permute-start.33) | collective-permute-done | bytes 20512 | tf_op jit(solution)/shard_map/ppermute | solution.py:20
  174.0 4.8 %collective-permute-start.34 = (f32[5,10,1,128]{3,2,1,0:T(1,128)S(1)}, f32[5,10,1,128]{3,2,1,0:T(1,128)S(1)}, u32[]{:S(2)}, u32[]{:S(2)}) collective-permute-start(f32[5,10,1,128]{3,2,1,0:T(1,128)S(1)} %get-tuple-element.88), channel_id=1, source_target_pairs={{0,1},{1,2},{2,3},{3,4},{4,5},{5,6},{6,7},{7,8},{8,9},{9,10},{10,1... | collective-permute-start | bytes 76808 | tf_op jit(solution)/shard_map/ppermute | solution.py:18
  180.2 3.5 %collective-permute-done.35 = f32[5,10,1,128]{3,2,1,0:T(1,128)S(1)} collective-permute-done((f32[5,10,1,128]{3,2,1,0:T(1,128)S(1)}, f32[5,10,1,128]{3,2,1,0:T(1,128)S(1)}, u32[]{:S(2)}, u32[]{:S(2)}) %collective-permute-start.35) | collective-permute-done | bytes 25632 | tf_op jit(solution)/shard_map/ppermute | solution.py:20
  184.0 3.1 collective-permute-start.36
  189.1 5.2 %collective-permute-done.37 = f32[3,1,8,128]{3,2,1,0:T(8,128)S(1)} collective-permute-done((f32[3,1,8,128]{3,2,1,0:T(8,128)S(1)}, f32[3,1,8,128]{3,2,1,0:T(8,128)S(1)}, u32[]{:S(2)}, u32[]{:S(2)}) %collective-permute-start.37) | collective-permute-done | bytes 12320 | tf_op jit(solution)/shard_map/ppermute | solution.py:20
  194.3 3.6 %collective-permute-start.38 = (f32[3,10,1,128]{3,2,1,0:T(1,128)S(1)}, f32[3,10,1,128]{3,2,1,0:T(1,128)S(1)}, u32[]{:S(2)}, u32[]{:S(2)}) collective-permute-start(f32[3,10,1,128]{3,2,1,0:T(1,128)S(1)} %get-tuple-element.120), channel_id=1, source_target_pairs={{0,1},{1,2},{2,3},{3,4},{4,5},{5,6},{6,7},{7,8},{8,9},{9,10},{10,1... | collective-permute-start | bytes 46088 | tf_op jit(solution)/shard_map/ppermute | solution.py:18
  199.2 3.4 %collective-permute-done.39 = f32[3,10,1,128]{3,2,1,0:T(1,128)S(1)} collective-permute-done((f32[3,10,1,128]{3,2,1,0:T(1,128)S(1)}, f32[3,10,1,128]{3,2,1,0:T(1,128)S(1)}, u32[]{:S(2)}, u32[]{:S(2)}) %collective-permute-start.39) | collective-permute-done | bytes 15392 | tf_op jit(solution)/shard_map/ppermute | solution.py:20
  203.3 3.1 collective-permute-start.40
  208.3 5.3 %collective-permute-done.41 = f32[5,1,8,128]{3,2,1,0:T(8,128)S(1)} collective-permute-done((f32[5,1,8,128]{3,2,1,0:T(8,128)S(1)}, f32[5,1,8,128]{3,2,1,0:T(8,128)S(1)}, u32[]{:S(2)}, u32[]{:S(2)}) %collective-permute-start.41) | collective-permute-done | bytes 20512 | tf_op jit(solution)/shard_map/ppermute | solution.py:20
  213.6 4.5 %collective-permute-start.42 = (f32[5,10,1,128]{3,2,1,0:T(1,128)S(1)}, f32[5,10,1,128]{3,2,1,0:T(1,128)S(1)}, u32[]{:S(2)}, u32[]{:S(2)}) collective-permute-start(f32[5,10,1,128]{3,2,1,0:T(1,128)S(1)} %get-tuple-element.86), channel_id=1, source_target_pairs={{0,1},{1,2},{2,3},{3,4},{4,5},{5,6},{6,7},{7,8},{8,9},{9,10},{10,1... | collective-permute-start | bytes 76808 | tf_op jit(solution)/shard_map/ppermute | solution.py:18
  219.5 3.5 %collective-permute-done.43 = f32[5,10,1,128]{3,2,1,0:T(1,128)S(1)} collective-permute-done((f32[5,10,1,128]{3,2,1,0:T(1,128)S(1)}, f32[5,10,1,128]{3,2,1,0:T(1,128)S(1)}, u32[]{:S(2)}, u32[]{:S(2)}) %collective-permute-start.43) | collective-permute-done | bytes 25632 | tf_op jit(solution)/shard_map/ppermute | solution.py:20
  223.3 3.1 collective-permute-start.44
  228.3 5.2 %collective-permute-done.45 = f32[3,1,8,128]{3,2,1,0:T(8,128)S(1)} collective-permute-done((f32[3,1,8,128]{3,2,1,0:T(8,128)S(1)}, f32[3,1,8,128]{3,2,1,0:T(8,128)S(1)}, u32[]{:S(2)}, u32[]{:S(2)}) %collective-permute-start.45) | collective-permute-done | bytes 12320 | tf_op jit(solution)/shard_map/ppermute | solution.py:20
  233.5 4.8 %collective-permute-start.46 = (f32[3,10,1,128]{3,2,1,0:T(1,128)S(1)}, f32[3,10,1,128]{3,2,1,0:T(1,128)S(1)}, u32[]{:S(2)}, u32[]{:S(2)}) collective-permute-start(f32[3,10,1,128]{3,2,1,0:T(1,128)S(1)} %get-tuple-element.118), channel_id=1, source_target_pairs={{0,1},{1,2},{2,3},{3,4},{4,5},{5,6},{6,7},{7,8},{8,9},{9,10},{10,1... | collective-permute-start | bytes 46088 | tf_op jit(solution)/shard_map/ppermute | solution.py:18
  239.7 3.4 %collective-permute-done.47 = f32[3,10,1,128]{3,2,1,0:T(1,128)S(1)} collective-permute-done((f32[3,10,1,128]{3,2,1,0:T(1,128)S(1)}, f32[3,10,1,128]{3,2,1,0:T(1,128)S(1)}, u32[]{:S(2)}, u32[]{:S(2)}) %collective-permute-start.47) | collective-permute-done | bytes 15392 | tf_op jit(solution)/shard_map/ppermute | solution.py:20
  243.7 3.1 collective-permute-start.48
  248.8 5.3 %collective-permute-done.49 = f32[5,1,8,128]{3,2,1,0:T(8,128)S(1)} collective-permute-done((f32[5,1,8,128]{3,2,1,0:T(8,128)S(1)}, f32[5,1,8,128]{3,2,1,0:T(8,128)S(1)}, u32[]{:S(2)}, u32[]{:S(2)}) %collective-permute-start.49) | collective-permute-done | bytes 20512 | tf_op jit(solution)/shard_map/ppermute | solution.py:20
  254.1 3.6 %collective-permute-start.50 = (f32[5,10,1,128]{3,2,1,0:T(1,128)S(1)}, f32[5,10,1,128]{3,2,1,0:T(1,128)S(1)}, u32[]{:S(2)}, u32[]{:S(2)}) collective-permute-start(f32[5,10,1,128]{3,2,1,0:T(1,128)S(1)} %get-tuple-element.84), channel_id=1, source_target_pairs={{0,1},{1,2},{2,3},{3,4},{4,5},{5,6},{6,7},{7,8},{8,9},{9,10},{10,1... | collective-permute-start | bytes 76808 | tf_op jit(solution)/shard_map/ppermute | solution.py:18
  259.1 3.5 %collective-permute-done.51 = f32[5,10,1,128]{3,2,1,0:T(1,128)S(1)} collective-permute-done((f32[5,10,1,128]{3,2,1,0:T(1,128)S(1)}, f32[5,10,1,128]{3,2,1,0:T(1,128)S(1)}, u32[]{:S(2)}, u32[]{:S(2)}) %collective-permute-start.51) | collective-permute-done | bytes 25632 | tf_op jit(solution)/shard_map/ppermute | solution.py:20
  262.9 3.1 collective-permute-start.52
  268.0 5.2 %collective-permute-done.53 = f32[3,1,8,128]{3,2,1,0:T(8,128)S(1)} collective-permute-done((f32[3,1,8,128]{3,2,1,0:T(8,128)S(1)}, f32[3,1,8,128]{3,2,1,0:T(8,128)S(1)}, u32[]{:S(2)}, u32[]{:S(2)}) %collective-permute-start.53) | collective-permute-done | bytes 12320 | tf_op jit(solution)/shard_map/ppermute | solution.py:20
  273.2 3.6 %collective-permute-start.54 = (f32[3,10,1,128]{3,2,1,0:T(1,128)S(1)}, f32[3,10,1,128]{3,2,1,0:T(1,128)S(1)}, u32[]{:S(2)}, u32[]{:S(2)}) collective-permute-start(f32[3,10,1,128]{3,2,1,0:T(1,128)S(1)} %get-tuple-element.116), channel_id=1, source_target_pairs={{0,1},{1,2},{2,3},{3,4},{4,5},{5,6},{6,7},{7,8},{8,9},{9,10},{10,1... | collective-permute-start | bytes 46088 | tf_op jit(solution)/shard_map/ppermute | solution.py:18
  278.1 3.4 %collective-permute-done.55 = f32[3,10,1,128]{3,2,1,0:T(1,128)S(1)} collective-permute-done((f32[3,10,1,128]{3,2,1,0:T(1,128)S(1)}, f32[3,10,1,128]{3,2,1,0:T(1,128)S(1)}, u32[]{:S(2)}, u32[]{:S(2)}) %collective-permute-start.55) | collective-permute-done | bytes 15392 | tf_op jit(solution)/shard_map/ppermute | solution.py:20
  282.2 3.1 collective-permute-start.56
  287.2 5.3 %collective-permute-done.57 = f32[5,1,8,128]{3,2,1,0:T(8,128)S(1)} collective-permute-done((f32[5,1,8,128]{3,2,1,0:T(8,128)S(1)}, f32[5,1,8,128]{3,2,1,0:T(8,128)S(1)}, u32[]{:S(2)}, u32[]{:S(2)}) %collective-permute-start.57) | collective-permute-done | bytes 20512 | tf_op jit(solution)/shard_map/ppermute | solution.py:20
  292.5 3.6 %collective-permute-start.58 = (f32[5,10,1,128]{3,2,1,0:T(1,128)S(1)}, f32[5,10,1,128]{3,2,1,0:T(1,128)S(1)}, u32[]{:S(2)}, u32[]{:S(2)}) collective-permute-start(f32[5,10,1,128]{3,2,1,0:T(1,128)S(1)} %get-tuple-element.82), channel_id=1, source_target_pairs={{0,1},{1,2},{2,3},{3,4},{4,5},{5,6},{6,7},{7,8},{8,9},{9,10},{10,1... | collective-permute-start | bytes 76808 | tf_op jit(solution)/shard_map/ppermute | solution.py:18
  297.6 3.5 %collective-permute-done.59 = f32[5,10,1,128]{3,2,1,0:T(1,128)S(1)} collective-permute-done((f32[5,10,1,128]{3,2,1,0:T(1,128)S(1)}, f32[5,10,1,128]{3,2,1,0:T(1,128)S(1)}, u32[]{:S(2)}, u32[]{:S(2)}) %collective-permute-start.59) | collective-permute-done | bytes 25632 | tf_op jit(solution)/shard_map/ppermute | solution.py:20
  301.4 3.1 collective-permute-start.60
  306.5 5.2 %collective-permute-done.61 = f32[3,1,8,128]{3,2,1,0:T(8,128)S(1)} collective-permute-done((f32[3,1,8,128]{3,2,1,0:T(8,128)S(1)}, f32[3,1,8,128]{3,2,1,0:T(8,128)S(1)}, u32[]{:S(2)}, u32[]{:S(2)}) %collective-permute-start.61) | collective-permute-done | bytes 12320 | tf_op jit(solution)/shard_map/ppermute | solution.py:20
  311.7 3.6 %collective-permute-start.62 = (f32[3,10,1,128]{3,2,1,0:T(1,128)S(1)}, f32[3,10,1,128]{3,2,1,0:T(1,128)S(1)}, u32[]{:S(2)}, u32[]{:S(2)}) collective-permute-start(f32[3,10,1,128]{3,2,1,0:T(1,128)S(1)} %get-tuple-element.114), channel_id=1, source_target_pairs={{0,1},{1,2},{2,3},{3,4},{4,5},{5,6},{6,7},{7,8},{8,9},{9,10},{10,1... | collective-permute-start | bytes 46088 | tf_op jit(solution)/shard_map/ppermute | solution.py:18
  316.6 3.2 collective-permute-done.63
  (277 shorter events, 64.6 us)
Async XLA Ops:
  1.4 8.0 %collective-permute-start = (f32[5,1,8,128]{3,2,1,0:T(8,128)S(1)}, f32[5,1,8,128]{3,2,1,0:T(8,128)S(1)}, u32[]{:S(2)}, u32[]{:S(2)}) collective-permute-start(f32[5,1,8,128]{3,2,1,0:T(8,128)S(1)} %get-tuple-element.112), channel_id=1, source_target_pairs={{0,32},{32,64},{64,96},{96,128},{128,160},{160,192},{192,224},{224... | collective-permute-start | bytes 61448 | tf_op jit(solution)/shard_map/ppermute | solution.py:18
  5.1 7.2 %collective-permute-start.1 = (f32[5,1,8,128]{3,2,1,0:T(8,128)S(1)}, f32[5,1,8,128]{3,2,1,0:T(8,128)S(1)}, u32[]{:S(2)}, u32[]{:S(2)}) collective-permute-start(f32[5,1,8,128]{3,2,1,0:T(8,128)S(1)} %get-tuple-element.113), channel_id=1, source_target_pairs={{32,0},{64,32},{96,64},{128,96},{160,128},{192,160},{224,192},{256... | collective-permute-start | bytes 61448 | tf_op jit(solution)/shard_map/ppermute | solution.py:20
  12.3 5.0 %collective-permute-start.2 = (f32[5,10,1,128]{3,2,1,0:T(1,128)S(1)}, f32[5,10,1,128]{3,2,1,0:T(1,128)S(1)}, u32[]{:S(2)}, u32[]{:S(2)}) collective-permute-start(f32[5,10,1,128]{3,2,1,0:T(1,128)S(1)} %get-tuple-element.96), channel_id=1, source_target_pairs={{0,1},{1,2},{2,3},{3,4},{4,5},{5,6},{6,7},{7,8},{8,9},{9,10},{10,1... | collective-permute-start | bytes 76808 | tf_op jit(solution)/shard_map/ppermute | solution.py:18
  15.9 4.8 %collective-permute-start.3 = (f32[5,10,1,128]{3,2,1,0:T(1,128)S(1)}, f32[5,10,1,128]{3,2,1,0:T(1,128)S(1)}, u32[]{:S(2)}, u32[]{:S(2)}) collective-permute-start(f32[5,10,1,128]{3,2,1,0:T(1,128)S(1)} %get-tuple-element.97), channel_id=1, source_target_pairs={{1,0},{2,1},{3,2},{4,3},{5,4},{6,5},{7,6},{8,7},{9,8},{10,9},{11,1... | collective-permute-start | bytes 76808 | tf_op jit(solution)/shard_map/ppermute | solution.py:20
  22.6 6.0 %collective-permute-start.4 = (f32[3,1,8,128]{3,2,1,0:T(8,128)S(1)}, f32[3,1,8,128]{3,2,1,0:T(8,128)S(1)}, u32[]{:S(2)}, u32[]{:S(2)}) collective-permute-start(f32[3,1,8,128]{3,2,1,0:T(8,128)S(1)} %get-tuple-element.144), channel_id=1, source_target_pairs={{0,32},{32,64},{64,96},{96,128},{128,160},{160,192},{192,224},{224... | collective-permute-start | bytes 36872 | tf_op jit(solution)/shard_map/ppermute | solution.py:18
  26.7 7.1 %collective-permute-start.5 = (f32[3,1,8,128]{3,2,1,0:T(8,128)S(1)}, f32[3,1,8,128]{3,2,1,0:T(8,128)S(1)}, u32[]{:S(2)}, u32[]{:S(2)}) collective-permute-start(f32[3,1,8,128]{3,2,1,0:T(8,128)S(1)} %get-tuple-element.145), channel_id=1, source_target_pairs={{32,0},{64,32},{96,64},{128,96},{160,128},{192,160},{224,192},{256... | collective-permute-start | bytes 36872 | tf_op jit(solution)/shard_map/ppermute | solution.py:20
  33.8 4.9 %collective-permute-start.6 = (f32[3,10,1,128]{3,2,1,0:T(1,128)S(1)}, f32[3,10,1,128]{3,2,1,0:T(1,128)S(1)}, u32[]{:S(2)}, u32[]{:S(2)}) collective-permute-start(f32[3,10,1,128]{3,2,1,0:T(1,128)S(1)} %get-tuple-element.128), channel_id=1, source_target_pairs={{0,1},{1,2},{2,3},{3,4},{4,5},{5,6},{6,7},{7,8},{8,9},{9,10},{10,1... | collective-permute-start | bytes 46088 | tf_op jit(solution)/shard_map/ppermute | solution.py:18
  37.4 5.8 %collective-permute-start.7 = (f32[3,10,1,128]{3,2,1,0:T(1,128)S(1)}, f32[3,10,1,128]{3,2,1,0:T(1,128)S(1)}, u32[]{:S(2)}, u32[]{:S(2)}) collective-permute-start(f32[3,10,1,128]{3,2,1,0:T(1,128)S(1)} %get-tuple-element.129), channel_id=1, source_target_pairs={{1,0},{2,1},{3,2},{4,3},{5,4},{6,5},{7,6},{8,7},{9,8},{10,9},{11,1... | collective-permute-start | bytes 46088 | tf_op jit(solution)/shard_map/ppermute | solution.py:20
  44.4 5.1 %collective-permute-start.8 = (f32[5,1,8,128]{3,2,1,0:T(8,128)S(1)}, f32[5,1,8,128]{3,2,1,0:T(8,128)S(1)}, u32[]{:S(2)}, u32[]{:S(2)}) collective-permute-start(f32[5,1,8,128]{3,2,1,0:T(8,128)S(1)} %get-tuple-element.110), channel_id=1, source_target_pairs={{0,32},{32,64},{64,96},{96,128},{128,160},{160,192},{192,224},{224... | collective-permute-start | bytes 61448 | tf_op jit(solution)/shard_map/ppermute | solution.py:18
  47.5 7.2 %collective-permute-start.9 = (f32[5,1,8,128]{3,2,1,0:T(8,128)S(1)}, f32[5,1,8,128]{3,2,1,0:T(8,128)S(1)}, u32[]{:S(2)}, u32[]{:S(2)}) collective-permute-start(f32[5,1,8,128]{3,2,1,0:T(8,128)S(1)} %get-tuple-element.111), channel_id=1, source_target_pairs={{32,0},{64,32},{96,64},{128,96},{160,128},{192,160},{224,192},{256... | collective-permute-start | bytes 61448 | tf_op jit(solution)/shard_map/ppermute | solution.py:20
  54.8 6.2 %collective-permute-start.10 = (f32[5,10,1,128]{3,2,1,0:T(1,128)S(1)}, f32[5,10,1,128]{3,2,1,0:T(1,128)S(1)}, u32[]{:S(2)}, u32[]{:S(2)}) collective-permute-start(f32[5,10,1,128]{3,2,1,0:T(1,128)S(1)} %get-tuple-element.94), channel_id=1, source_target_pairs={{0,1},{1,2},{2,3},{3,4},{4,5},{5,6},{6,7},{7,8},{8,9},{9,10},{10,1... | collective-permute-start | bytes 76808 | tf_op jit(solution)/shard_map/ppermute | solution.py:18
  59.6 4.9 %collective-permute-start.11 = (f32[5,10,1,128]{3,2,1,0:T(1,128)S(1)}, f32[5,10,1,128]{3,2,1,0:T(1,128)S(1)}, u32[]{:S(2)}, u32[]{:S(2)}) collective-permute-start(f32[5,10,1,128]{3,2,1,0:T(1,128)S(1)} %get-tuple-element.95), channel_id=1, source_target_pairs={{1,0},{2,1},{3,2},{4,3},{5,4},{6,5},{7,6},{8,7},{9,8},{10,9},{11,1... | collective-permute-start | bytes 76808 | tf_op jit(solution)/shard_map/ppermute | solution.py:20
  64.8 5.0 %collective-permute-start.12 = (f32[3,1,8,128]{3,2,1,0:T(8,128)S(1)}, f32[3,1,8,128]{3,2,1,0:T(8,128)S(1)}, u32[]{:S(2)}, u32[]{:S(2)}) collective-permute-start(f32[3,1,8,128]{3,2,1,0:T(8,128)S(1)} %get-tuple-element.142), channel_id=1, source_target_pairs={{0,32},{32,64},{64,96},{96,128},{128,160},{160,192},{192,224},{224... | collective-permute-start | bytes 36872 | tf_op jit(solution)/shard_map/ppermute | solution.py:18
  67.9 7.1 %collective-permute-start.13 = (f32[3,1,8,128]{3,2,1,0:T(8,128)S(1)}, f32[3,1,8,128]{3,2,1,0:T(8,128)S(1)}, u32[]{:S(2)}, u32[]{:S(2)}) collective-permute-start(f32[3,1,8,128]{3,2,1,0:T(8,128)S(1)} %get-tuple-element.143), channel_id=1, source_target_pairs={{32,0},{64,32},{96,64},{128,96},{160,128},{192,160},{224,192},{256... | collective-permute-start | bytes 36872 | tf_op jit(solution)/shard_map/ppermute | solution.py:20
  75.0 4.9 %collective-permute-start.14 = (f32[3,10,1,128]{3,2,1,0:T(1,128)S(1)}, f32[3,10,1,128]{3,2,1,0:T(1,128)S(1)}, u32[]{:S(2)}, u32[]{:S(2)}) collective-permute-start(f32[3,10,1,128]{3,2,1,0:T(1,128)S(1)} %get-tuple-element.126), channel_id=1, source_target_pairs={{0,1},{1,2},{2,3},{3,4},{4,5},{5,6},{6,7},{7,8},{8,9},{9,10},{10,1... | collective-permute-start | bytes 46088 | tf_op jit(solution)/shard_map/ppermute | solution.py:18
  78.7 4.7 %collective-permute-start.15 = (f32[3,10,1,128]{3,2,1,0:T(1,128)S(1)}, f32[3,10,1,128]{3,2,1,0:T(1,128)S(1)}, u32[]{:S(2)}, u32[]{:S(2)}) collective-permute-start(f32[3,10,1,128]{3,2,1,0:T(1,128)S(1)} %get-tuple-element.127), channel_id=1, source_target_pairs={{1,0},{2,1},{3,2},{4,3},{5,4},{6,5},{7,6},{8,7},{9,8},{10,9},{11,1... | collective-permute-start | bytes 46088 | tf_op jit(solution)/shard_map/ppermute | solution.py:20
  83.9 5.1 %collective-permute-start.16 = (f32[5,1,8,128]{3,2,1,0:T(8,128)S(1)}, f32[5,1,8,128]{3,2,1,0:T(8,128)S(1)}, u32[]{:S(2)}, u32[]{:S(2)}) collective-permute-start(f32[5,1,8,128]{3,2,1,0:T(8,128)S(1)} %get-tuple-element.108), channel_id=1, source_target_pairs={{0,32},{32,64},{64,96},{96,128},{128,160},{160,192},{192,224},{224... | collective-permute-start | bytes 61448 | tf_op jit(solution)/shard_map/ppermute | solution.py:18
  87.1 7.2 %collective-permute-start.17 = (f32[5,1,8,128]{3,2,1,0:T(8,128)S(1)}, f32[5,1,8,128]{3,2,1,0:T(8,128)S(1)}, u32[]{:S(2)}, u32[]{:S(2)}) collective-permute-start(f32[5,1,8,128]{3,2,1,0:T(8,128)S(1)} %get-tuple-element.109), channel_id=1, source_target_pairs={{32,0},{64,32},{96,64},{128,96},{160,128},{192,160},{224,192},{256... | collective-permute-start | bytes 61448 | tf_op jit(solution)/shard_map/ppermute | solution.py:20
  94.3 5.9 %collective-permute-start.18 = (f32[5,10,1,128]{3,2,1,0:T(1,128)S(1)}, f32[5,10,1,128]{3,2,1,0:T(1,128)S(1)}, u32[]{:S(2)}, u32[]{:S(2)}) collective-permute-start(f32[5,10,1,128]{3,2,1,0:T(1,128)S(1)} %get-tuple-element.92), channel_id=1, source_target_pairs={{0,1},{1,2},{2,3},{3,4},{4,5},{5,6},{6,7},{7,8},{8,9},{9,10},{10,1... | collective-permute-start | bytes 76808 | tf_op jit(solution)/shard_map/ppermute | solution.py:18
  98.8 4.9 %collective-permute-start.19 = (f32[5,10,1,128]{3,2,1,0:T(1,128)S(1)}, f32[5,10,1,128]{3,2,1,0:T(1,128)S(1)}, u32[]{:S(2)}, u32[]{:S(2)}) collective-permute-start(f32[5,10,1,128]{3,2,1,0:T(1,128)S(1)} %get-tuple-element.93), channel_id=1, source_target_pairs={{1,0},{2,1},{3,2},{4,3},{5,4},{6,5},{7,6},{8,7},{9,8},{10,9},{11,1... | collective-permute-start | bytes 76808 | tf_op jit(solution)/shard_map/ppermute | solution.py:20
  104.0 5.0 %collective-permute-start.20 = (f32[3,1,8,128]{3,2,1,0:T(8,128)S(1)}, f32[3,1,8,128]{3,2,1,0:T(8,128)S(1)}, u32[]{:S(2)}, u32[]{:S(2)}) collective-permute-start(f32[3,1,8,128]{3,2,1,0:T(8,128)S(1)} %get-tuple-element.140), channel_id=1, source_target_pairs={{0,32},{32,64},{64,96},{96,128},{128,160},{160,192},{192,224},{224... | collective-permute-start | bytes 36872 | tf_op jit(solution)/shard_map/ppermute | solution.py:18
  107.1 7.1 %collective-permute-start.21 = (f32[3,1,8,128]{3,2,1,0:T(8,128)S(1)}, f32[3,1,8,128]{3,2,1,0:T(8,128)S(1)}, u32[]{:S(2)}, u32[]{:S(2)}) collective-permute-start(f32[3,1,8,128]{3,2,1,0:T(8,128)S(1)} %get-tuple-element.141), channel_id=1, source_target_pairs={{32,0},{64,32},{96,64},{128,96},{160,128},{192,160},{224,192},{256... | collective-permute-start | bytes 36872 | tf_op jit(solution)/shard_map/ppermute | solution.py:20
  114.2 6.2 %collective-permute-start.22 = (f32[3,10,1,128]{3,2,1,0:T(1,128)S(1)}, f32[3,10,1,128]{3,2,1,0:T(1,128)S(1)}, u32[]{:S(2)}, u32[]{:S(2)}) collective-permute-start(f32[3,10,1,128]{3,2,1,0:T(1,128)S(1)} %get-tuple-element.124), channel_id=1, source_target_pairs={{0,1},{1,2},{2,3},{3,4},{4,5},{5,6},{6,7},{7,8},{8,9},{9,10},{10,1... | collective-permute-start | bytes 46088 | tf_op jit(solution)/shard_map/ppermute | solution.py:18
  119.1 4.8 %collective-permute-start.23 = (f32[3,10,1,128]{3,2,1,0:T(1,128)S(1)}, f32[3,10,1,128]{3,2,1,0:T(1,128)S(1)}, u32[]{:S(2)}, u32[]{:S(2)}) collective-permute-start(f32[3,10,1,128]{3,2,1,0:T(1,128)S(1)} %get-tuple-element.125), channel_id=1, source_target_pairs={{1,0},{2,1},{3,2},{4,3},{5,4},{6,5},{7,6},{8,7},{9,8},{10,9},{11,1... | collective-permute-start | bytes 46088 | tf_op jit(solution)/shard_map/ppermute | solution.py:20
  124.4 5.1 %collective-permute-start.24 = (f32[5,1,8,128]{3,2,1,0:T(8,128)S(1)}, f32[5,1,8,128]{3,2,1,0:T(8,128)S(1)}, u32[]{:S(2)}, u32[]{:S(2)}) collective-permute-start(f32[5,1,8,128]{3,2,1,0:T(8,128)S(1)} %get-tuple-element.106), channel_id=1, source_target_pairs={{0,32},{32,64},{64,96},{96,128},{128,160},{160,192},{192,224},{224... | collective-permute-start | bytes 61448 | tf_op jit(solution)/shard_map/ppermute | solution.py:18
  127.5 7.2 %collective-permute-start.25 = (f32[5,1,8,128]{3,2,1,0:T(8,128)S(1)}, f32[5,1,8,128]{3,2,1,0:T(8,128)S(1)}, u32[]{:S(2)}, u32[]{:S(2)}) collective-permute-start(f32[5,1,8,128]{3,2,1,0:T(8,128)S(1)} %get-tuple-element.107), channel_id=1, source_target_pairs={{32,0},{64,32},{96,64},{128,96},{160,128},{192,160},{224,192},{256... | collective-permute-start | bytes 61448 | tf_op jit(solution)/shard_map/ppermute | solution.py:20
  134.8 5.0 %collective-permute-start.26 = (f32[5,10,1,128]{3,2,1,0:T(1,128)S(1)}, f32[5,10,1,128]{3,2,1,0:T(1,128)S(1)}, u32[]{:S(2)}, u32[]{:S(2)}) collective-permute-start(f32[5,10,1,128]{3,2,1,0:T(1,128)S(1)} %get-tuple-element.90), channel_id=1, source_target_pairs={{0,1},{1,2},{2,3},{3,4},{4,5},{5,6},{6,7},{7,8},{8,9},{9,10},{10,1... | collective-permute-start | bytes 76808 | tf_op jit(solution)/shard_map/ppermute | solution.py:18
  138.4 4.9 %collective-permute-start.27 = (f32[5,10,1,128]{3,2,1,0:T(1,128)S(1)}, f32[5,10,1,128]{3,2,1,0:T(1,128)S(1)}, u32[]{:S(2)}, u32[]{:S(2)}) collective-permute-start(f32[5,10,1,128]{3,2,1,0:T(1,128)S(1)} %get-tuple-element.91), channel_id=1, source_target_pairs={{1,0},{2,1},{3,2},{4,3},{5,4},{6,5},{7,6},{8,7},{9,8},{10,9},{11,1... | collective-permute-start | bytes 76808 | tf_op jit(solution)/shard_map/ppermute | solution.py:20
  143.6 5.0 %collective-permute-start.28 = (f32[3,1,8,128]{3,2,1,0:T(8,128)S(1)}, f32[3,1,8,128]{3,2,1,0:T(8,128)S(1)}, u32[]{:S(2)}, u32[]{:S(2)}) collective-permute-start(f32[3,1,8,128]{3,2,1,0:T(8,128)S(1)} %get-tuple-element.138), channel_id=1, source_target_pairs={{0,32},{32,64},{64,96},{96,128},{128,160},{160,192},{192,224},{224... | collective-permute-start | bytes 36872 | tf_op jit(solution)/shard_map/ppermute | solution.py:18
  146.7 7.1 %collective-permute-start.29 = (f32[3,1,8,128]{3,2,1,0:T(8,128)S(1)}, f32[3,1,8,128]{3,2,1,0:T(8,128)S(1)}, u32[]{:S(2)}, u32[]{:S(2)}) collective-permute-start(f32[3,1,8,128]{3,2,1,0:T(8,128)S(1)} %get-tuple-element.139), channel_id=1, source_target_pairs={{32,0},{64,32},{96,64},{128,96},{160,128},{192,160},{224,192},{256... | collective-permute-start | bytes 36872 | tf_op jit(solution)/shard_map/ppermute | solution.py:20
  153.8 5.8 %collective-permute-start.30 = (f32[3,10,1,128]{3,2,1,0:T(1,128)S(1)}, f32[3,10,1,128]{3,2,1,0:T(1,128)S(1)}, u32[]{:S(2)}, u32[]{:S(2)}) collective-permute-start(f32[3,10,1,128]{3,2,1,0:T(1,128)S(1)} %get-tuple-element.122), channel_id=1, source_target_pairs={{0,1},{1,2},{2,3},{3,4},{4,5},{5,6},{6,7},{7,8},{8,9},{9,10},{10,1... | collective-permute-start | bytes 46088 | tf_op jit(solution)/shard_map/ppermute | solution.py:18
  158.3 4.8 %collective-permute-start.31 = (f32[3,10,1,128]{3,2,1,0:T(1,128)S(1)}, f32[3,10,1,128]{3,2,1,0:T(1,128)S(1)}, u32[]{:S(2)}, u32[]{:S(2)}) collective-permute-start(f32[3,10,1,128]{3,2,1,0:T(1,128)S(1)} %get-tuple-element.123), channel_id=1, source_target_pairs={{1,0},{2,1},{3,2},{4,3},{5,4},{6,5},{7,6},{8,7},{9,8},{10,9},{11,1... | collective-permute-start | bytes 46088 | tf_op jit(solution)/shard_map/ppermute | solution.py:20
  163.6 5.0 %collective-permute-start.32 = (f32[5,1,8,128]{3,2,1,0:T(8,128)S(1)}, f32[5,1,8,128]{3,2,1,0:T(8,128)S(1)}, u32[]{:S(2)}, u32[]{:S(2)}) collective-permute-start(f32[5,1,8,128]{3,2,1,0:T(8,128)S(1)} %get-tuple-element.104), channel_id=1, source_target_pairs={{0,32},{32,64},{64,96},{96,128},{128,160},{160,192},{192,224},{224... | collective-permute-start | bytes 61448 | tf_op jit(solution)/shard_map/ppermute | solution.py:18
  166.7 7.2 %collective-permute-start.33 = (f32[5,1,8,128]{3,2,1,0:T(8,128)S(1)}, f32[5,1,8,128]{3,2,1,0:T(8,128)S(1)}, u32[]{:S(2)}, u32[]{:S(2)}) collective-permute-start(f32[5,1,8,128]{3,2,1,0:T(8,128)S(1)} %get-tuple-element.105), channel_id=1, source_target_pairs={{32,0},{64,32},{96,64},{128,96},{160,128},{192,160},{224,192},{256... | collective-permute-start | bytes 61448 | tf_op jit(solution)/shard_map/ppermute | solution.py:20
  174.0 6.2 %collective-permute-start.34 = (f32[5,10,1,128]{3,2,1,0:T(1,128)S(1)}, f32[5,10,1,128]{3,2,1,0:T(1,128)S(1)}, u32[]{:S(2)}, u32[]{:S(2)}) collective-permute-start(f32[5,10,1,128]{3,2,1,0:T(1,128)S(1)} %get-tuple-element.88), channel_id=1, source_target_pairs={{0,1},{1,2},{2,3},{3,4},{4,5},{5,6},{6,7},{7,8},{8,9},{9,10},{10,1... | collective-permute-start | bytes 76808 | tf_op jit(solution)/shard_map/ppermute | solution.py:18
  178.8 4.9 %collective-permute-start.35 = (f32[5,10,1,128]{3,2,1,0:T(1,128)S(1)}, f32[5,10,1,128]{3,2,1,0:T(1,128)S(1)}, u32[]{:S(2)}, u32[]{:S(2)}) collective-permute-start(f32[5,10,1,128]{3,2,1,0:T(1,128)S(1)} %get-tuple-element.89), channel_id=1, source_target_pairs={{1,0},{2,1},{3,2},{4,3},{5,4},{6,5},{7,6},{8,7},{9,8},{10,9},{11,1... | collective-permute-start | bytes 76808 | tf_op jit(solution)/shard_map/ppermute | solution.py:20
  184.0 5.0 %collective-permute-start.36 = (f32[3,1,8,128]{3,2,1,0:T(8,128)S(1)}, f32[3,1,8,128]{3,2,1,0:T(8,128)S(1)}, u32[]{:S(2)}, u32[]{:S(2)}) collective-permute-start(f32[3,1,8,128]{3,2,1,0:T(8,128)S(1)} %get-tuple-element.136), channel_id=1, source_target_pairs={{0,32},{32,64},{64,96},{96,128},{128,160},{160,192},{192,224},{224... | collective-permute-start | bytes 36872 | tf_op jit(solution)/shard_map/ppermute | solution.py:18
  187.1 7.1 %collective-permute-start.37 = (f32[3,1,8,128]{3,2,1,0:T(8,128)S(1)}, f32[3,1,8,128]{3,2,1,0:T(8,128)S(1)}, u32[]{:S(2)}, u32[]{:S(2)}) collective-permute-start(f32[3,1,8,128]{3,2,1,0:T(8,128)S(1)} %get-tuple-element.137), channel_id=1, source_target_pairs={{32,0},{64,32},{96,64},{128,96},{160,128},{192,160},{224,192},{256... | collective-permute-start | bytes 36872 | tf_op jit(solution)/shard_map/ppermute | solution.py:20
  194.3 4.9 %collective-permute-start.38 = (f32[3,10,1,128]{3,2,1,0:T(1,128)S(1)}, f32[3,10,1,128]{3,2,1,0:T(1,128)S(1)}, u32[]{:S(2)}, u32[]{:S(2)}) collective-permute-start(f32[3,10,1,128]{3,2,1,0:T(1,128)S(1)} %get-tuple-element.120), channel_id=1, source_target_pairs={{0,1},{1,2},{2,3},{3,4},{4,5},{5,6},{6,7},{7,8},{8,9},{9,10},{10,1... | collective-permute-start | bytes 46088 | tf_op jit(solution)/shard_map/ppermute | solution.py:18
  197.9 4.8 %collective-permute-start.39 = (f32[3,10,1,128]{3,2,1,0:T(1,128)S(1)}, f32[3,10,1,128]{3,2,1,0:T(1,128)S(1)}, u32[]{:S(2)}, u32[]{:S(2)}) collective-permute-start(f32[3,10,1,128]{3,2,1,0:T(1,128)S(1)} %get-tuple-element.121), channel_id=1, source_target_pairs={{1,0},{2,1},{3,2},{4,3},{5,4},{6,5},{7,6},{8,7},{9,8},{10,9},{11,1... | collective-permute-start | bytes 46088 | tf_op jit(solution)/shard_map/ppermute | solution.py:20
  203.3 5.0 %collective-permute-start.40 = (f32[5,1,8,128]{3,2,1,0:T(8,128)S(1)}, f32[5,1,8,128]{3,2,1,0:T(8,128)S(1)}, u32[]{:S(2)}, u32[]{:S(2)}) collective-permute-start(f32[5,1,8,128]{3,2,1,0:T(8,128)S(1)} %get-tuple-element.102), channel_id=1, source_target_pairs={{0,32},{32,64},{64,96},{96,128},{128,160},{160,192},{192,224},{224... | collective-permute-start | bytes 61448 | tf_op jit(solution)/shard_map/ppermute | solution.py:18
  206.4 7.2 %collective-permute-start.41 = (f32[5,1,8,128]{3,2,1,0:T(8,128)S(1)}, f32[5,1,8,128]{3,2,1,0:T(8,128)S(1)}, u32[]{:S(2)}, u32[]{:S(2)}) collective-permute-start(f32[5,1,8,128]{3,2,1,0:T(8,128)S(1)} %get-tuple-element.103), channel_id=1, source_target_pairs={{32,0},{64,32},{96,64},{128,96},{160,128},{192,160},{224,192},{256... | collective-permute-start | bytes 61448 | tf_op jit(solution)/shard_map/ppermute | solution.py:20
  213.6 5.9 %collective-permute-start.42 = (f32[5,10,1,128]{3,2,1,0:T(1,128)S(1)}, f32[5,10,1,128]{3,2,1,0:T(1,128)S(1)}, u32[]{:S(2)}, u32[]{:S(2)}) collective-permute-start(f32[5,10,1,128]{3,2,1,0:T(1,128)S(1)} %get-tuple-element.86), channel_id=1, source_target_pairs={{0,1},{1,2},{2,3},{3,4},{4,5},{5,6},{6,7},{7,8},{8,9},{9,10},{10,1... | collective-permute-start | bytes 76808 | tf_op jit(solution)/shard_map/ppermute | solution.py:18
  218.1 4.9 %collective-permute-start.43 = (f32[5,10,1,128]{3,2,1,0:T(1,128)S(1)}, f32[5,10,1,128]{3,2,1,0:T(1,128)S(1)}, u32[]{:S(2)}, u32[]{:S(2)}) collective-permute-start(f32[5,10,1,128]{3,2,1,0:T(1,128)S(1)} %get-tuple-element.87), channel_id=1, source_target_pairs={{1,0},{2,1},{3,2},{4,3},{5,4},{6,5},{7,6},{8,7},{9,8},{10,9},{11,1... | collective-permute-start | bytes 76808 | tf_op jit(solution)/shard_map/ppermute | solution.py:20
  223.3 5.0 %collective-permute-start.44 = (f32[3,1,8,128]{3,2,1,0:T(8,128)S(1)}, f32[3,1,8,128]{3,2,1,0:T(8,128)S(1)}, u32[]{:S(2)}, u32[]{:S(2)}) collective-permute-start(f32[3,1,8,128]{3,2,1,0:T(8,128)S(1)} %get-tuple-element.134), channel_id=1, source_target_pairs={{0,32},{32,64},{64,96},{96,128},{128,160},{160,192},{192,224},{224... | collective-permute-start | bytes 36872 | tf_op jit(solution)/shard_map/ppermute | solution.py:18
  226.4 7.1 %collective-permute-start.45 = (f32[3,1,8,128]{3,2,1,0:T(8,128)S(1)}, f32[3,1,8,128]{3,2,1,0:T(8,128)S(1)}, u32[]{:S(2)}, u32[]{:S(2)}) collective-permute-start(f32[3,1,8,128]{3,2,1,0:T(8,128)S(1)} %get-tuple-element.135), channel_id=1, source_target_pairs={{32,0},{64,32},{96,64},{128,96},{160,128},{192,160},{224,192},{256... | collective-permute-start | bytes 36872 | tf_op jit(solution)/shard_map/ppermute | solution.py:20
  233.5 6.2 %collective-permute-start.46 = (f32[3,10,1,128]{3,2,1,0:T(1,128)S(1)}, f32[3,10,1,128]{3,2,1,0:T(1,128)S(1)}, u32[]{:S(2)}, u32[]{:S(2)}) collective-permute-start(f32[3,10,1,128]{3,2,1,0:T(1,128)S(1)} %get-tuple-element.118), channel_id=1, source_target_pairs={{0,1},{1,2},{2,3},{3,4},{4,5},{5,6},{6,7},{7,8},{8,9},{9,10},{10,1... | collective-permute-start | bytes 46088 | tf_op jit(solution)/shard_map/ppermute | solution.py:18
  238.4 4.8 %collective-permute-start.47 = (f32[3,10,1,128]{3,2,1,0:T(1,128)S(1)}, f32[3,10,1,128]{3,2,1,0:T(1,128)S(1)}, u32[]{:S(2)}, u32[]{:S(2)}) collective-permute-start(f32[3,10,1,128]{3,2,1,0:T(1,128)S(1)} %get-tuple-element.119), channel_id=1, source_target_pairs={{1,0},{2,1},{3,2},{4,3},{5,4},{6,5},{7,6},{8,7},{9,8},{10,9},{11,1... | collective-permute-start | bytes 46088 | tf_op jit(solution)/shard_map/ppermute | solution.py:20
  243.7 5.0 %collective-permute-start.48 = (f32[5,1,8,128]{3,2,1,0:T(8,128)S(1)}, f32[5,1,8,128]{3,2,1,0:T(8,128)S(1)}, u32[]{:S(2)}, u32[]{:S(2)}) collective-permute-start(f32[5,1,8,128]{3,2,1,0:T(8,128)S(1)} %get-tuple-element.100), channel_id=1, source_target_pairs={{0,32},{32,64},{64,96},{96,128},{128,160},{160,192},{192,224},{224... | collective-permute-start | bytes 61448 | tf_op jit(solution)/shard_map/ppermute | solution.py:18
  246.8 7.2 %collective-permute-start.49 = (f32[5,1,8,128]{3,2,1,0:T(8,128)S(1)}, f32[5,1,8,128]{3,2,1,0:T(8,128)S(1)}, u32[]{:S(2)}, u32[]{:S(2)}) collective-permute-start(f32[5,1,8,128]{3,2,1,0:T(8,128)S(1)} %get-tuple-element.101), channel_id=1, source_target_pairs={{32,0},{64,32},{96,64},{128,96},{160,128},{192,160},{224,192},{256... | collective-permute-start | bytes 61448 | tf_op jit(solution)/shard_map/ppermute | solution.py:20
  254.1 5.0 %collective-permute-start.50 = (f32[5,10,1,128]{3,2,1,0:T(1,128)S(1)}, f32[5,10,1,128]{3,2,1,0:T(1,128)S(1)}, u32[]{:S(2)}, u32[]{:S(2)}) collective-permute-start(f32[5,10,1,128]{3,2,1,0:T(1,128)S(1)} %get-tuple-element.84), channel_id=1, source_target_pairs={{0,1},{1,2},{2,3},{3,4},{4,5},{5,6},{6,7},{7,8},{8,9},{9,10},{10,1... | collective-permute-start | bytes 76808 | tf_op jit(solution)/shard_map/ppermute | solution.py:18
  257.7 4.9 %collective-permute-start.51 = (f32[5,10,1,128]{3,2,1,0:T(1,128)S(1)}, f32[5,10,1,128]{3,2,1,0:T(1,128)S(1)}, u32[]{:S(2)}, u32[]{:S(2)}) collective-permute-start(f32[5,10,1,128]{3,2,1,0:T(1,128)S(1)} %get-tuple-element.85), channel_id=1, source_target_pairs={{1,0},{2,1},{3,2},{4,3},{5,4},{6,5},{7,6},{8,7},{9,8},{10,9},{11,1... | collective-permute-start | bytes 76808 | tf_op jit(solution)/shard_map/ppermute | solution.py:20
  262.9 5.0 %collective-permute-start.52 = (f32[3,1,8,128]{3,2,1,0:T(8,128)S(1)}, f32[3,1,8,128]{3,2,1,0:T(8,128)S(1)}, u32[]{:S(2)}, u32[]{:S(2)}) collective-permute-start(f32[3,1,8,128]{3,2,1,0:T(8,128)S(1)} %get-tuple-element.132), channel_id=1, source_target_pairs={{0,32},{32,64},{64,96},{96,128},{128,160},{160,192},{192,224},{224... | collective-permute-start | bytes 36872 | tf_op jit(solution)/shard_map/ppermute | solution.py:18
  266.0 7.1 %collective-permute-start.53 = (f32[3,1,8,128]{3,2,1,0:T(8,128)S(1)}, f32[3,1,8,128]{3,2,1,0:T(8,128)S(1)}, u32[]{:S(2)}, u32[]{:S(2)}) collective-permute-start(f32[3,1,8,128]{3,2,1,0:T(8,128)S(1)} %get-tuple-element.133), channel_id=1, source_target_pairs={{32,0},{64,32},{96,64},{128,96},{160,128},{192,160},{224,192},{256... | collective-permute-start | bytes 36872 | tf_op jit(solution)/shard_map/ppermute | solution.py:20
  273.2 4.9 %collective-permute-start.54 = (f32[3,10,1,128]{3,2,1,0:T(1,128)S(1)}, f32[3,10,1,128]{3,2,1,0:T(1,128)S(1)}, u32[]{:S(2)}, u32[]{:S(2)}) collective-permute-start(f32[3,10,1,128]{3,2,1,0:T(1,128)S(1)} %get-tuple-element.116), channel_id=1, source_target_pairs={{0,1},{1,2},{2,3},{3,4},{4,5},{5,6},{6,7},{7,8},{8,9},{9,10},{10,1... | collective-permute-start | bytes 46088 | tf_op jit(solution)/shard_map/ppermute | solution.py:18
  276.8 4.8 %collective-permute-start.55 = (f32[3,10,1,128]{3,2,1,0:T(1,128)S(1)}, f32[3,10,1,128]{3,2,1,0:T(1,128)S(1)}, u32[]{:S(2)}, u32[]{:S(2)}) collective-permute-start(f32[3,10,1,128]{3,2,1,0:T(1,128)S(1)} %get-tuple-element.117), channel_id=1, source_target_pairs={{1,0},{2,1},{3,2},{4,3},{5,4},{6,5},{7,6},{8,7},{9,8},{10,9},{11,1... | collective-permute-start | bytes 46088 | tf_op jit(solution)/shard_map/ppermute | solution.py:20
  282.2 5.0 %collective-permute-start.56 = (f32[5,1,8,128]{3,2,1,0:T(8,128)S(1)}, f32[5,1,8,128]{3,2,1,0:T(8,128)S(1)}, u32[]{:S(2)}, u32[]{:S(2)}) collective-permute-start(f32[5,1,8,128]{3,2,1,0:T(8,128)S(1)} %get-tuple-element.98), channel_id=1, source_target_pairs={{0,32},{32,64},{64,96},{96,128},{128,160},{160,192},{192,224},{224... | collective-permute-start | bytes 61448 | tf_op jit(solution)/shard_map/ppermute | solution.py:18
  285.3 7.2 %collective-permute-start.57 = (f32[5,1,8,128]{3,2,1,0:T(8,128)S(1)}, f32[5,1,8,128]{3,2,1,0:T(8,128)S(1)}, u32[]{:S(2)}, u32[]{:S(2)}) collective-permute-start(f32[5,1,8,128]{3,2,1,0:T(8,128)S(1)} %get-tuple-element.99), channel_id=1, source_target_pairs={{32,0},{64,32},{96,64},{128,96},{160,128},{192,160},{224,192},{256... | collective-permute-start | bytes 61448 | tf_op jit(solution)/shard_map/ppermute | solution.py:20
  292.5 5.0 %collective-permute-start.58 = (f32[5,10,1,128]{3,2,1,0:T(1,128)S(1)}, f32[5,10,1,128]{3,2,1,0:T(1,128)S(1)}, u32[]{:S(2)}, u32[]{:S(2)}) collective-permute-start(f32[5,10,1,128]{3,2,1,0:T(1,128)S(1)} %get-tuple-element.82), channel_id=1, source_target_pairs={{0,1},{1,2},{2,3},{3,4},{4,5},{5,6},{6,7},{7,8},{8,9},{9,10},{10,1... | collective-permute-start | bytes 76808 | tf_op jit(solution)/shard_map/ppermute | solution.py:18
  296.2 4.9 %collective-permute-start.59 = (f32[5,10,1,128]{3,2,1,0:T(1,128)S(1)}, f32[5,10,1,128]{3,2,1,0:T(1,128)S(1)}, u32[]{:S(2)}, u32[]{:S(2)}) collective-permute-start(f32[5,10,1,128]{3,2,1,0:T(1,128)S(1)} %get-tuple-element.83), channel_id=1, source_target_pairs={{1,0},{2,1},{3,2},{4,3},{5,4},{6,5},{7,6},{8,7},{9,8},{10,9},{11,1... | collective-permute-start | bytes 76808 | tf_op jit(solution)/shard_map/ppermute | solution.py:20
  301.4 5.0 %collective-permute-start.60 = (f32[3,1,8,128]{3,2,1,0:T(8,128)S(1)}, f32[3,1,8,128]{3,2,1,0:T(8,128)S(1)}, u32[]{:S(2)}, u32[]{:S(2)}) collective-permute-start(f32[3,1,8,128]{3,2,1,0:T(8,128)S(1)} %get-tuple-element.130), channel_id=1, source_target_pairs={{0,32},{32,64},{64,96},{96,128},{128,160},{160,192},{192,224},{224... | collective-permute-start | bytes 36872 | tf_op jit(solution)/shard_map/ppermute | solution.py:18
  304.5 7.1 %collective-permute-start.61 = (f32[3,1,8,128]{3,2,1,0:T(8,128)S(1)}, f32[3,1,8,128]{3,2,1,0:T(8,128)S(1)}, u32[]{:S(2)}, u32[]{:S(2)}) collective-permute-start(f32[3,1,8,128]{3,2,1,0:T(8,128)S(1)} %get-tuple-element.131), channel_id=1, source_target_pairs={{32,0},{64,32},{96,64},{128,96},{160,128},{192,160},{224,192},{256... | collective-permute-start | bytes 36872 | tf_op jit(solution)/shard_map/ppermute | solution.py:20
  311.7 4.9 %collective-permute-start.62 = (f32[3,10,1,128]{3,2,1,0:T(1,128)S(1)}, f32[3,10,1,128]{3,2,1,0:T(1,128)S(1)}, u32[]{:S(2)}, u32[]{:S(2)}) collective-permute-start(f32[3,10,1,128]{3,2,1,0:T(1,128)S(1)} %get-tuple-element.114), channel_id=1, source_target_pairs={{0,1},{1,2},{2,3},{3,4},{4,5},{5,6},{6,7},{7,8},{8,9},{9,10},{10,1... | collective-permute-start | bytes 46088 | tf_op jit(solution)/shard_map/ppermute | solution.py:18
  315.3 4.5 %collective-permute-start.63 = (f32[3,10,1,128]{3,2,1,0:T(1,128)S(1)}, f32[3,10,1,128]{3,2,1,0:T(1,128)S(1)}, u32[]{:S(2)}, u32[]{:S(2)}) collective-permute-start(f32[3,10,1,128]{3,2,1,0:T(1,128)S(1)} %get-tuple-element.115), channel_id=1, source_target_pairs={{1,0},{2,1},{3,2},{4,3},{5,4},{6,5},{7,6},{8,7},{9,8},{10,9},{11,1... | collective-permute-start | bytes 46088 | tf_op jit(solution)/shard_map/ppermute | solution.py:20
  (6 other events, 29.6 us)
where the time goes:
time: 323 us; the launch traced here: 321 us
  starting transfers between devices  168 us (52%)
  waiting for transfers between devices  137 us (42%)
  local copies, waits for them, and re-layouts  7.36 us (2%)
  other arithmetic  5.77 us (2%)
    ppermute x32, waiting for transfers between devices, with_halo(): lax.ppermute(head, axis, [((i + 1) % count, i) for i in range(ends)])  137 us
    ppermute x32, starting transfers between devices, with_halo(): lax.ppermute(tail, axis, [(i, (i + 1) % count) for i in range(ends)])  116 us
    ppermute x32, starting transfers between devices, with_halo(): lax.ppermute(head, axis, [((i + 1) % count, i) for i in range(ends)])  51.4 us
  transfers between devices with their start and end apart: 64, of which 32 were waited for; matrix products, arithmetic and copies ran while one was open for 1% of the time, Pallas kernels for 0%

commit v1 on v0

--- a/solution.py
+++ b/solution.py
@@ -5,38 +5,11 @@
 
 TILE = 8
 COARSE = 2
-
-
-def with_halo(cells, sides, width):
-    for axis, dim in sides:
-        count = lax.axis_size(axis)
-        ends = count - 1
-        head = lax.slice_in_dim(cells, 0, width, axis=dim)
-        tail = lax.slice_in_dim(cells, cells.shape[dim] - width, cells.shape[dim], axis=dim)
-        cells = jnp.concatenate(
-            [
-                lax.ppermute(tail, axis, [(i, (i + 1) % count) for i in range(ends)]),
-                cells,
-                lax.ppermute(head, axis, [((i + 1) % count, i) for i in range(ends)]),
-            ],
-            axis=dim,
-        )
-    return cells
-
-
-def expand_levels(rate_exponent):
-    cells = jnp.repeat(jnp.repeat(rate_exponent, TILE, axis=0), TILE, axis=1)
-    return cells[:, :, None]
+SUBSTEPS = 4
 
 
 def level_scale(exponent):
     return jnp.where(exponent == 2, 0.25, jnp.where(exponent == 1, 0.5, 1.0)).astype(jnp.float32)
-
-
-def substep_active(exponent, sub):
-    odd_sub = sub % 2 == 1
-    last_sub = sub == 3
-    return (exponent == 2) | (exponent == 1) & odd_sub | (exponent >= 0) & last_sub
 
 
 def centre(field):
@@ -97,7 +70,10 @@
 
 
 def advance_velocity(velocity, forces, push_coef, active):
-    return jnp.where(active, velocity + push_coef * forces, velocity)
+    fresh = velocity + push_coef * forces
+    if active is None:
+        return fresh
+    return jnp.where(active, fresh, velocity)
 
 
 def advance_stress(stress, vel_padded, lam_coef, shear_coef, active):
@@ -120,35 +96,58 @@
             stress[5] + (lam_coef * trace_sum + two_shear * strain_z),
         ]
     )
+    if active is None:
+        return fresh
     return jnp.where(active, fresh, stress)
 
 
-def stress_faces(fields):
-    return with_halo(fields, (("gx", 1), ("gy", 2)), 1)
-
-
-def velocity_faces(fields):
-    return with_halo(fields, (("gx", 1), ("gy", 2)), 1)
+def with_blocks(cells, axis, dim):
+    count = lax.axis_size(axis)
+    from_below = lax.ppermute(cells, axis, [(i, i + 1) for i in range(count - 1)])
+    from_above = lax.ppermute(cells, axis, [(i + 1, i) for i in range(count - 1)])
+    return jnp.concatenate([from_below, cells, from_above], axis=dim)
 
 
 def per_device(velocity, stress, buoyancy, lame_lambda, lame_mu, rate_exponent):
-    exponent = expand_levels(rate_exponent)
+    nx, ny = velocity.shape[1], velocity.shape[2]
+    exponent = rate_exponent[0, 0]
     scale = level_scale(exponent)
-    push_coef = buoyancy * scale
-    lam_coef = lame_lambda * scale
-    shear_coef = lame_mu * scale
+    level = jnp.full(buoyancy.shape, exponent.astype(jnp.float32))
+    block = jnp.concatenate(
+        [
+            velocity,
+            stress,
+            (buoyancy * scale)[None],
+            (lame_lambda * scale)[None],
+            (lame_mu * scale)[None],
+            level[None],
+        ],
+        axis=0,
+    )
+    block = with_blocks(block, "gx", 1)
+    block = with_blocks(block, "gy", 2)
+    vel = block[0:3]
+    strs = block[3:9]
+    push, lam, shear, lvl = block[9], block[10], block[11], block[12]
+    widths = ((0, 0), (1, 1), (1, 1), (0, 0))
     for step in range(COARSE):
-        for sub in range(4):
-            active = substep_active(exponent, sub)
-            padded = stress_faces(stress[:5])
-            previous = velocity
-            stress_now = stress
-            velocity = advance_velocity(
-                previous, velocity_forces(padded, stress_now[5]), push_coef, active
-            )
-            vel_padded = velocity_faces(velocity)
-            stress = advance_stress(stress_now, vel_padded, lam_coef, shear_coef, active)
-    return (velocity, stress)
+        for sub in range(SUBSTEPS):
+            if sub == 3:
+                active = None
+            elif sub == 1:
+                active = lvl >= 1.0
+            else:
+                active = lvl == 2.0
+            padded = jnp.pad(strs[:5], widths)
+            vel = advance_velocity(vel, velocity_forces(padded, strs[5]), push, active)
+            vel_padded = jnp.pad(vel, widths)
+            strs = advance_stress(strs, vel_padded, lam, shear, active)
+            vel = vel[:, 1:-1]
+            strs = strs[:, 1:-1]
+            push, lam, shear, lvl = push[1:-1], lam[1:-1], shear[1:-1], lvl[1:-1]
+    vel = vel[:, :, ny : 2 * ny]
+    strs = strs[:, :, ny : 2 * ny]
+    return (vel, strs)
 
 
 def solution(mesh):

time: 323 us -> 76.1 us (0.24)
  the two profiles are of different devices: /device:TPU:7 before, /device:TPU:1 now
where the time goes in v1:
time: 76.1 us; the launch traced here: 75.7 us
  waiting for transfers between devices  31.2 us (41%)
  starting transfers between devices  20 us (26%)
  other arithmetic  12.4 us (16%)
  local copies, waits for them, and re-layouts  9.67 us (13%)
  between operations  2.37 us (3%)
    ppermute x2, waiting for transfers between devices, with_blocks(): lax.ppermute(cells, axis, [(i, i + 1) for i in range(count - 1)])  25.9 us
    ppermute x2, starting transfers between devices, with_blocks(): lax.ppermute(cells, axis, [(i + 1, i) for i in range(count - 1)])  14.1 us
    unnamed x43, other arithmetic  6.67 us
    ppermute x2, starting transfers between devices, with_blocks(): lax.ppermute(cells, axis, [(i, i + 1) for i in range(count - 1)])  5.86 us
    ppermute x2, waiting for transfers between devices, with_blocks(): lax.ppermute(cells, axis, [(i + 1, i) for i in range(count - 1)])  5.28 us
    slice x24, local copies, waits for them, and re-layouts, z_forward(): field[..., 1:]  2.75 us
    another operation x8, other arithmetic, velocity_forces(): return jnp.stack([force_x, force_y, force_z])  2.11 us
    unnamed x5, local copies, waits for them, and re-layouts  1.89 us
  transfers between devices with their start and end apart: 4, of which 3 were waited for; matrix products, arithmetic and copies ran while one was open for 0% of the time, Pallas kernels for 0%

profile of v1, /device:TPU:1, one launch (start us, length us, event | category | flops | bytes accessed | tf_op | source)
XLA Modules:
  0.0 75.7 jit_solution(4499072734221191835)
XLA Ops:
  1.3 0.9 %constant_dynamic-update-slice_fusion.5 = f32[13,8,8,128]{3,2,1,0:T(8,128)S(1)} fusion(f32[3,8,8,128]{3,2,1,0:T(8,128)} %param.6), kind=kLoop, calls=%fused_computation.594 | loop fusion | bytes 196608
  2.2 0.9 %constant_dynamic-update-slice_fusion.4 = f32[13,8,8,128]{3,2,1,0:T(8,128)S(1)} fusion(f32[13,8,8,128]{3,2,1,0:T(8,128)S(1)} %constant_dynamic-update-slice_fusion.5, f32[6,8,8,128]{3,2,1,0:T(8,128)} %param.7), kind=kLoop, calls=%fused_computation.593 | loop fusion | bytes 393216
  3.1 0.8 %constant_dynamic-update-slice_fusion.3 = f32[13,8,8,128]{3,2,1,0:T(8,128)S(1)} fusion(f32[13,8,8,128]{3,2,1,0:T(8,128)S(1)} %constant_dynamic-update-slice_fusion.4, f32[8,8,128]{2,1,0:T(8,128)} %param.8, f32[]{:T(128)} %bitcast), kind=kLoop, calls=%fused_computation.592 | loop fusion | flops 8192 | bytes 65540
  3.9 0.8 %constant_dynamic-update-slice_fusion.2 = f32[13,8,8,128]{3,2,1,0:T(8,128)S(1)} fusion(f32[13,8,8,128]{3,2,1,0:T(8,128)S(1)} %constant_dynamic-update-slice_fusion.3, f32[8,8,128]{2,1,0:T(8,128)} %param.9, f32[]{:T(128)} %bitcast), kind=kLoop, calls=%fused_computation.591 | loop fusion | flops 8192 | bytes 65540
  4.7 0.8 %constant_dynamic-update-slice_fusion.1 = f32[13,8,8,128]{3,2,1,0:T(8,128)S(1)} fusion(f32[13,8,8,128]{3,2,1,0:T(8,128)S(1)} %constant_dynamic-update-slice_fusion.2, f32[8,8,128]{2,1,0:T(8,128)} %param.10, f32[]{:T(128)} %bitcast), kind=kLoop, calls=%fused_computation.590 | loop fusion | flops 8192 | bytes 65540
  5.4 4.5 %collective-permute-start = (f32[13,8,8,128]{3,2,1,0:T(8,128)S(1)}, f32[13,8,8,128]{3,2,1,0:T(8,128)S(1)}, u32[]{:S(2)}, u32[]{:S(2)}) collective-permute-start(f32[13,8,8,128]{3,2,1,0:T(8,128)S(1)} %constant_dynamic-update-slice_fusion), channel_id=1, source_target_pairs={{0,32},{32,64},{64,96},{96,128},{128,160},{160,192},{192,224},{224... | collective-permute-start | bytes 1277960 | tf_op jit(solution)/shard_map/ppermute | solution.py:106
  9.9 12.8 %collective-permute-start.1 = (f32[13,8,8,128]{3,2,1,0:T(8,128)S(1)}, f32[13,8,8,128]{3,2,1,0:T(8,128)S(1)}, u32[]{:S(2)}, u32[]{:S(2)}) collective-permute-start(f32[13,8,8,128]{3,2,1,0:T(8,128)S(1)} %constant_dynamic-update-slice_fusion), channel_id=1, source_target_pairs={{32,0},{64,32},{96,64},{128,96},{160,128},{192,160},{224,192},{256... | collective-permute-start | bytes 1277960 | tf_op jit(solution)/shard_map/ppermute | solution.py:107
  22.8 1.4 %collective-permute-done.1 = f32[13,8,8,128]{3,2,1,0:T(8,128)S(1)} collective-permute-done((f32[13,8,8,128]{3,2,1,0:T(8,128)S(1)}, f32[13,8,8,128]{3,2,1,0:T(8,128)S(1)}, u32[]{:S(2)}, u32[]{:S(2)}) %collective-permute-start.1) | collective-permute-done | bytes 426016 | tf_op jit(solution)/shard_map/ppermute | solution.py:107
  24.2 1.4 %collective-permute-start.2 = (f32[13,24,8,128]{3,2,1,0:T(8,128)S(1)}, f32[13,24,8,128]{3,2,1,0:T(8,128)S(1)}, u32[]{:S(2)}, u32[]{:S(2)}) collective-permute-start(f32[13,24,8,128]{3,2,1,0:T(8,128)S(1)} %pad_maximum_fusion.1), channel_id=1, source_target_pairs={{0,1},{1,2},{2,3},{3,4},{4,5},{5,6},{6,7},{7,8},{8,9},{9,10},{10,1... | collective-permute-start | bytes 3833864 | tf_op jit(solution)/shard_map/ppermute | solution.py:106
  25.6 1.3 %collective-permute-start.3 = (f32[13,24,8,128]{3,2,1,0:T(8,128)S(1)}, f32[13,24,8,128]{3,2,1,0:T(8,128)S(1)}, u32[]{:S(2)}, u32[]{:S(2)}) collective-permute-start(f32[13,24,8,128]{3,2,1,0:T(8,128)S(1)} %pad_maximum_fusion.1), channel_id=1, source_target_pairs={{1,0},{2,1},{3,2},{4,3},{5,4},{6,5},{7,6},{8,7},{9,8},{10,9},{11,1... | collective-permute-start | bytes 3833864 | tf_op jit(solution)/shard_map/ppermute | solution.py:107
  26.9 25.9 %collective-permute-done.2 = f32[13,24,8,128]{3,2,1,0:T(8,128)S(1)} collective-permute-done((f32[13,24,8,128]{3,2,1,0:T(8,128)S(1)}, f32[13,24,8,128]{3,2,1,0:T(8,128)S(1)}, u32[]{:S(2)}, u32[]{:S(2)}) %collective-permute-start.2) | collective-permute-done | bytes 1277984 | tf_op jit(solution)/shard_map/ppermute | solution.py:106
  52.9 3.9 %collective-permute-done.3 = f32[13,24,8,128]{3,2,1,0:T(8,128)S(1)} collective-permute-done((f32[13,24,8,128]{3,2,1,0:T(8,128)S(1)}, f32[13,24,8,128]{3,2,1,0:T(8,128)S(1)}, u32[]{:S(2)}, u32[]{:S(2)}) %collective-permute-start.3) | collective-permute-done | bytes 1277984 | tf_op jit(solution)/shard_map/ppermute | solution.py:107
  56.8 0.3 pad_maximum_fusion
  57.3 0.3 fusion.3
  57.7 0.1 slice.1805
  57.8 0.3 fusion.70
  58.2 0.2 add_select_fusion
  58.3 0.2 fusion.1
  58.6 0.1 slice.1822
  58.7 0.1 slice.1825
  58.9 0.3 fusion.61
  59.2 0.1 fusion.54
  59.4 0.1 fusion.49
  59.5 0.1 fusion.44
  59.7 0.2 bitcast_dynamic-update-slice_fusion
  59.8 0.2 slice_select_fusion
  60.3 0.3 fusion.11
  60.8 0.3 fusion.102
  61.1 0.1 add_select_fusion.1
  61.3 0.1 fusion.9
  61.5 0.1 slice.1860
  61.6 0.1 slice.1863
  61.7 0.2 fusion.93
  62.4 0.2 bitcast_dynamic-update-slice_fusion.1
  62.6 0.2 slice_select_fusion.1
  63.0 0.2 fusion.19
  63.4 0.3 fusion.142
  63.8 0.1 fusion.17
  63.9 0.1 slice.1898
  64.1 0.1 slice.1901
  64.2 0.2 fusion.133
  64.8 0.1 bitcast_dynamic-update-slice_fusion.2
  65.0 0.3 slice_select_fusion.2
  65.5 0.2 fusion.27
  65.8 0.3 fusion.177
  66.6 0.2 constant_dynamic-update-slice_fusion.16
  67.2 0.1 constant_dynamic-update-slice_fusion.11
  67.5 0.1 fusion.35
  67.9 0.3 fusion.216
  68.6 0.2 fusion.207
  69.1 0.1 bitcast_dynamic-update-slice_fusion.3
  69.3 0.1 slice_select_fusion.3
  69.6 0.2 fusion.107
  69.9 0.2 fusion.248
  70.6 0.1 fusion.239
  71.0 0.1 bitcast_dynamic-update-slice_fusion.4
  71.2 0.1 slice_select_fusion.4
  71.4 0.1 fusion.147
  71.7 0.2 fusion.280
  72.3 0.1 fusion.271
  72.9 0.2 slice_select_fusion.5
  73.3 0.2 fusion.312
  73.6 0.7 slice.2071
  75.0 0.7 slice.2091
  (121 shorter events, 7.4 us)
Async XLA Ops:
  5.4 17.3 %collective-permute-start = (f32[13,8,8,128]{3,2,1,0:T(8,128)S(1)}, f32[13,8,8,128]{3,2,1,0:T(8,128)S(1)}, u32[]{:S(2)}, u32[]{:S(2)}) collective-permute-start(f32[13,8,8,128]{3,2,1,0:T(8,128)S(1)} %constant_dynamic-update-slice_fusion), channel_id=1, source_target_pairs={{0,32},{32,64},{64,96},{96,128},{128,160},{160,192},{192,224},{224... | collective-permute-start | bytes 1277960 | tf_op jit(solution)/shard_map/ppermute | solution.py:106
  9.9 14.2 %collective-permute-start.1 = (f32[13,8,8,128]{3,2,1,0:T(8,128)S(1)}, f32[13,8,8,128]{3,2,1,0:T(8,128)S(1)}, u32[]{:S(2)}, u32[]{:S(2)}) collective-permute-start(f32[13,8,8,128]{3,2,1,0:T(8,128)S(1)} %constant_dynamic-update-slice_fusion), channel_id=1, source_target_pairs={{32,0},{64,32},{96,64},{128,96},{160,128},{192,160},{224,192},{256... | collective-permute-start | bytes 1277960 | tf_op jit(solution)/shard_map/ppermute | solution.py:107
  24.2 28.6 %collective-permute-start.2 = (f32[13,24,8,128]{3,2,1,0:T(8,128)S(1)}, f32[13,24,8,128]{3,2,1,0:T(8,128)S(1)}, u32[]{:S(2)}, u32[]{:S(2)}) collective-permute-start(f32[13,24,8,128]{3,2,1,0:T(8,128)S(1)} %pad_maximum_fusion.1), channel_id=1, source_target_pairs={{0,1},{1,2},{2,3},{3,4},{4,5},{5,6},{6,7},{7,8},{8,9},{9,10},{10,1... | collective-permute-start | bytes 3833864 | tf_op jit(solution)/shard_map/ppermute | solution.py:106
  25.6 31.2 %collective-permute-start.3 = (f32[13,24,8,128]{3,2,1,0:T(8,128)S(1)}, f32[13,24,8,128]{3,2,1,0:T(8,128)S(1)}, u32[]{:S(2)}, u32[]{:S(2)}) collective-permute-start(f32[13,24,8,128]{3,2,1,0:T(8,128)S(1)} %pad_maximum_fusion.1), channel_id=1, source_target_pairs={{1,0},{2,1},{3,2},{4,3},{5,4},{6,5},{7,6},{8,7},{9,8},{10,9},{11,1... | collective-permute-start | bytes 3833864 | tf_op jit(solution)/shard_map/ppermute | solution.py:107

commit v2 on v1

--- a/solution.py
+++ b/solution.py
@@ -124,8 +124,8 @@
         ],
         axis=0,
     )
+    block = with_blocks(block, "gy", 2)
     block = with_blocks(block, "gx", 1)
-    block = with_blocks(block, "gy", 2)
     vel = block[0:3]
     strs = block[3:9]
     push, lam, shear, lvl = block[9], block[10], block[11], block[12]

time: 76.1 us -> 68.8 us (0.904)
  the two profiles are of different devices: /device:TPU:1 before, /device:TPU:495 now
where the time goes in v2:
time: 68.8 us; the launch traced here: 68.3 us
  waiting for transfers between devices  30.4 us (44%)
  starting transfers between devices  13.4 us (19%)
  other arithmetic  12.4 us (18%)
  local copies, waits for them, and re-layouts  9.75 us (14%)
  between operations  2.38 us (3%)
    ppermute x2, waiting for transfers between devices, with_blocks(): lax.ppermute(cells, axis, [(i, i + 1) for i in range(count - 1)])  18.8 us
    ppermute x2, waiting for transfers between devices, with_blocks(): lax.ppermute(cells, axis, [(i + 1, i) for i in range(count - 1)])  11.6 us
    ppermute x2, starting transfers between devices, with_blocks(): lax.ppermute(cells, axis, [(i, i + 1) for i in range(count - 1)])  9.56 us
    unnamed x43, other arithmetic  6.8 us
    ppermute x2, starting transfers between devices, with_blocks(): lax.ppermute(cells, axis, [(i + 1, i) for i in range(count - 1)])  3.84 us
    slice x24, local copies, waits for them, and re-layouts, z_forward(): field[..., 1:]  2.75 us
    another operation x8, other arithmetic, velocity_forces(): return jnp.stack([force_x, force_y, force_z])  2.08 us
    unnamed x5, local copies, waits for them, and re-layouts  1.89 us
  transfers between devices with their start and end apart: 4, of which 4 were waited for; matrix products, arithmetic and copies ran while one was open for 0% of the time, Pallas kernels for 0%

profile of v2, /device:TPU:495, one launch (start us, length us, event | category | flops | bytes accessed | tf_op | source)
XLA Modules:
  0.0 68.3 jit_solution(984912710110248139)
XLA Ops:
  1.3 0.9 %constant_dynamic-update-slice_fusion.5 = f32[13,8,8,128]{3,2,1,0:T(8,128)S(1)} fusion(f32[3,8,8,128]{3,2,1,0:T(8,128)} %param.6), kind=kLoop, calls=%fused_computation.594 | loop fusion | bytes 196608
  2.2 0.9 %constant_dynamic-update-slice_fusion.4 = f32[13,8,8,128]{3,2,1,0:T(8,128)S(1)} fusion(f32[13,8,8,128]{3,2,1,0:T(8,128)S(1)} %constant_dynamic-update-slice_fusion.5, f32[6,8,8,128]{3,2,1,0:T(8,128)} %param.7), kind=kLoop, calls=%fused_computation.593 | loop fusion | bytes 393216
  3.1 0.8 %constant_dynamic-update-slice_fusion.3 = f32[13,8,8,128]{3,2,1,0:T(8,128)S(1)} fusion(f32[13,8,8,128]{3,2,1,0:T(8,128)S(1)} %constant_dynamic-update-slice_fusion.4, f32[8,8,128]{2,1,0:T(8,128)} %param.8, f32[]{:T(128)} %bitcast), kind=kLoop, calls=%fused_computation.592 | loop fusion | flops 8192 | bytes 65540
  3.9 0.8 %constant_dynamic-update-slice_fusion.2 = f32[13,8,8,128]{3,2,1,0:T(8,128)S(1)} fusion(f32[13,8,8,128]{3,2,1,0:T(8,128)S(1)} %constant_dynamic-update-slice_fusion.3, f32[8,8,128]{2,1,0:T(8,128)} %param.9, f32[]{:T(128)} %bitcast), kind=kLoop, calls=%fused_computation.591 | loop fusion | flops 8192 | bytes 65540
  4.7 0.8 %constant_dynamic-update-slice_fusion.1 = f32[13,8,8,128]{3,2,1,0:T(8,128)S(1)} fusion(f32[13,8,8,128]{3,2,1,0:T(8,128)S(1)} %constant_dynamic-update-slice_fusion.2, f32[8,8,128]{2,1,0:T(8,128)} %param.10, f32[]{:T(128)} %bitcast), kind=kLoop, calls=%fused_computation.590 | loop fusion | flops 8192 | bytes 65540
  5.4 4.7 %collective-permute-start = (f32[13,8,8,128]{3,2,1,0:T(8,128)S(1)}, f32[13,8,8,128]{3,2,1,0:T(8,128)S(1)}, u32[]{:S(2)}, u32[]{:S(2)}) collective-permute-start(f32[13,8,8,128]{3,2,1,0:T(8,128)S(1)} %constant_dynamic-update-slice_fusion), channel_id=1, source_target_pairs={{0,1},{1,2},{2,3},{3,4},{4,5},{5,6},{6,7},{7,8},{8,9},{9,10},{10,1... | collective-permute-start | bytes 1277960 | tf_op jit(solution)/shard_map/ppermute | solution.py:106
  10.2 1.9 %collective-permute-start.1 = (f32[13,8,8,128]{3,2,1,0:T(8,128)S(1)}, f32[13,8,8,128]{3,2,1,0:T(8,128)S(1)}, u32[]{:S(2)}, u32[]{:S(2)}) collective-permute-start(f32[13,8,8,128]{3,2,1,0:T(8,128)S(1)} %constant_dynamic-update-slice_fusion), channel_id=1, source_target_pairs={{1,0},{2,1},{3,2},{4,3},{5,4},{6,5},{7,6},{8,7},{9,8},{10,9},{11,1... | collective-permute-start | bytes 1277960 | tf_op jit(solution)/shard_map/ppermute | solution.py:107
  12.1 6.6 %collective-permute-done = f32[13,8,8,128]{3,2,1,0:T(8,128)S(1)} collective-permute-done((f32[13,8,8,128]{3,2,1,0:T(8,128)S(1)}, f32[13,8,8,128]{3,2,1,0:T(8,128)S(1)}, u32[]{:S(2)}, u32[]{:S(2)}) %collective-permute-start) | collective-permute-done | bytes 426016 | tf_op jit(solution)/shard_map/ppermute | solution.py:106
  18.7 5.0 %collective-permute-done.1 = f32[13,8,8,128]{3,2,1,0:T(8,128)S(1)} collective-permute-done((f32[13,8,8,128]{3,2,1,0:T(8,128)S(1)}, f32[13,8,8,128]{3,2,1,0:T(8,128)S(1)}, u32[]{:S(2)}, u32[]{:S(2)}) %collective-permute-start.1) | collective-permute-done | bytes 426016 | tf_op jit(solution)/shard_map/ppermute | solution.py:107
  23.8 4.8 %collective-permute-start.2 = (f32[13,8,24,128]{3,2,1,0:T(8,128)S(1)}, f32[13,8,24,128]{3,2,1,0:T(8,128)S(1)}, u32[]{:S(2)}, u32[]{:S(2)}) collective-permute-start(f32[13,8,24,128]{3,2,1,0:T(8,128)S(1)} %pad_maximum_fusion.1), channel_id=1, source_target_pairs={{0,32},{32,64},{64,96},{96,128},{128,160},{160,192},{192,224},{224... | collective-permute-start | bytes 3833864 | tf_op jit(solution)/shard_map/ppermute | solution.py:106
  28.6 1.9 %collective-permute-start.3 = (f32[13,8,24,128]{3,2,1,0:T(8,128)S(1)}, f32[13,8,24,128]{3,2,1,0:T(8,128)S(1)}, u32[]{:S(2)}, u32[]{:S(2)}) collective-permute-start(f32[13,8,24,128]{3,2,1,0:T(8,128)S(1)} %pad_maximum_fusion.1), channel_id=1, source_target_pairs={{32,0},{64,32},{96,64},{128,96},{160,128},{192,160},{224,192},{256... | collective-permute-start | bytes 3833864 | tf_op jit(solution)/shard_map/ppermute | solution.py:107
  30.6 12.3 %collective-permute-done.2 = f32[13,8,24,128]{3,2,1,0:T(8,128)S(1)} collective-permute-done((f32[13,8,24,128]{3,2,1,0:T(8,128)S(1)}, f32[13,8,24,128]{3,2,1,0:T(8,128)S(1)}, u32[]{:S(2)}, u32[]{:S(2)}) %collective-permute-start.2) | collective-permute-done | bytes 1277984 | tf_op jit(solution)/shard_map/ppermute | solution.py:106
  42.8 6.5 %collective-permute-done.3 = f32[13,8,24,128]{3,2,1,0:T(8,128)S(1)} collective-permute-done((f32[13,8,24,128]{3,2,1,0:T(8,128)S(1)}, f32[13,8,24,128]{3,2,1,0:T(8,128)S(1)}, u32[]{:S(2)}, u32[]{:S(2)}) %collective-permute-start.3) | collective-permute-done | bytes 1277984 | tf_op jit(solution)/shard_map/ppermute | solution.py:107
  49.3 0.3 pad_maximum_fusion
  49.8 0.3 fusion.3
  50.2 0.1 slice.1805
  50.4 0.3 fusion.70
  50.8 0.2 fusion.1
  51.0 0.1 slice.1822
  51.2 0.1 slice.1825
  51.3 0.3 fusion.61
  51.7 0.1 fusion.54
  51.8 0.1 fusion.49
  52.0 0.1 fusion.44
  52.1 0.2 bitcast_dynamic-update-slice_fusion
  52.3 0.2 slice_select_fusion
  52.7 0.3 fusion.11
  53.2 0.3 fusion.102
  53.5 0.1 add_select_fusion.1
  53.7 0.1 fusion.9
  53.9 0.1 slice.1860
  54.0 0.1 slice.1863
  54.1 0.2 fusion.93
  54.6 0.1 fusion.81
  54.7 0.1 fusion.76
  54.9 0.2 bitcast_dynamic-update-slice_fusion.1
  55.1 0.2 slice_select_fusion.1
  55.4 0.2 fusion.19
  55.8 0.3 fusion.142
  56.3 0.1 fusion.17
  56.7 0.2 fusion.133
  57.3 0.1 bitcast_dynamic-update-slice_fusion.2
  57.5 0.2 slice_select_fusion.2
  57.8 0.2 fusion.27
  58.2 0.3 fusion.177
  59.0 0.2 constant_dynamic-update-slice_fusion.16
  59.6 0.1 constant_dynamic-update-slice_fusion.11
  60.0 0.2 fusion.35
  60.4 0.3 fusion.216
  61.1 0.2 fusion.207
  61.7 0.1 bitcast_dynamic-update-slice_fusion.3
  61.8 0.2 slice_select_fusion.3
  62.1 0.2 fusion.107
  62.4 0.2 fusion.248
  63.1 0.2 fusion.239
  63.6 0.1 bitcast_dynamic-update-slice_fusion.4
  63.7 0.1 slice_select_fusion.4
  64.0 0.1 fusion.147
  64.3 0.2 fusion.280
  64.9 0.1 fusion.271
  65.5 0.2 slice_select_fusion.5
  65.9 0.2 fusion.312
  66.2 0.7 slice.2071
  67.6 0.7 %slice.2091 = f32[6,8,8,128]{3,2,1,0:T(8,128)} slice(f32[6,10,24,128]{3,2,1,0:T(8,128)S(1)} %constant_dynamic-update-slice_fusion.17), slice={[0:6], [1:9], [8:16], [0:128]} | slice | bytes 393216 | tf_op jit(solution)/shard_map/slice | solution.py:149
  (121 shorter events, 7.7 us)
Async XLA Ops:
  5.4 13.2 %collective-permute-start = (f32[13,8,8,128]{3,2,1,0:T(8,128)S(1)}, f32[13,8,8,128]{3,2,1,0:T(8,128)S(1)}, u32[]{:S(2)}, u32[]{:S(2)}) collective-permute-start(f32[13,8,8,128]{3,2,1,0:T(8,128)S(1)} %constant_dynamic-update-slice_fusion), channel_id=1, source_target_pairs={{0,1},{1,2},{2,3},{3,4},{4,5},{5,6},{6,7},{7,8},{8,9},{9,10},{10,1... | collective-permute-start | bytes 1277960 | tf_op jit(solution)/shard_map/ppermute | solution.py:106
  10.2 13.5 %collective-permute-start.1 = (f32[13,8,8,128]{3,2,1,0:T(8,128)S(1)}, f32[13,8,8,128]{3,2,1,0:T(8,128)S(1)}, u32[]{:S(2)}, u32[]{:S(2)}) collective-permute-start(f32[13,8,8,128]{3,2,1,0:T(8,128)S(1)} %constant_dynamic-update-slice_fusion), channel_id=1, source_target_pairs={{1,0},{2,1},{3,2},{4,3},{5,4},{6,5},{7,6},{8,7},{9,8},{10,9},{11,1... | collective-permute-start | bytes 1277960 | tf_op jit(solution)/shard_map/ppermute | solution.py:107
  23.8 19.0 %collective-permute-start.2 = (f32[13,8,24,128]{3,2,1,0:T(8,128)S(1)}, f32[13,8,24,128]{3,2,1,0:T(8,128)S(1)}, u32[]{:S(2)}, u32[]{:S(2)}) collective-permute-start(f32[13,8,24,128]{3,2,1,0:T(8,128)S(1)} %pad_maximum_fusion.1), channel_id=1, source_target_pairs={{0,32},{32,64},{64,96},{96,128},{128,160},{160,192},{192,224},{224... | collective-permute-start | bytes 3833864 | tf_op jit(solution)/shard_map/ppermute | solution.py:106
  28.6 20.7 %collective-permute-start.3 = (f32[13,8,24,128]{3,2,1,0:T(8,128)S(1)}, f32[13,8,24,128]{3,2,1,0:T(8,128)S(1)}, u32[]{:S(2)}, u32[]{:S(2)}) collective-permute-start(f32[13,8,24,128]{3,2,1,0:T(8,128)S(1)} %pad_maximum_fusion.1), channel_id=1, source_target_pairs={{32,0},{64,32},{96,64},{128,96},{160,128},{192,160},{224,192},{256... | collective-permute-start | bytes 3833864 | tf_op jit(solution)/shard_map/ppermute | solution.py:107

commit v3 on v2

--- a/solution.py
+++ b/solution.py
@@ -2,6 +2,8 @@
 import jax.numpy as jnp
 from jax import lax
 from jax.sharding import PartitionSpec as P
+from jax.experimental import pallas as pl
+from jax.experimental.pallas import tpu as pltpu
 
 TILE = 8
 COARSE = 2
@@ -108,6 +110,156 @@
     return jnp.concatenate([from_below, cells, from_above], axis=dim)
 
 
+INTERPRET = False
+YOFF = 8
+
+
+def lane_shifts(shape):
+    lane = lax.broadcasted_iota(jnp.int32, shape, len(shape) - 1)
+    width = shape[-1]
+    from_below = pltpu.roll(lane, 1, len(shape) - 1) == (lane + (width - 1)) % width
+    first = lane == 0
+    last = lane == width - 1
+    axis = len(shape) - 1
+
+    def z_backward(f):
+        one, back = pltpu.roll(f, 1, axis), pltpu.roll(f, width - 1, axis)
+        prev = jnp.where(first, 0.0, jnp.where(from_below, one, back))
+        return f - prev
+
+    def z_forward(f):
+        one, back = pltpu.roll(f, 1, axis), pltpu.roll(f, width - 1, axis)
+        nxt = jnp.where(last, 0.0, jnp.where(from_below, back, one))
+        return nxt - f
+
+    return z_backward, z_forward
+
+
+def substeps_kernel(ext_ref, vel_out, strs_out, vbuf, sbuf):
+    rows, cols, depth = ext_ref.shape[1], ext_ref.shape[2], ext_ref.shape[3]
+    ny = vel_out.shape[2]
+    nx = vel_out.shape[1]
+    halo = (rows - nx) // 2
+    pad_rows = vbuf.shape[2] - cols - YOFF
+    zero_y = jnp.zeros((vbuf.shape[1], YOFF, depth), jnp.float32)
+    zero_y2 = jnp.zeros((vbuf.shape[1], pad_rows, depth), jnp.float32)
+    zero_x = jnp.zeros((1, vbuf.shape[2], depth), jnp.float32)
+    for buf, count in ((vbuf, 3), (sbuf, 6)):
+        for c in range(count):
+            buf[c, :, 0:YOFF, :] = zero_y
+            buf[c, :, YOFF + cols :, :] = zero_y2
+            buf[c, 0:1, :, :] = zero_x
+            buf[c, rows + 1 : rows + 2, :, :] = zero_x
+    for c in range(3):
+        vbuf[c, 1 : rows + 1, YOFF : YOFF + cols, :] = ext_ref[c]
+    for c in range(6):
+        sbuf[c, 1 : rows + 1, YOFF : YOFF + cols, :] = ext_ref[3 + c]
+    z_backward, z_forward = lane_shifts((1, cols, depth))
+    ys = pl.ds(YOFF, cols)
+    ym = pl.ds(YOFF - 1, cols)
+    yp = pl.ds(YOFF + 1, cols)
+
+    def mask_of(sub, r):
+        if sub == 3:
+            return None
+        lvl = ext_ref[12, pl.ds(r, 1), :, :]
+        return lvl >= 1.0 if sub == 1 else lvl == 2.0
+
+    def keep(active, fresh, old):
+        return fresh if active is None else jnp.where(active, fresh, old)
+
+    for step in range(COARSE):
+        for sub in range(SUBSTEPS):
+            t = step * SUBSTEPS + sub
+            lo, hi = t + 1, rows + 1 - t
+
+            def vel_row(b, carry, sub=sub):
+                r = b - 1
+                sxx_c = sbuf[0, pl.ds(b, 1), ys, :]
+                sxx_px = sbuf[0, pl.ds(b + 1, 1), ys, :]
+                syy_c = sbuf[1, pl.ds(b, 1), ys, :]
+                syy_py = sbuf[1, pl.ds(b, 1), yp, :]
+                sxy_c = sbuf[2, pl.ds(b, 1), ys, :]
+                sxy_my = sbuf[2, pl.ds(b, 1), ym, :]
+                sxy_mx = sbuf[2, pl.ds(b - 1, 1), ys, :]
+                sxz_c = sbuf[3, pl.ds(b, 1), ys, :]
+                sxz_mx = sbuf[3, pl.ds(b - 1, 1), ys, :]
+                syz_c = sbuf[4, pl.ds(b, 1), ys, :]
+                syz_my = sbuf[4, pl.ds(b, 1), ym, :]
+                szz_c = sbuf[5, pl.ds(b, 1), ys, :]
+                force_x = sxx_px - sxx_c + (sxy_c - sxy_my) + z_backward(sxz_c)
+                force_y = sxy_c - sxy_mx + (syy_py - syy_c) + z_backward(syz_c)
+                force_z = sxz_c - sxz_mx + (syz_c - syz_my) + z_forward(szz_c)
+                push = ext_ref[9, pl.ds(r, 1), :, :]
+                active = mask_of(sub, r)
+                for c, force in enumerate((force_x, force_y, force_z)):
+                    old = vbuf[c, pl.ds(b, 1), ys, :]
+                    vbuf[c, pl.ds(b, 1), ys, :] = keep(active, old + push * force, old)
+                return carry
+
+            lax.fori_loop(lo, hi, vel_row, 0)
+
+            def strs_row(b, carry, sub=sub):
+                r = b - 1
+                vx_c = vbuf[0, pl.ds(b, 1), ys, :]
+                vx_mx = vbuf[0, pl.ds(b - 1, 1), ys, :]
+                vx_py = vbuf[0, pl.ds(b, 1), yp, :]
+                vy_c = vbuf[1, pl.ds(b, 1), ys, :]
+                vy_my = vbuf[1, pl.ds(b, 1), ym, :]
+                vy_px = vbuf[1, pl.ds(b + 1, 1), ys, :]
+                vz_c = vbuf[2, pl.ds(b, 1), ys, :]
+                vz_px = vbuf[2, pl.ds(b + 1, 1), ys, :]
+                vz_py = vbuf[2, pl.ds(b, 1), yp, :]
+                strain_x = vx_c - vx_mx
+                strain_y = vy_c - vy_my
+                strain_z = z_backward(vz_c)
+                shear_xy = vx_py - vx_c + (vy_px - vy_c)
+                shear_xz = z_forward(vx_c) + (vz_px - vz_c)
+                shear_yz = z_forward(vy_c) + (vz_py - vz_c)
+                trace_sum = strain_x + strain_y + strain_z
+                lam = ext_ref[10, pl.ds(r, 1), :, :]
+                shear = ext_ref[11, pl.ds(r, 1), :, :]
+                two_shear = 2.0 * shear
+                adds = (
+                    lam * trace_sum + two_shear * strain_x,
+                    lam * trace_sum + two_shear * strain_y,
+                    shear * shear_xy,
+                    shear * shear_xz,
+                    shear * shear_yz,
+                    lam * trace_sum + two_shear * strain_z,
+                )
+                active = mask_of(sub, r)
+                for c, add in enumerate(adds):
+                    old = sbuf[c, pl.ds(b, 1), ys, :]
+                    sbuf[c, pl.ds(b, 1), ys, :] = keep(active, old + add, old)
+                return carry
+
+            lax.fori_loop(lo, hi, strs_row, 0)
+
+    xs = slice(halo + 1, halo + 1 + nx)
+    yc = slice(YOFF + halo, YOFF + halo + ny)
+    for c in range(3):
+        vel_out[c] = vbuf[c, xs, yc, :]
+    for c in range(6):
+        strs_out[c] = sbuf[c, xs, yc, :]
+
+
+def substeps(ext, nx, ny):
+    fields, rows, cols, depth = ext.shape
+    return pl.pallas_call(
+        substeps_kernel,
+        out_shape=(
+            jax.ShapeDtypeStruct((3, nx, ny, depth), jnp.float32),
+            jax.ShapeDtypeStruct((6, nx, ny, depth), jnp.float32),
+        ),
+        scratch_shapes=[
+            pltpu.VMEM((3, rows + 2, cols + 2 * YOFF, depth), jnp.float32),
+            pltpu.VMEM((6, rows + 2, cols + 2 * YOFF, depth), jnp.float32),
+        ],
+        interpret=INTERPRET,
+    )(ext)
+
+
 def per_device(velocity, stress, buoyancy, lame_lambda, lame_mu, rate_exponent):
     nx, ny = velocity.shape[1], velocity.shape[2]
     exponent = rate_exponent[0, 0]
@@ -126,28 +278,7 @@
     )
     block = with_blocks(block, "gy", 2)
     block = with_blocks(block, "gx", 1)
-    vel = block[0:3]
-    strs = block[3:9]
-    push, lam, shear, lvl = block[9], block[10], block[11], block[12]
-    widths = ((0, 0), (1, 1), (1, 1), (0, 0))
-    for step in range(COARSE):
-        for sub in range(SUBSTEPS):
-            if sub == 3:
-                active = None
-            elif sub == 1:
-                active = lvl >= 1.0
-            else:
-                active = lvl == 2.0
-            padded = jnp.pad(strs[:5], widths)
-            vel = advance_velocity(vel, velocity_forces(padded, strs[5]), push, active)
-            vel_padded = jnp.pad(vel, widths)
-            strs = advance_stress(strs, vel_padded, lam, shear, active)
-            vel = vel[:, 1:-1]
-            strs = strs[:, 1:-1]
-            push, lam, shear, lvl = push[1:-1], lam[1:-1], shear[1:-1], lvl[1:-1]
-    vel = vel[:, :, ny : 2 * ny]
-    strs = strs[:, :, ny : 2 * ny]
-    return (vel, strs)
+    return substeps(block, nx, ny)
 
 
 def solution(mesh):

time: 68.8 us -> 80.7 us (1.17)
  the two profiles are of different devices: /device:TPU:495 before, /device:TPU:1 now
where the time goes in v3:
time: 80.7 us; the launch traced here: 79.7 us
  Pallas kernels  28.4 us (35%)
  starting transfers between devices  24.4 us (30%)
  waiting for transfers between devices  19.2 us (24%)
  other arithmetic  4.51 us (6%)
  local copies, waits for them, and re-layouts  1.84 us (2%)
  between operations  1.34 us (2%)
    pallas_call x1, Pallas kernels, substeps(): pl.pallas_call(substeps_kernel, out_shape=(jax.ShapeDtypeStruct((3, nx, n...  28.4 us
    ppermute x2, starting transfers between devices, with_blocks(): lax.ppermute(cells, axis, [(i + 1, i) for i in range(count - 1)])  17.4 us
    ppermute x2, waiting for transfers between devices, with_blocks(): lax.ppermute(cells, axis, [(i, i + 1) for i in range(count - 1)])  10.8 us
    ppermute x2, waiting for transfers between devices, with_blocks(): lax.ppermute(cells, axis, [(i + 1, i) for i in range(count - 1)])  8.36 us
    ppermute x2, starting transfers between devices, with_blocks(): lax.ppermute(cells, axis, [(i, i + 1) for i in range(count - 1)])  6.93 us
    unnamed x3, other arithmetic  2.29 us
    concatenate x2, other arithmetic, with_blocks(): return jnp.concatenate([from_below, cells, from_above], axis=dim)  2.22 us
    unnamed x2, local copies, waits for them, and re-layouts  1.84 us
  transfers between devices with their start and end apart: 4, of which 4 were waited for; matrix products, arithmetic and copies ran while one was open for 0% of the time, Pallas kernels for 0%

profile of v3, /device:TPU:1, one launch (start us, length us, event | category | flops | bytes accessed | tf_op | source)
XLA Modules:
  0.0 79.7 jit_solution(11596502586514582820)
XLA Ops:
  1.3 0.9 %constant_dynamic-update-slice_fusion.1 = f32[13,8,8,128]{3,2,1,0:T(8,128)S(1)} fusion(f32[3,8,8,128]{3,2,1,0:T(8,128)} %param.6), kind=kLoop, calls=%fused_computation.7 | loop fusion | bytes 196608
  2.2 0.9 %constant_dynamic-update-slice_fusion = f32[13,8,8,128]{3,2,1,0:T(8,128)S(1)} fusion(f32[13,8,8,128]{3,2,1,0:T(8,128)S(1)} %constant_dynamic-update-slice_fusion.1, f32[6,8,8,128]{3,2,1,0:T(8,128)} %param.7), kind=kLoop, calls=%fused_computation.6 | loop fusion | bytes 393216
  3.1 0.8 bitcast_dynamic-update-slice_fusion.2
  3.9 0.8 bitcast_dynamic-update-slice_fusion.1
  4.7 0.8 bitcast_dynamic-update-slice_fusion
  5.4 1.3 %collective-permute-start.1 = (f32[13,8,8,128]{3,2,1,0:T(8,128)S(1)}, f32[13,8,8,128]{3,2,1,0:T(8,128)S(1)}, u32[]{:S(2)}, u32[]{:S(2)}) collective-permute-start(f32[13,8,8,128]{3,2,1,0:T(8,128)S(1)} %broadcast_dynamic-update-slice_fusion), channel_id=1, source_target_pairs={{1,0},{2,1},{3,2},{4,3},{5,4},{6,5},{7,6},{8,7},{9,8},{10,9},{11,1... | collective-permute-start | bytes 1277960 | tf_op jit(solution)/shard_map/ppermute | solution.py:109
  6.7 5.0 %collective-permute-start = (f32[13,8,8,128]{3,2,1,0:T(8,128)S(1)}, f32[13,8,8,128]{3,2,1,0:T(8,128)S(1)}, u32[]{:S(2)}, u32[]{:S(2)}) collective-permute-start(f32[13,8,8,128]{3,2,1,0:T(8,128)S(1)} %broadcast_dynamic-update-slice_fusion), channel_id=1, source_target_pairs={{0,1},{1,2},{2,3},{3,4},{4,5},{5,6},{6,7},{7,8},{8,9},{9,10},{10,1... | collective-permute-start | bytes 1277960 | tf_op jit(solution)/shard_map/ppermute | solution.py:108
  11.7 3.6 %collective-permute-done.1 = f32[13,8,8,128]{3,2,1,0:T(8,128)S(1)} collective-permute-done((f32[13,8,8,128]{3,2,1,0:T(8,128)S(1)}, f32[13,8,8,128]{3,2,1,0:T(8,128)S(1)}, u32[]{:S(2)}, u32[]{:S(2)}) %collective-permute-start.1) | collective-permute-done | bytes 426016 | tf_op jit(solution)/shard_map/ppermute | solution.py:109
  15.3 1.5 %collective-permute-done = f32[13,8,8,128]{3,2,1,0:T(8,128)S(1)} collective-permute-done((f32[13,8,8,128]{3,2,1,0:T(8,128)S(1)}, f32[13,8,8,128]{3,2,1,0:T(8,128)S(1)}, u32[]{:S(2)}, u32[]{:S(2)}) %collective-permute-start) | collective-permute-done | bytes 426016 | tf_op jit(solution)/shard_map/ppermute | solution.py:108
  16.8 0.1 pad_maximum_fusion.1
  16.9 16.2 %collective-permute-start.3 = (f32[13,8,24,128]{3,2,1,0:T(8,128)S(1)}, f32[13,8,24,128]{3,2,1,0:T(8,128)S(1)}, u32[]{:S(2)}, u32[]{:S(2)}) collective-permute-start(f32[13,8,24,128]{3,2,1,0:T(8,128)S(1)} %pad_maximum_fusion.1), channel_id=1, source_target_pairs={{32,0},{64,32},{96,64},{128,96},{160,128},{192,160},{224,192},{256... | collective-permute-start | bytes 3833864 | tf_op jit(solution)/shard_map/ppermute | solution.py:109
  33.0 1.9 %collective-permute-start.2 = (f32[13,8,24,128]{3,2,1,0:T(8,128)S(1)}, f32[13,8,24,128]{3,2,1,0:T(8,128)S(1)}, u32[]{:S(2)}, u32[]{:S(2)}) collective-permute-start(f32[13,8,24,128]{3,2,1,0:T(8,128)S(1)} %pad_maximum_fusion.1), channel_id=1, source_target_pairs={{0,32},{32,64},{64,96},{96,128},{128,160},{160,192},{192,224},{224... | collective-permute-start | bytes 3833864 | tf_op jit(solution)/shard_map/ppermute | solution.py:108
  35.0 4.8 %collective-permute-done.3 = f32[13,8,24,128]{3,2,1,0:T(8,128)S(1)} collective-permute-done((f32[13,8,24,128]{3,2,1,0:T(8,128)S(1)}, f32[13,8,24,128]{3,2,1,0:T(8,128)S(1)}, u32[]{:S(2)}, u32[]{:S(2)}) %collective-permute-start.3) | collective-permute-done | bytes 1277984 | tf_op jit(solution)/shard_map/ppermute | solution.py:109
  39.8 9.4 %collective-permute-done.2 = f32[13,8,24,128]{3,2,1,0:T(8,128)S(1)} collective-permute-done((f32[13,8,24,128]{3,2,1,0:T(8,128)S(1)}, f32[13,8,24,128]{3,2,1,0:T(8,128)S(1)}, u32[]{:S(2)}, u32[]{:S(2)}) %collective-permute-start.2) | collective-permute-done | bytes 1277984 | tf_op jit(solution)/shard_map/ppermute | solution.py:108
  49.1 2.1 %pad_maximum_fusion.ext_ref = f32[13,24,24,128]{3,2,1,0:T(8,128)} fusion(f32[13,8,24,128]{3,2,1,0:T(8,128)S(1)} %collective-permute-done.3, f32[13,8,8,128]{3,2,1,0:T(8,128)S(1)} %collective-permute-done.1, f32[13,8,8,128]{3,2,1,0:T(8,128)S(1)} %broadcast_dynamic-update-slice_fusion, f32[13,8,8,128]{3,2,1,0:T(8,128)S(1)} %collective-permute-done, ...), kind=kLoop, calls=%fused_computation | loop fusion | flops 3833856 | bytes 7667712 | tf_op jit(solution)/shard_map/concatenate | solution.py:110
  51.3 28.4 %shard_map.77 = (f32[3,8,8,128]{3,2,1,0:T(8,128)}, f32[6,8,8,128]{3,2,1,0:T(8,128)}) custom-call(f32[13,24,24,128]{3,2,1,0:T(8,128)} %pad_maximum_fusion.ext_ref), custom_call_target="tpu_custom_call" | custom-call | tf_op jit(solution)/shard_map/pallas_call | solution.py:249
  (1 shorter events, 0.0 us)
Async XLA Ops:
  5.4 9.9 %collective-permute-start.1 = (f32[13,8,8,128]{3,2,1,0:T(8,128)S(1)}, f32[13,8,8,128]{3,2,1,0:T(8,128)S(1)}, u32[]{:S(2)}, u32[]{:S(2)}) collective-permute-start(f32[13,8,8,128]{3,2,1,0:T(8,128)S(1)} %broadcast_dynamic-update-slice_fusion), channel_id=1, source_target_pairs={{1,0},{2,1},{3,2},{4,3},{5,4},{6,5},{7,6},{8,7},{9,8},{10,9},{11,1... | collective-permute-start | bytes 1277960 | tf_op jit(solution)/shard_map/ppermute | solution.py:109
  6.7 10.1 %collective-permute-start = (f32[13,8,8,128]{3,2,1,0:T(8,128)S(1)}, f32[13,8,8,128]{3,2,1,0:T(8,128)S(1)}, u32[]{:S(2)}, u32[]{:S(2)}) collective-permute-start(f32[13,8,8,128]{3,2,1,0:T(8,128)S(1)} %broadcast_dynamic-update-slice_fusion), channel_id=1, source_target_pairs={{0,1},{1,2},{2,3},{3,4},{4,5},{5,6},{6,7},{7,8},{8,9},{9,10},{10,1... | collective-permute-start | bytes 1277960 | tf_op jit(solution)/shard_map/ppermute | solution.py:108
  16.9 22.9 %collective-permute-start.3 = (f32[13,8,24,128]{3,2,1,0:T(8,128)S(1)}, f32[13,8,24,128]{3,2,1,0:T(8,128)S(1)}, u32[]{:S(2)}, u32[]{:S(2)}) collective-permute-start(f32[13,8,24,128]{3,2,1,0:T(8,128)S(1)} %pad_maximum_fusion.1), channel_id=1, source_target_pairs={{32,0},{64,32},{96,64},{128,96},{160,128},{192,160},{224,192},{256... | collective-permute-start | bytes 3833864 | tf_op jit(solution)/shard_map/ppermute | solution.py:109
  33.0 16.1 %collective-permute-start.2 = (f32[13,8,24,128]{3,2,1,0:T(8,128)S(1)}, f32[13,8,24,128]{3,2,1,0:T(8,128)S(1)}, u32[]{:S(2)}, u32[]{:S(2)}) collective-permute-start(f32[13,8,24,128]{3,2,1,0:T(8,128)S(1)} %pad_maximum_fusion.1), channel_id=1, source_target_pairs={{0,32},{32,64},{64,96},{96,128},{128,160},{160,192},{192,224},{224... | collective-permute-start | bytes 3833864 | tf_op jit(solution)/shard_map/ppermute | solution.py:108

commit v4 on v3

--- a/solution.py
+++ b/solution.py
@@ -135,8 +135,9 @@
     return z_backward, z_forward
 
 
-def substeps_kernel(ext_ref, vel_out, strs_out, vbuf, sbuf):
-    rows, cols, depth = ext_ref.shape[1], ext_ref.shape[2], ext_ref.shape[3]
+def substeps_kernel(below_ref, mid_ref, above_ref, vel_out, strs_out, vbuf, sbuf, ext_ref):
+    piece = mid_ref.shape[1]
+    rows, cols, depth = 3 * piece, mid_ref.shape[2], mid_ref.shape[3]
     ny = vel_out.shape[2]
     nx = vel_out.shape[1]
     halo = (rows - nx) // 2
@@ -150,10 +151,14 @@
             buf[c, :, YOFF + cols :, :] = zero_y2
             buf[c, 0:1, :, :] = zero_x
             buf[c, rows + 1 : rows + 2, :, :] = zero_x
-    for c in range(3):
-        vbuf[c, 1 : rows + 1, YOFF : YOFF + cols, :] = ext_ref[c]
-    for c in range(6):
-        sbuf[c, 1 : rows + 1, YOFF : YOFF + cols, :] = ext_ref[3 + c]
+    for k, src in enumerate((below_ref, mid_ref, above_ref)):
+        at = 1 + k * piece
+        for c in range(3):
+            vbuf[c, at : at + piece, YOFF : YOFF + cols, :] = src[c]
+        for c in range(6):
+            sbuf[c, at : at + piece, YOFF : YOFF + cols, :] = src[3 + c]
+        for c in range(4):
+            ext_ref[9 + c, at - 1 : at - 1 + piece, :, :] = src[9 + c]
     z_backward, z_forward = lane_shifts((1, cols, depth))
     ys = pl.ds(YOFF, cols)
     ym = pl.ds(YOFF - 1, cols)
@@ -197,7 +202,7 @@
                     vbuf[c, pl.ds(b, 1), ys, :] = keep(active, old + push * force, old)
                 return carry
 
-            lax.fori_loop(lo, hi, vel_row, 0)
+            lax.fori_loop(lo, hi, vel_row, 0, unroll=True)
 
             def strs_row(b, carry, sub=sub):
                 r = b - 1
@@ -234,7 +239,7 @@
                     sbuf[c, pl.ds(b, 1), ys, :] = keep(active, old + add, old)
                 return carry
 
-            lax.fori_loop(lo, hi, strs_row, 0)
+            lax.fori_loop(lo, hi, strs_row, 0, unroll=True)
 
     xs = slice(halo + 1, halo + 1 + nx)
     yc = slice(YOFF + halo, YOFF + halo + ny)
@@ -244,8 +249,9 @@
         strs_out[c] = sbuf[c, xs, yc, :]
 
 
-def substeps(ext, nx, ny):
-    fields, rows, cols, depth = ext.shape
+def substeps(below, mid, above, nx, ny):
+    fields, piece, cols, depth = mid.shape
+    rows = 3 * piece
     return pl.pallas_call(
         substeps_kernel,
         out_shape=(
@@ -255,9 +261,10 @@
         scratch_shapes=[
             pltpu.VMEM((3, rows + 2, cols + 2 * YOFF, depth), jnp.float32),
             pltpu.VMEM((6, rows + 2, cols + 2 * YOFF, depth), jnp.float32),
+            pltpu.VMEM((fields, rows, cols, depth), jnp.float32),
         ],
         interpret=INTERPRET,
-    )(ext)
+    )(below, mid, above)
 
 
 def per_device(velocity, stress, buoyancy, lame_lambda, lame_mu, rate_exponent):
@@ -277,8 +284,10 @@
         axis=0,
     )
     block = with_blocks(block, "gy", 2)
-    block = with_blocks(block, "gx", 1)
-    return substeps(block, nx, ny)
+    count = lax.axis_size("gx")
+    below = lax.ppermute(block, "gx", [(i, i + 1) for i in range(count - 1)])
+    above = lax.ppermute(block, "gx", [(i + 1, i) for i in range(count - 1)])
+    return substeps(below, block, above, nx, ny)
 
 
 def solution(mesh):

time: 80.7 us -> 58.3 us (0.72)
  Pallas kernels: 28.4 us -> 8.15 us
  other arithmetic: 4.51 us -> 2.38 us
    pallas_call x1, Pallas kernels: 28.4 us -> 8.15 us  [substeps(): pl.pallas_call(substeps_kernel, out_shape=(jax.ShapeDtypeStruct((3, nx, n...]
    ppermute x0 -> x2, starting transfers between devices: none -> 18.1 us  [the longest x1 16.2 us: per_device(): above = lax.ppermute(block, 'gx', [(i + 1, i) for i in range(count - 1)])]
    ppermute x2 -> x1, starting transfers between devices: 17.4 us -> 1.28 us  [with_blocks(): lax.ppermute(cells, axis, [(i + 1, i) for i in range(count - 1)])]
    ppermute x0 -> x2, waiting for transfers between devices: none -> 14.2 us  [the longest x1 9.37 us: per_device(): below = lax.ppermute(block, 'gx', [(i, i + 1) for i in range(count - 1)])]
    ppermute x2 -> x1, waiting for transfers between devices: 10.8 us -> 1.48 us  [with_blocks(): lax.ppermute(cells, axis, [(i, i + 1) for i in range(count - 1)])]
    ppermute x2 -> x1, waiting for transfers between devices: 8.36 us -> 3.55 us  [with_blocks(): lax.ppermute(cells, axis, [(i + 1, i) for i in range(count - 1)])]
    concatenate x2 -> x1, other arithmetic: 2.22 us -> 0.09 us  [with_blocks(): return jnp.concatenate([from_below, cells, from_above], axis=dim)]
    ppermute x2 -> x1, starting transfers between devices: 6.93 us -> 5.01 us  [with_blocks(): lax.ppermute(cells, axis, [(i, i + 1) for i in range(count - 1)])]
where the time goes in v4:
time: 58.3 us; the launch traced here: 57.3 us
  starting transfers between devices  24.4 us (42%)
  waiting for transfers between devices  19.2 us (33%)
  Pallas kernels  8.15 us (14%)
  other arithmetic  2.38 us (4%)
  local copies, waits for them, and re-layouts  1.85 us (3%)
  between operations  1.35 us (2%)
    ppermute x1, starting transfers between devices, per_device(): above = lax.ppermute(block, 'gx', [(i + 1, i) for i in range(count - 1)])  16.2 us
    ppermute x1, waiting for transfers between devices, per_device(): below = lax.ppermute(block, 'gx', [(i, i + 1) for i in range(count - 1)])  9.37 us
    pallas_call x1, Pallas kernels, substeps(): pl.pallas_call(substeps_kernel, out_shape=(jax.ShapeDtypeStruct((3, nx, n...  8.15 us
    ppermute x1, starting transfers between devices, with_blocks(): lax.ppermute(cells, axis, [(i, i + 1) for i in range(count - 1)])  5.01 us
    ppermute x1, waiting for transfers between devices, per_device(): above = lax.ppermute(block, 'gx', [(i + 1, i) for i in range(count - 1)])  4.8 us
    ppermute x1, waiting for transfers between devices, with_blocks(): lax.ppermute(cells, axis, [(i + 1, i) for i in range(count - 1)])  3.55 us
    unnamed x3, other arithmetic  2.29 us
    ppermute x1, starting transfers between devices, per_device(): below = lax.ppermute(block, 'gx', [(i, i + 1) for i in range(count - 1)])  1.92 us
  transfers between devices with their start and end apart: 4, of which 4 were waited for; matrix products, arithmetic and copies ran while one was open for 0% of the time, Pallas kernels for 0%

profile of v4, /device:TPU:1, one launch (start us, length us, event | category | flops | bytes accessed | tf_op | source)
XLA Modules:
  0.0 57.3 jit_solution(8424376950368926111)
XLA Ops:
  1.3 0.9 %constant_dynamic-update-slice_fusion.1 = f32[13,8,8,128]{3,2,1,0:T(8,128)S(1)} fusion(f32[3,8,8,128]{3,2,1,0:T(8,128)} %param.6), kind=kLoop, calls=%fused_computation.6 | loop fusion | bytes 196608
  2.2 0.9 %constant_dynamic-update-slice_fusion = f32[13,8,8,128]{3,2,1,0:T(8,128)S(1)} fusion(f32[13,8,8,128]{3,2,1,0:T(8,128)S(1)} %constant_dynamic-update-slice_fusion.1, f32[6,8,8,128]{3,2,1,0:T(8,128)} %param.7), kind=kLoop, calls=%fused_computation.5 | loop fusion | bytes 393216
  3.1 0.8 %bitcast_dynamic-update-slice_fusion.2 = f32[13,8,8,128]{3,2,1,0:T(8,128)S(1)} fusion(f32[13,8,8,128]{3,2,1,0:T(8,128)S(1)} %constant_dynamic-update-slice_fusion, f32[8,8,128]{2,1,0:T(8,128)} %param.8, f32[]{:T(128)} %bitcast), kind=kLoop, calls=%fused_computation.3 | loop fusion | flops 8192 | bytes 65540
  3.9 0.8 %bitcast_dynamic-update-slice_fusion.1 = f32[13,8,8,128]{3,2,1,0:T(8,128)S(1)} fusion(f32[13,8,8,128]{3,2,1,0:T(8,128)S(1)} %bitcast_dynamic-update-slice_fusion.2, f32[8,8,128]{2,1,0:T(8,128)} %param.9, f32[]{:T(128)} %bitcast), kind=kLoop, calls=%fused_computation.2 | loop fusion | flops 8192 | bytes 65540
  4.7 0.8 %bitcast_dynamic-update-slice_fusion = f32[13,8,8,128]{3,2,1,0:T(8,128)S(1)} fusion(f32[13,8,8,128]{3,2,1,0:T(8,128)S(1)} %bitcast_dynamic-update-slice_fusion.1, f32[8,8,128]{2,1,0:T(8,128)} %param.10, f32[]{:T(128)} %bitcast), kind=kLoop, calls=%fused_computation.1 | loop fusion | flops 8192 | bytes 65540
  5.4 1.3 %collective-permute-start.1 = (f32[13,8,8,128]{3,2,1,0:T(8,128)S(1)}, f32[13,8,8,128]{3,2,1,0:T(8,128)S(1)}, u32[]{:S(2)}, u32[]{:S(2)}) collective-permute-start(f32[13,8,8,128]{3,2,1,0:T(8,128)S(1)} %broadcast_dynamic-update-slice_fusion), channel_id=1, source_target_pairs={{1,0},{2,1},{3,2},{4,3},{5,4},{6,5},{7,6},{8,7},{9,8},{10,9},{11,1... | collective-permute-start | bytes 1277960 | tf_op jit(solution)/shard_map/ppermute | solution.py:109
  6.7 5.0 %collective-permute-start = (f32[13,8,8,128]{3,2,1,0:T(8,128)S(1)}, f32[13,8,8,128]{3,2,1,0:T(8,128)S(1)}, u32[]{:S(2)}, u32[]{:S(2)}) collective-permute-start(f32[13,8,8,128]{3,2,1,0:T(8,128)S(1)} %broadcast_dynamic-update-slice_fusion), channel_id=1, source_target_pairs={{0,1},{1,2},{2,3},{3,4},{4,5},{5,6},{6,7},{7,8},{8,9},{9,10},{10,1... | collective-permute-start | bytes 1277960 | tf_op jit(solution)/shard_map/ppermute | solution.py:108
  11.7 3.6 %collective-permute-done.1 = f32[13,8,8,128]{3,2,1,0:T(8,128)S(1)} collective-permute-done((f32[13,8,8,128]{3,2,1,0:T(8,128)S(1)}, f32[13,8,8,128]{3,2,1,0:T(8,128)S(1)}, u32[]{:S(2)}, u32[]{:S(2)}) %collective-permute-start.1) | collective-permute-done | bytes 426016 | tf_op jit(solution)/shard_map/ppermute | solution.py:109
  15.3 1.5 %collective-permute-done = f32[13,8,8,128]{3,2,1,0:T(8,128)S(1)} collective-permute-done((f32[13,8,8,128]{3,2,1,0:T(8,128)S(1)}, f32[13,8,8,128]{3,2,1,0:T(8,128)S(1)}, u32[]{:S(2)}, u32[]{:S(2)}) %collective-permute-start) | collective-permute-done | bytes 426016 | tf_op jit(solution)/shard_map/ppermute | solution.py:108
  16.8 0.1 pad_maximum_fusion.mid_ref
  16.9 0.0 copy-start
  16.9 16.2 %collective-permute-start.3 = (f32[13,8,24,128]{3,2,1,0:T(8,128)S(1)}, f32[13,8,24,128]{3,2,1,0:T(8,128)S(1)}, u32[]{:S(2)}, u32[]{:S(2)}) collective-permute-start(f32[13,8,24,128]{3,2,1,0:T(8,128)S(1)} %pad_maximum_fusion.mid_ref), channel_id=1, source_target_pairs={{32,0},{64,32},{96,64},{128,96},{160,128},{192,160},{224,192},{256... | collective-permute-start | bytes 3833864 | tf_op jit(solution)/shard_map/ppermute | solution.py:289
  33.0 1.9 %collective-permute-start.2 = (f32[13,8,24,128]{3,2,1,0:T(8,128)S(1)}, f32[13,8,24,128]{3,2,1,0:T(8,128)}, u32[]{:S(2)}, u32[]{:S(2)}) collective-permute-start(f32[13,8,24,128]{3,2,1,0:T(8,128)S(1)} %pad_maximum_fusion.mid_ref), channel_id=1, source_target_pairs={{0,32},{32,64},{64,96},{96,128},{128,160},{160,192},{192,224},{224... | collective-permute-start | bytes 3833864 | tf_op jit(solution)/shard_map/ppermute | solution.py:288
  35.0 4.8 %collective-permute-done.3.above_ref = f32[13,8,24,128]{3,2,1,0:T(8,128)S(1)} collective-permute-done((f32[13,8,24,128]{3,2,1,0:T(8,128)S(1)}, f32[13,8,24,128]{3,2,1,0:T(8,128)S(1)}, u32[]{:S(2)}, u32[]{:S(2)}) %collective-permute-start.3) | collective-permute-done | bytes 1277984 | tf_op jit(solution)/shard_map/ppermute | solution.py:289
  39.8 0.0 copy-start.1
  39.8 9.4 %collective-permute-done.2.below_ref = f32[13,8,24,128]{3,2,1,0:T(8,128)} collective-permute-done((f32[13,8,24,128]{3,2,1,0:T(8,128)S(1)}, f32[13,8,24,128]{3,2,1,0:T(8,128)}, u32[]{:S(2)}, u32[]{:S(2)}) %collective-permute-start.2) | collective-permute-done | bytes 1277984 | tf_op jit(solution)/shard_map/ppermute | solution.py:288
  49.2 0.0 copy-done
  49.2 0.0 copy-done.1
  49.2 8.1 %shard_map.77 = (f32[3,8,8,128]{3,2,1,0:T(8,128)}, f32[6,8,8,128]{3,2,1,0:T(8,128)}) custom-call(f32[13,8,24,128]{3,2,1,0:T(8,128)} %collective-permute-done.2.below_ref, f32[13,8,24,128]{3,2,1,0:T(8,128)} %copy-done, f32[13,8,24,128]{3,2,1,0:T(8,128)} %copy-done.1), custom_call_target="tpu_custom_call" | custom-call | tf_op jit(solution)/shard_map/pallas_call | solution.py:255
  (1 shorter events, 0.0 us)
Async XLA Ops:
  5.4 9.9 %collective-permute-start.1 = (f32[13,8,8,128]{3,2,1,0:T(8,128)S(1)}, f32[13,8,8,128]{3,2,1,0:T(8,128)S(1)}, u32[]{:S(2)}, u32[]{:S(2)}) collective-permute-start(f32[13,8,8,128]{3,2,1,0:T(8,128)S(1)} %broadcast_dynamic-update-slice_fusion), channel_id=1, source_target_pairs={{1,0},{2,1},{3,2},{4,3},{5,4},{6,5},{7,6},{8,7},{9,8},{10,9},{11,1... | collective-permute-start | bytes 1277960 | tf_op jit(solution)/shard_map/ppermute | solution.py:109
  6.7 10.1 %collective-permute-start = (f32[13,8,8,128]{3,2,1,0:T(8,128)S(1)}, f32[13,8,8,128]{3,2,1,0:T(8,128)S(1)}, u32[]{:S(2)}, u32[]{:S(2)}) collective-permute-start(f32[13,8,8,128]{3,2,1,0:T(8,128)S(1)} %broadcast_dynamic-update-slice_fusion), channel_id=1, source_target_pairs={{0,1},{1,2},{2,3},{3,4},{4,5},{5,6},{6,7},{7,8},{8,9},{9,10},{10,1... | collective-permute-start | bytes 1277960 | tf_op jit(solution)/shard_map/ppermute | solution.py:108
  16.9 32.3 %copy-start = (f32[13,8,24,128]{3,2,1,0:T(8,128)}, f32[13,8,24,128]{3,2,1,0:T(8,128)S(1)}, u32[]{:S(2)}) copy-start(f32[13,8,24,128]{3,2,1,0:T(8,128)S(1)} %pad_maximum_fusion.mid_ref) | copy-start | bytes 3833860
  16.9 22.9 %collective-permute-start.3 = (f32[13,8,24,128]{3,2,1,0:T(8,128)S(1)}, f32[13,8,24,128]{3,2,1,0:T(8,128)S(1)}, u32[]{:S(2)}, u32[]{:S(2)}) collective-permute-start(f32[13,8,24,128]{3,2,1,0:T(8,128)S(1)} %pad_maximum_fusion.mid_ref), channel_id=1, source_target_pairs={{32,0},{64,32},{96,64},{128,96},{160,128},{192,160},{224,192},{256... | collective-permute-start | bytes 3833864 | tf_op jit(solution)/shard_map/ppermute | solution.py:289
  33.0 16.1 %collective-permute-start.2 = (f32[13,8,24,128]{3,2,1,0:T(8,128)S(1)}, f32[13,8,24,128]{3,2,1,0:T(8,128)}, u32[]{:S(2)}, u32[]{:S(2)}) collective-permute-start(f32[13,8,24,128]{3,2,1,0:T(8,128)S(1)} %pad_maximum_fusion.mid_ref), channel_id=1, source_target_pairs={{0,32},{32,64},{64,96},{96,128},{128,160},{160,192},{192,224},{224... | collective-permute-start | bytes 3833864 | tf_op jit(solution)/shard_map/ppermute | solution.py:288
  39.8 9.4 %copy-start.1 = (f32[13,8,24,128]{3,2,1,0:T(8,128)}, f32[13,8,24,128]{3,2,1,0:T(8,128)S(1)}, u32[]{:S(2)}) copy-start(f32[13,8,24,128]{3,2,1,0:T(8,128)S(1)} %collective-permute-done.3.above_ref) | copy-start | bytes 3833860

commit v5 on v4

--- a/solution.py
+++ b/solution.py
@@ -135,9 +135,11 @@
     return z_backward, z_forward
 
 
-def substeps_kernel(below_ref, mid_ref, above_ref, vel_out, strs_out, vbuf, sbuf, ext_ref):
-    piece = mid_ref.shape[1]
-    rows, cols, depth = 3 * piece, mid_ref.shape[2], mid_ref.shape[3]
+def substeps_kernel(*refs):
+    pieces = refs[:9]
+    vel_out, strs_out, vbuf, sbuf, ext_ref = refs[9:]
+    piece, side = pieces[0].shape[1], pieces[0].shape[2]
+    rows, cols, depth = 3 * piece, 3 * side, pieces[0].shape[3]
     ny = vel_out.shape[2]
     nx = vel_out.shape[1]
     halo = (rows - nx) // 2
@@ -151,14 +153,15 @@
             buf[c, :, YOFF + cols :, :] = zero_y2
             buf[c, 0:1, :, :] = zero_x
             buf[c, rows + 1 : rows + 2, :, :] = zero_x
-    for k, src in enumerate((below_ref, mid_ref, above_ref)):
-        at = 1 + k * piece
+    for k, src in enumerate(pieces):
+        at = 1 + (k // 3) * piece
+        yat = (k % 3) * side
         for c in range(3):
-            vbuf[c, at : at + piece, YOFF : YOFF + cols, :] = src[c]
+            vbuf[c, at : at + piece, YOFF + yat : YOFF + yat + side, :] = src[c]
         for c in range(6):
-            sbuf[c, at : at + piece, YOFF : YOFF + cols, :] = src[3 + c]
+            sbuf[c, at : at + piece, YOFF + yat : YOFF + yat + side, :] = src[3 + c]
         for c in range(4):
-            ext_ref[9 + c, at - 1 : at - 1 + piece, :, :] = src[9 + c]
+            ext_ref[9 + c, at - 1 : at - 1 + piece, yat : yat + side, :] = src[9 + c]
     z_backward, z_forward = lane_shifts((1, cols, depth))
     ys = pl.ds(YOFF, cols)
     ym = pl.ds(YOFF - 1, cols)
@@ -249,9 +252,9 @@
         strs_out[c] = sbuf[c, xs, yc, :]
 
 
-def substeps(below, mid, above, nx, ny):
-    fields, piece, cols, depth = mid.shape
-    rows = 3 * piece
+def substeps(pieces, nx, ny):
+    fields, piece, side, depth = pieces[0].shape
+    rows, cols = 3 * piece, 3 * side
     return pl.pallas_call(
         substeps_kernel,
         out_shape=(
@@ -264,7 +267,31 @@
             pltpu.VMEM((fields, rows, cols, depth), jnp.float32),
         ],
         interpret=INTERPRET,
-    )(below, mid, above)
+    )(*pieces)
+
+
+def neighbour_blocks(block):
+    count_x, count_y = lax.axis_size("gx"), lax.axis_size("gy")
+    pieces = []
+    for i in (-1, 0, 1):
+        for j in (-1, 0, 1):
+            if i == 0 and j == 0:
+                pieces.append(block)
+            elif i == 0:
+                pairs = [(b + j, b) for b in range(count_y) if 0 <= b + j < count_y]
+                pieces.append(lax.ppermute(block, "gy", pairs))
+            elif j == 0:
+                pairs = [(a + i, a) for a in range(count_x) if 0 <= a + i < count_x]
+                pieces.append(lax.ppermute(block, "gx", pairs))
+            else:
+                pairs = [
+                    ((a + i) * count_y + b + j, a * count_y + b)
+                    for a in range(count_x)
+                    for b in range(count_y)
+                    if 0 <= a + i < count_x and 0 <= b + j < count_y
+                ]
+                pieces.append(lax.ppermute(block, ("gx", "gy"), pairs))
+    return pieces
 
 
 def per_device(velocity, stress, buoyancy, lame_lambda, lame_mu, rate_exponent):
@@ -283,11 +310,7 @@
         ],
         axis=0,
     )
-    block = with_blocks(block, "gy", 2)
-    count = lax.axis_size("gx")
-    below = lax.ppermute(block, "gx", [(i, i + 1) for i in range(count - 1)])
-    above = lax.ppermute(block, "gx", [(i + 1, i) for i in range(count - 1)])
-    return substeps(below, block, above, nx, ny)
+    return substeps(neighbour_blocks(block), nx, ny)
 
 
 def solution(mesh):

time: 58.3 us -> 62.5 us (1.072)
  the two profiles are of different devices: /device:TPU:1 before, /device:TPU:35 now
where the time goes in v5:
time: 62.5 us; the launch traced here: 61.9 us
  starting transfers between devices  30.3 us (48%)
  waiting for transfers between devices  18.7 us (30%)
  Pallas kernels  8.14 us (13%)
  local copies, waits for them, and re-layouts  3.18 us (5%)
  between operations  1.53 us (2%)
    ppermute x2, starting transfers between devices, neighbour_blocks(): pieces.append(lax.ppermute(block, 'gy', pairs))  16.3 us
    ppermute x4, starting transfers between devices, neighbour_blocks(): pieces.append(lax.ppermute(block, ('gx', 'gy'), pairs))  9.92 us
    ppermute x2, waiting for transfers between devices, neighbour_blocks(): pieces.append(lax.ppermute(block, 'gy', pairs))  9.84 us
    ppermute x4, waiting for transfers between devices, neighbour_blocks(): pieces.append(lax.ppermute(block, ('gx', 'gy'), pairs))  8.86 us
    pallas_call x1, Pallas kernels, substeps(): pl.pallas_call(substeps_kernel, out_shape=(jax.ShapeDtypeStruct((3, nx, n...  8.14 us
    ppermute x2, starting transfers between devices, neighbour_blocks(): pieces.append(lax.ppermute(block, 'gx', pairs))  4.13 us
    unnamed x26, local copies, waits for them, and re-layouts  3.18 us
  transfers between devices with their start and end apart: 8, of which 4 were waited for; matrix products, arithmetic and copies ran while one was open for 0% of the time, Pallas kernels for 0%

profile of v5, /device:TPU:35, one launch (start us, length us, event | category | flops | bytes accessed | tf_op | source)
XLA Modules:
  0.0 61.9 jit_solution(11873337107282566264)
XLA Ops:
  0.6 0.0 copy-start.8
  1.3 0.9 %constant_dynamic-update-slice_fusion.1 = f32[13,8,8,128]{3,2,1,0:T(8,128)S(1)} fusion(f32[3,8,8,128]{3,2,1,0:T(8,128)} %param.6), kind=kLoop, calls=%fused_computation.5 | loop fusion | bytes 196608
  2.2 0.0 copy-done.8
  2.2 0.0 copy-start.9
  2.3 0.7 %copy-done.9 = f32[8,8,128]{2,1,0:T(8,128)S(1)} copy-done((f32[8,8,128]{2,1,0:T(8,128)S(1)}, f32[8,8,128]{2,1,0:T(8,128)}, u32[]{:S(2)}) %copy-start.9) | copy-done | bytes 32792
  3.0 0.0 copy-start.10
  3.0 0.8 %copy-done.10 = f32[8,8,128]{2,1,0:T(8,128)S(1)} copy-done((f32[8,8,128]{2,1,0:T(8,128)S(1)}, f32[8,8,128]{2,1,0:T(8,128)}, u32[]{:S(2)}) %copy-start.10) | copy-done | bytes 32792
  3.8 0.0 copy-start.11
  3.8 0.8 %copy-done.11 = f32[8,8,128]{2,1,0:T(8,128)S(1)} copy-done((f32[8,8,128]{2,1,0:T(8,128)S(1)}, f32[8,8,128]{2,1,0:T(8,128)}, u32[]{:S(2)}) %copy-start.11) | copy-done | bytes 32792
  4.5 0.0 copy-start
  4.5 2.3 %collective-permute-start.7 = (f32[13,8,8,128]{3,2,1,0:T(8,128)S(1)}, f32[13,8,8,128]{3,2,1,0:T(8,128)S(1)}, u32[]{:S(2)}, u32[]{:S(2)}) collective-permute-start(f32[13,8,8,128]{3,2,1,0:T(8,128)S(1)} %broadcast_dynamic-update-slice_fusion.refs_4_), channel_id=1, source_target_pairs={{33,0},{34,1},{35,2},{36,3},{37,4},{38,5},{39,6},{40,7},{41,8},{42... | collective-permute-start | bytes 1277960 | tf_op jit(solution)/shard_map/ppermute | solution.py:293
  6.8 2.2 %collective-permute-start.6 = (f32[13,8,8,128]{3,2,1,0:T(8,128)S(1)}, f32[13,8,8,128]{3,2,1,0:T(8,128)S(1)}, u32[]{:S(2)}, u32[]{:S(2)}) collective-permute-start(f32[13,8,8,128]{3,2,1,0:T(8,128)S(1)} %broadcast_dynamic-update-slice_fusion.refs_4_), channel_id=1, source_target_pairs={{32,0},{64,32},{96,64},{128,96},{160,128},{192,160},{224,192},{256... | collective-permute-start | bytes 1277960 | tf_op jit(solution)/shard_map/ppermute | solution.py:285
  9.1 3.8 %collective-permute-start.5 = (f32[13,8,8,128]{3,2,1,0:T(8,128)S(1)}, f32[13,8,8,128]{3,2,1,0:T(8,128)S(1)}, u32[]{:S(2)}, u32[]{:S(2)}) collective-permute-start(f32[13,8,8,128]{3,2,1,0:T(8,128)S(1)} %broadcast_dynamic-update-slice_fusion.refs_4_), channel_id=1, source_target_pairs={{32,1},{33,2},{34,3},{35,4},{36,5},{37,6},{38,7},{39,8},{40,9},{41... | collective-permute-start | bytes 1277960 | tf_op jit(solution)/shard_map/ppermute | solution.py:293
  12.8 14.4 %collective-permute-start.4 = (f32[13,8,8,128]{3,2,1,0:T(8,128)S(1)}, f32[13,8,8,128]{3,2,1,0:T(8,128)S(1)}, u32[]{:S(2)}, u32[]{:S(2)}) collective-permute-start(f32[13,8,8,128]{3,2,1,0:T(8,128)S(1)} %broadcast_dynamic-update-slice_fusion.refs_4_), channel_id=1, source_target_pairs={{1,0},{2,1},{3,2},{4,3},{5,4},{6,5},{7,6},{8,7},{9,8},{10,9},{11,1... | collective-permute-start | bytes 1277960 | tf_op jit(solution)/shard_map/ppermute | solution.py:282
  27.2 1.9 %collective-permute-start.3 = (f32[13,8,8,128]{3,2,1,0:T(8,128)S(1)}, f32[13,8,8,128]{3,2,1,0:T(8,128)S(1)}, u32[]{:S(2)}, u32[]{:S(2)}) collective-permute-start(f32[13,8,8,128]{3,2,1,0:T(8,128)S(1)} %broadcast_dynamic-update-slice_fusion.refs_4_), channel_id=1, source_target_pairs={{0,1},{1,2},{2,3},{3,4},{4,5},{5,6},{6,7},{7,8},{8,9},{9,10},{10,1... | collective-permute-start | bytes 1277960 | tf_op jit(solution)/shard_map/ppermute | solution.py:282
  29.2 0.0 collective-permute-done.7.refs_8_
  29.2 0.0 copy-start.1
  29.2 1.9 %collective-permute-start.2 = (f32[13,8,8,128]{3,2,1,0:T(8,128)S(1)}, f32[13,8,8,128]{3,2,1,0:T(8,128)S(1)}, u32[]{:S(2)}, u32[]{:S(2)}) collective-permute-start(f32[13,8,8,128]{3,2,1,0:T(8,128)S(1)} %broadcast_dynamic-update-slice_fusion.refs_4_), channel_id=1, source_target_pairs={{1,32},{2,33},{3,34},{4,35},{5,36},{6,37},{7,38},{8,39},{9,40},{10... | collective-permute-start | bytes 1277960 | tf_op jit(solution)/shard_map/ppermute | solution.py:293
  31.1 0.0 collective-permute-done.6.refs_7_
  31.1 0.0 copy-start.2
  31.1 1.9 %collective-permute-start.1 = (f32[13,8,8,128]{3,2,1,0:T(8,128)S(1)}, f32[13,8,8,128]{3,2,1,0:T(8,128)S(1)}, u32[]{:S(2)}, u32[]{:S(2)}) collective-permute-start(f32[13,8,8,128]{3,2,1,0:T(8,128)S(1)} %broadcast_dynamic-update-slice_fusion.refs_4_), channel_id=1, source_target_pairs={{0,32},{32,64},{64,96},{96,128},{128,160},{160,192},{192,224},{224... | collective-permute-start | bytes 1277960 | tf_op jit(solution)/shard_map/ppermute | solution.py:285
  33.1 0.0 collective-permute-done.5.refs_6_
  33.1 0.0 copy-start.3
  33.1 1.9 %collective-permute-start = (f32[13,8,8,128]{3,2,1,0:T(8,128)S(1)}, f32[13,8,8,128]{3,2,1,0:T(8,128)}, u32[]{:S(2)}, u32[]{:S(2)}) collective-permute-start(f32[13,8,8,128]{3,2,1,0:T(8,128)S(1)} %broadcast_dynamic-update-slice_fusion.refs_4_), channel_id=1, source_target_pairs={{0,33},{1,34},{2,35},{3,36},{4,37},{5,38},{6,39},{7,40},{8,41},{9,... | collective-permute-start | bytes 1277960 | tf_op jit(solution)/shard_map/ppermute | solution.py:293
  35.0 1.5 %collective-permute-done.4.refs_5_ = f32[13,8,8,128]{3,2,1,0:T(8,128)S(1)} collective-permute-done((f32[13,8,8,128]{3,2,1,0:T(8,128)S(1)}, f32[13,8,8,128]{3,2,1,0:T(8,128)S(1)}, u32[]{:S(2)}, u32[]{:S(2)}) %collective-permute-start.4) | collective-permute-done | bytes 426016 | tf_op jit(solution)/shard_map/ppermute | solution.py:282
  36.5 0.0 copy-start.4
  36.5 8.3 %collective-permute-done.3.refs_3_ = f32[13,8,8,128]{3,2,1,0:T(8,128)S(1)} collective-permute-done((f32[13,8,8,128]{3,2,1,0:T(8,128)S(1)}, f32[13,8,8,128]{3,2,1,0:T(8,128)S(1)}, u32[]{:S(2)}, u32[]{:S(2)}) %collective-permute-start.3) | collective-permute-done | bytes 426016 | tf_op jit(solution)/shard_map/ppermute | solution.py:282
  44.9 0.0 copy-start.5
  44.9 0.8 %collective-permute-done.2.refs_2_ = f32[13,8,8,128]{3,2,1,0:T(8,128)S(1)} collective-permute-done((f32[13,8,8,128]{3,2,1,0:T(8,128)S(1)}, f32[13,8,8,128]{3,2,1,0:T(8,128)S(1)}, u32[]{:S(2)}, u32[]{:S(2)}) %collective-permute-start.2) | collective-permute-done | bytes 426016 | tf_op jit(solution)/shard_map/ppermute | solution.py:293
  45.7 0.0 copy-start.6
  45.7 0.0 collective-permute-done.1.refs_1_
  45.7 0.0 copy-start.7
  45.7 8.0 %collective-permute-done.refs_0_ = f32[13,8,8,128]{3,2,1,0:T(8,128)} collective-permute-done((f32[13,8,8,128]{3,2,1,0:T(8,128)S(1)}, f32[13,8,8,128]{3,2,1,0:T(8,128)}, u32[]{:S(2)}, u32[]{:S(2)}) %collective-permute-start) | collective-permute-done | bytes 426016 | tf_op jit(solution)/shard_map/ppermute | solution.py:293
  53.7 0.0 copy-done
  53.7 0.0 copy-done.1
  53.7 0.0 copy-done.2
  53.7 0.0 copy-done.3
  53.7 0.0 copy-done.4
  53.7 0.0 copy-done.5
  53.8 0.0 copy-done.6
  53.8 0.0 copy-done.7
  53.8 8.1 %shard_map.77 = (f32[3,8,8,128]{3,2,1,0:T(8,128)}, f32[6,8,8,128]{3,2,1,0:T(8,128)}) custom-call(f32[13,8,8,128]{3,2,1,0:T(8,128)} %collective-permute-done.refs_0_, f32[13,8,8,128]{3,2,1,0:T(8,128)} %copy-done.7, f32[13,8,8,128]{3,2,1,0:T(8,128)} %copy-done.6, f32[13,8,8,128]{3,2,1,0:T(8,128)} %copy-done.5, f32[13,8,8,128]{3,2,1,0:T(8,128)} %copy-done, ...), custom_call_target="tpu_custom_call" | custom-call | tf_op jit(solution)/shard_map/pallas_call | solution.py:258
  (5 shorter events, 0.0 us)
Async XLA Ops:
  0.6 1.6 %copy-start.8 = (f32[6,8,8,128]{3,2,1,0:T(8,128)S(1)}, f32[6,8,8,128]{3,2,1,0:T(8,128)}, u32[]{:S(2)}) copy-start(f32[6,8,8,128]{3,2,1,0:T(8,128)} %param.7) | copy-start | bytes 589828
  2.2 0.8 %copy-start.9 = (f32[8,8,128]{2,1,0:T(8,128)S(1)}, f32[8,8,128]{2,1,0:T(8,128)}, u32[]{:S(2)}) copy-start(f32[8,8,128]{2,1,0:T(8,128)} %param.8) | copy-start | bytes 98308
  3.0 0.8 %copy-start.10 = (f32[8,8,128]{2,1,0:T(8,128)S(1)}, f32[8,8,128]{2,1,0:T(8,128)}, u32[]{:S(2)}) copy-start(f32[8,8,128]{2,1,0:T(8,128)} %param.9) | copy-start | bytes 98308
  3.8 0.8 %copy-start.11 = (f32[8,8,128]{2,1,0:T(8,128)S(1)}, f32[8,8,128]{2,1,0:T(8,128)}, u32[]{:S(2)}) copy-start(f32[8,8,128]{2,1,0:T(8,128)} %param.10) | copy-start | bytes 98308
  4.5 49.2 %copy-start = (f32[13,8,8,128]{3,2,1,0:T(8,128)}, f32[13,8,8,128]{3,2,1,0:T(8,128)S(1)}, u32[]{:S(2)}) copy-start(f32[13,8,8,128]{3,2,1,0:T(8,128)S(1)} %broadcast_dynamic-update-slice_fusion.refs_4_) | copy-start | bytes 1277956
  4.5 24.6 %collective-permute-start.7 = (f32[13,8,8,128]{3,2,1,0:T(8,128)S(1)}, f32[13,8,8,128]{3,2,1,0:T(8,128)S(1)}, u32[]{:S(2)}, u32[]{:S(2)}) collective-permute-start(f32[13,8,8,128]{3,2,1,0:T(8,128)S(1)} %broadcast_dynamic-update-slice_fusion.refs_4_), channel_id=1, source_target_pairs={{33,0},{34,1},{35,2},{36,3},{37,4},{38,5},{39,6},{40,7},{41,8},{42... | collective-permute-start | bytes 1277960 | tf_op jit(solution)/shard_map/ppermute | solution.py:293
  6.8 24.3 %collective-permute-start.6 = (f32[13,8,8,128]{3,2,1,0:T(8,128)S(1)}, f32[13,8,8,128]{3,2,1,0:T(8,128)S(1)}, u32[]{:S(2)}, u32[]{:S(2)}) collective-permute-start(f32[13,8,8,128]{3,2,1,0:T(8,128)S(1)} %broadcast_dynamic-update-slice_fusion.refs_4_), channel_id=1, source_target_pairs={{32,0},{64,32},{96,64},{128,96},{160,128},{192,160},{224,192},{256... | collective-permute-start | bytes 1277960 | tf_op jit(solution)/shard_map/ppermute | solution.py:285
  9.1 24.0 %collective-permute-start.5 = (f32[13,8,8,128]{3,2,1,0:T(8,128)S(1)}, f32[13,8,8,128]{3,2,1,0:T(8,128)S(1)}, u32[]{:S(2)}, u32[]{:S(2)}) collective-permute-start(f32[13,8,8,128]{3,2,1,0:T(8,128)S(1)} %broadcast_dynamic-update-slice_fusion.refs_4_), channel_id=1, source_target_pairs={{32,1},{33,2},{34,3},{35,4},{36,5},{37,6},{38,7},{39,8},{40,9},{41... | collective-permute-start | bytes 1277960 | tf_op jit(solution)/shard_map/ppermute | solution.py:293
  12.8 23.7 %collective-permute-start.4 = (f32[13,8,8,128]{3,2,1,0:T(8,128)S(1)}, f32[13,8,8,128]{3,2,1,0:T(8,128)S(1)}, u32[]{:S(2)}, u32[]{:S(2)}) collective-permute-start(f32[13,8,8,128]{3,2,1,0:T(8,128)S(1)} %broadcast_dynamic-update-slice_fusion.refs_4_), channel_id=1, source_target_pairs={{1,0},{2,1},{3,2},{4,3},{5,4},{6,5},{7,6},{8,7},{9,8},{10,9},{11,1... | collective-permute-start | bytes 1277960 | tf_op jit(solution)/shard_map/ppermute | solution.py:282
  27.2 17.6 %collective-permute-start.3 = (f32[13,8,8,128]{3,2,1,0:T(8,128)S(1)}, f32[13,8,8,128]{3,2,1,0:T(8,128)S(1)}, u32[]{:S(2)}, u32[]{:S(2)}) collective-permute-start(f32[13,8,8,128]{3,2,1,0:T(8,128)S(1)} %broadcast_dynamic-update-slice_fusion.refs_4_), channel_id=1, source_target_pairs={{0,1},{1,2},{2,3},{3,4},{4,5},{5,6},{6,7},{7,8},{8,9},{9,10},{10,1... | collective-permute-start | bytes 1277960 | tf_op jit(solution)/shard_map/ppermute | solution.py:282
  29.2 24.5 %copy-start.1 = (f32[13,8,8,128]{3,2,1,0:T(8,128)}, f32[13,8,8,128]{3,2,1,0:T(8,128)S(1)}, u32[]{:S(2)}) copy-start(f32[13,8,8,128]{3,2,1,0:T(8,128)S(1)} %collective-permute-done.7.refs_8_) | copy-start | bytes 1277956
  29.2 16.5 %collective-permute-start.2 = (f32[13,8,8,128]{3,2,1,0:T(8,128)S(1)}, f32[13,8,8,128]{3,2,1,0:T(8,128)S(1)}, u32[]{:S(2)}, u32[]{:S(2)}) collective-permute-start(f32[13,8,8,128]{3,2,1,0:T(8,128)S(1)} %broadcast_dynamic-update-slice_fusion.refs_4_), channel_id=1, source_target_pairs={{1,32},{2,33},{3,34},{4,35},{5,36},{6,37},{7,38},{8,39},{9,40},{10... | collective-permute-start | bytes 1277960 | tf_op jit(solution)/shard_map/ppermute | solution.py:293
  31.1 22.6 %copy-start.2 = (f32[13,8,8,128]{3,2,1,0:T(8,128)}, f32[13,8,8,128]{3,2,1,0:T(8,128)S(1)}, u32[]{:S(2)}) copy-start(f32[13,8,8,128]{3,2,1,0:T(8,128)S(1)} %collective-permute-done.6.refs_7_) | copy-start | bytes 1277956
  31.1 14.5 %collective-permute-start.1 = (f32[13,8,8,128]{3,2,1,0:T(8,128)S(1)}, f32[13,8,8,128]{3,2,1,0:T(8,128)S(1)}, u32[]{:S(2)}, u32[]{:S(2)}) collective-permute-start(f32[13,8,8,128]{3,2,1,0:T(8,128)S(1)} %broadcast_dynamic-update-slice_fusion.refs_4_), channel_id=1, source_target_pairs={{0,32},{32,64},{64,96},{96,128},{128,160},{160,192},{192,224},{224... | collective-permute-start | bytes 1277960 | tf_op jit(solution)/shard_map/ppermute | solution.py:285
  33.1 20.7 %copy-start.3 = (f32[13,8,8,128]{3,2,1,0:T(8,128)}, f32[13,8,8,128]{3,2,1,0:T(8,128)S(1)}, u32[]{:S(2)}) copy-start(f32[13,8,8,128]{3,2,1,0:T(8,128)S(1)} %collective-permute-done.5.refs_6_) | copy-start | bytes 1277956
  33.1 20.6 %collective-permute-start = (f32[13,8,8,128]{3,2,1,0:T(8,128)S(1)}, f32[13,8,8,128]{3,2,1,0:T(8,128)}, u32[]{:S(2)}, u32[]{:S(2)}) collective-permute-start(f32[13,8,8,128]{3,2,1,0:T(8,128)S(1)} %broadcast_dynamic-update-slice_fusion.refs_4_), channel_id=1, source_target_pairs={{0,33},{1,34},{2,35},{3,36},{4,37},{5,38},{6,39},{7,40},{8,41},{9,... | collective-permute-start | bytes 1277960 | tf_op jit(solution)/shard_map/ppermute | solution.py:293
  36.5 17.2 %copy-start.4 = (f32[13,8,8,128]{3,2,1,0:T(8,128)}, f32[13,8,8,128]{3,2,1,0:T(8,128)S(1)}, u32[]{:S(2)}) copy-start(f32[13,8,8,128]{3,2,1,0:T(8,128)S(1)} %collective-permute-done.4.refs_5_) | copy-start | bytes 1277956
  44.9 8.9 %copy-start.5 = (f32[13,8,8,128]{3,2,1,0:T(8,128)}, f32[13,8,8,128]{3,2,1,0:T(8,128)S(1)}, u32[]{:S(2)}) copy-start(f32[13,8,8,128]{3,2,1,0:T(8,128)S(1)} %collective-permute-done.3.refs_3_) | copy-start | bytes 1277956
  45.7 8.1 %copy-start.6 = (f32[13,8,8,128]{3,2,1,0:T(8,128)}, f32[13,8,8,128]{3,2,1,0:T(8,128)S(1)}, u32[]{:S(2)}) copy-start(f32[13,8,8,128]{3,2,1,0:T(8,128)S(1)} %collective-permute-done.2.refs_2_) | copy-start | bytes 1277956
  45.7 8.1 %copy-start.7 = (f32[13,8,8,128]{3,2,1,0:T(8,128)}, f32[13,8,8,128]{3,2,1,0:T(8,128)S(1)}, u32[]{:S(2)}) copy-start(f32[13,8,8,128]{3,2,1,0:T(8,128)S(1)} %collective-permute-done.1.refs_1_) | copy-start | bytes 1277956

commit v6 on v4

--- a/solution.py
+++ b/solution.py
@@ -157,7 +157,7 @@
             vbuf[c, at : at + piece, YOFF : YOFF + cols, :] = src[c]
         for c in range(6):
             sbuf[c, at : at + piece, YOFF : YOFF + cols, :] = src[3 + c]
-        for c in range(4):
+        for c in range(3):
             ext_ref[9 + c, at - 1 : at - 1 + piece, :, :] = src[9 + c]
     z_backward, z_forward = lane_shifts((1, cols, depth))
     ys = pl.ds(YOFF, cols)
@@ -167,8 +167,8 @@
     def mask_of(sub, r):
         if sub == 3:
             return None
-        lvl = ext_ref[12, pl.ds(r, 1), :, :]
-        return lvl >= 1.0 if sub == 1 else lvl == 2.0
+        field = 10 if sub == 1 else 11
+        return ext_ref[field, pl.ds(r, 1), :, :] < 0.0
 
     def keep(active, fresh, old):
         return fresh if active is None else jnp.where(active, fresh, old)
@@ -222,8 +222,8 @@
                 shear_xz = z_forward(vx_c) + (vz_px - vz_c)
                 shear_yz = z_forward(vy_c) + (vz_py - vz_c)
                 trace_sum = strain_x + strain_y + strain_z
-                lam = ext_ref[10, pl.ds(r, 1), :, :]
-                shear = ext_ref[11, pl.ds(r, 1), :, :]
+                lam = jnp.abs(ext_ref[10, pl.ds(r, 1), :, :])
+                shear = jnp.abs(ext_ref[11, pl.ds(r, 1), :, :])
                 two_shear = 2.0 * shear
                 adds = (
                     lam * trace_sum + two_shear * strain_x,
@@ -267,22 +267,35 @@
     )(below, mid, above)
 
 
+def pack_kernel(e_ref, v_ref, s_ref, b_ref, l_ref, m_ref, out_ref):
+    e = e_ref[0, 0]
+    scale = jnp.where(e == 2, 0.25, jnp.where(e == 1, 0.5, 1.0)).astype(jnp.float32)
+    lam_sign = jnp.where(e >= 1, -1.0, 1.0).astype(jnp.float32)
+    shear_sign = jnp.where(e == 2, -1.0, 1.0).astype(jnp.float32)
+    for c in range(3):
+        out_ref[c] = v_ref[c]
+    for c in range(6):
+        out_ref[3 + c] = s_ref[c]
+    out_ref[9] = b_ref[...] * scale
+    out_ref[10] = (l_ref[...] * scale) * lam_sign
+    out_ref[11] = (m_ref[...] * scale) * shear_sign
+
+
+def pack(velocity, stress, buoyancy, lame_lambda, lame_mu, rate_exponent):
+    nx, ny, depth = buoyancy.shape
+    vmem = pl.BlockSpec(memory_space=pltpu.VMEM)
+    return pl.pallas_call(
+        pack_kernel,
+        out_shape=jax.ShapeDtypeStruct((12, nx, ny, depth), jnp.float32),
+        in_specs=[pl.BlockSpec(memory_space=pltpu.SMEM)] + [vmem] * 5,
+        out_specs=vmem,
+        interpret=INTERPRET,
+    )(rate_exponent, velocity, stress, buoyancy, lame_lambda, lame_mu)
+
+
 def per_device(velocity, stress, buoyancy, lame_lambda, lame_mu, rate_exponent):
     nx, ny = velocity.shape[1], velocity.shape[2]
-    exponent = rate_exponent[0, 0]
-    scale = level_scale(exponent)
-    level = jnp.full(buoyancy.shape, exponent.astype(jnp.float32))
-    block = jnp.concatenate(
-        [
-            velocity,
-            stress,
-            (buoyancy * scale)[None],
-            (lame_lambda * scale)[None],
-            (lame_mu * scale)[None],
-            level[None],
-        ],
-        axis=0,
-    )
+    block = pack(velocity, stress, buoyancy, lame_lambda, lame_mu, rate_exponent)
     block = with_blocks(block, "gy", 2)
     count = lax.axis_size("gx")
     below = lax.ppermute(block, "gx", [(i, i + 1) for i in range(count - 1)])

time: 58.3 us -> 56.4 us (0.967)
  Pallas kernels: 8.15 us -> 9.87 us
  other arithmetic: 2.38 us -> 1.08 us
  waiting for transfers between devices: 19.2 us -> 18.1 us
  local copies, waits for them, and re-layouts: 1.85 us -> 1.03 us
    unnamed x3 -> x0, other arithmetic: 2.29 us -> none
    pallas_call x0 -> x1, Pallas kernels: none -> 1.8 us  [pack(): pl.pallas_call(pack_kernel, out_shape=jax.ShapeDtypeStruct((12, nx, ny, d...]
    ppermute x1, waiting for transfers between devices: 4.8 us -> 3.4 us  [per_device(): above = lax.ppermute(block, 'gx', [(i + 1, i) for i in range(count - 1)])]
    concatenate x1, other arithmetic: 0.09 us -> 1.08 us  [with_blocks(): return jnp.concatenate([from_below, cells, from_above], axis=dim)]
    unnamed x6, local copies, waits for them, and re-layouts: 1.85 us -> 1.03 us
where the time goes in v6:
time: 56.4 us; the launch traced here: 55.8 us
  starting transfers between devices  24.4 us (43%)
  waiting for transfers between devices  18.1 us (32%)
  Pallas kernels  9.87 us (18%)
  between operations  1.33 us (2%)
  other arithmetic  1.08 us (2%)
  local copies, waits for them, and re-layouts  1.03 us (2%)
    ppermute x1, starting transfers between devices, per_device(): above = lax.ppermute(block, 'gx', [(i + 1, i) for i in range(count - 1)])  16.2 us
    ppermute x1, waiting for transfers between devices, per_device(): below = lax.ppermute(block, 'gx', [(i, i + 1) for i in range(count - 1)])  9.72 us
    pallas_call x1, Pallas kernels, substeps(): pl.pallas_call(substeps_kernel, out_shape=(jax.ShapeDtypeStruct((3, nx, n...  8.07 us
    ppermute x1, starting transfers between devices, with_blocks(): lax.ppermute(cells, axis, [(i, i + 1) for i in range(count - 1)])  5.01 us
    ppermute x1, waiting for transfers between devices, with_blocks(): lax.ppermute(cells, axis, [(i + 1, i) for i in range(count - 1)])  3.41 us
    ppermute x1, waiting for transfers between devices, per_device(): above = lax.ppermute(block, 'gx', [(i + 1, i) for i in range(count - 1)])  3.4 us
    ppermute x1, starting transfers between devices, per_device(): below = lax.ppermute(block, 'gx', [(i, i + 1) for i in range(count - 1)])  1.92 us
    pallas_call x1, Pallas kernels, pack(): pl.pallas_call(pack_kernel, out_shape=jax.ShapeDtypeStruct((12, nx, ny, d...  1.8 us
  transfers between devices with their start and end apart: 4, of which 4 were waited for; matrix products, arithmetic and copies ran while one was open for 0% of the time, Pallas kernels for 0%

profile of v6, /device:TPU:1, one launch (start us, length us, event | category | flops | bytes accessed | tf_op | source)
XLA Modules:
  0.0 55.8 jit_solution(6205472693403451105)
XLA Ops:
  1.3 1.8 %shard_map.77 = f32[12,8,8,128]{3,2,1,0:T(8,128)} custom-call(s32[1,1]{1,0:T(1,128)S(6)} %copy.8.e_ref, f32[3,8,8,128]{3,2,1,0:T(8,128)} %v_ref.1, f32[6,8,8,128]{3,2,1,0:T(8,128)} %s_ref.1, f32[8,8,128]{2,1,0:T(8,128)} %b_ref.1, f32[8,8,128]{2,1,0:T(8,128)} %l_ref.1, f32[8,8,128]{2,1,0:T(8,128)} %m_ref.1), custom_call_target="tpu_custom_call" | custom-call | tf_op jit(solution)/shard_map/pallas_call | solution.py:287
  3.1 1.3 %collective-permute-start.1 = (f32[12,8,8,128]{3,2,1,0:T(8,128)}, f32[12,8,8,128]{3,2,1,0:T(8,128)S(1)}, u32[]{:S(2)}, u32[]{:S(2)}) collective-permute-start(f32[12,8,8,128]{3,2,1,0:T(8,128)} %shard_map.77), channel_id=1, source_target_pairs={{1,0},{2,1},{3,2},{4,3},{5,4},{6,5},{7,6},{8,7},{9,8},{10,9},{11,1... | collective-permute-start | bytes 1179656 | tf_op jit(solution)/shard_map/ppermute | solution.py:109
  4.4 5.0 %collective-permute-start = (f32[12,8,8,128]{3,2,1,0:T(8,128)}, f32[12,8,8,128]{3,2,1,0:T(8,128)S(1)}, u32[]{:S(2)}, u32[]{:S(2)}) collective-permute-start(f32[12,8,8,128]{3,2,1,0:T(8,128)} %shard_map.77), channel_id=1, source_target_pairs={{0,1},{1,2},{2,3},{3,4},{4,5},{5,6},{6,7},{7,8},{8,9},{9,10},{10,1... | collective-permute-start | bytes 1179656 | tf_op jit(solution)/shard_map/ppermute | solution.py:108
  9.4 3.4 %collective-permute-done.1 = f32[12,8,8,128]{3,2,1,0:T(8,128)S(1)} collective-permute-done((f32[12,8,8,128]{3,2,1,0:T(8,128)}, f32[12,8,8,128]{3,2,1,0:T(8,128)S(1)}, u32[]{:S(2)}, u32[]{:S(2)}) %collective-permute-start.1) | collective-permute-done | bytes 393248 | tf_op jit(solution)/shard_map/ppermute | solution.py:109
  12.8 1.6 %collective-permute-done = f32[12,8,8,128]{3,2,1,0:T(8,128)S(1)} collective-permute-done((f32[12,8,8,128]{3,2,1,0:T(8,128)}, f32[12,8,8,128]{3,2,1,0:T(8,128)S(1)}, u32[]{:S(2)}, u32[]{:S(2)}) %collective-permute-start) | collective-permute-done | bytes 393248 | tf_op jit(solution)/shard_map/ppermute | solution.py:108
  14.4 1.1 %pad_maximum_fusion.mid_ref = f32[12,8,24,128]{3,2,1,0:T(8,128)S(1)} fusion(f32[12,8,8,128]{3,2,1,0:T(8,128)S(1)} %collective-permute-done.1, f32[12,8,8,128]{3,2,1,0:T(8,128)} %shard_map.77, f32[12,8,8,128]{3,2,1,0:T(8,128)S(1)} %collective-permute-done), kind=kLoop, calls=%fused_computation | loop fusion | flops 589824 | bytes 2359296 | tf_op jit(solution)/shard_map/concatenate | solution.py:110
  15.5 0.0 copy-start
  15.5 16.2 %collective-permute-start.3 = (f32[12,8,24,128]{3,2,1,0:T(8,128)S(1)}, f32[12,8,24,128]{3,2,1,0:T(8,128)S(1)}, u32[]{:S(2)}, u32[]{:S(2)}) collective-permute-start(f32[12,8,24,128]{3,2,1,0:T(8,128)S(1)} %pad_maximum_fusion.mid_ref), channel_id=1, source_target_pairs={{32,0},{64,32},{96,64},{128,96},{160,128},{192,160},{224,192},{256... | collective-permute-start | bytes 3538952 | tf_op jit(solution)/shard_map/ppermute | solution.py:302
  31.6 1.9 %collective-permute-start.2 = (f32[12,8,24,128]{3,2,1,0:T(8,128)S(1)}, f32[12,8,24,128]{3,2,1,0:T(8,128)S(1)}, u32[]{:S(2)}, u32[]{:S(2)}) collective-permute-start(f32[12,8,24,128]{3,2,1,0:T(8,128)S(1)} %pad_maximum_fusion.mid_ref), channel_id=1, source_target_pairs={{0,32},{32,64},{64,96},{96,128},{128,160},{160,192},{192,224},{224... | collective-permute-start | bytes 3538952 | tf_op jit(solution)/shard_map/ppermute | solution.py:301
  33.6 3.4 %collective-permute-done.3.above_ref = f32[12,8,24,128]{3,2,1,0:T(8,128)S(1)} collective-permute-done((f32[12,8,24,128]{3,2,1,0:T(8,128)S(1)}, f32[12,8,24,128]{3,2,1,0:T(8,128)S(1)}, u32[]{:S(2)}, u32[]{:S(2)}) %collective-permute-start.3) | collective-permute-done | bytes 1179680 | tf_op jit(solution)/shard_map/ppermute | solution.py:302
  37.0 0.0 copy-start.1
  37.0 9.7 %collective-permute-done.2.below_ref = f32[12,8,24,128]{3,2,1,0:T(8,128)S(1)} collective-permute-done((f32[12,8,24,128]{3,2,1,0:T(8,128)S(1)}, f32[12,8,24,128]{3,2,1,0:T(8,128)S(1)}, u32[]{:S(2)}, u32[]{:S(2)}) %collective-permute-start.2) | collective-permute-done | bytes 1179680 | tf_op jit(solution)/shard_map/ppermute | solution.py:301
  46.7 0.0 copy-done
  46.7 0.0 copy-done.1
  46.7 0.0 copy-start.2
  46.7 1.0 %copy-done.2 = f32[12,8,24,128]{3,2,1,0:T(8,128)} copy-done((f32[12,8,24,128]{3,2,1,0:T(8,128)}, f32[12,8,24,128]{3,2,1,0:T(8,128)S(1)}, u32[]{:S(2)}) %copy-start.2) | copy-done | bytes 1179672
  47.7 8.1 %shard_map.78 = (f32[3,8,8,128]{3,2,1,0:T(8,128)}, f32[6,8,8,128]{3,2,1,0:T(8,128)}) custom-call(f32[12,8,24,128]{3,2,1,0:T(8,128)} %copy-done.2, f32[12,8,24,128]{3,2,1,0:T(8,128)} %copy-done, f32[12,8,24,128]{3,2,1,0:T(8,128)} %copy-done.1), custom_call_target="tpu_custom_call" | custom-call | tf_op jit(solution)/shard_map/pallas_call | solution.py:255
Async XLA Ops:
  3.1 9.7 %collective-permute-start.1 = (f32[12,8,8,128]{3,2,1,0:T(8,128)}, f32[12,8,8,128]{3,2,1,0:T(8,128)S(1)}, u32[]{:S(2)}, u32[]{:S(2)}) collective-permute-start(f32[12,8,8,128]{3,2,1,0:T(8,128)} %shard_map.77), channel_id=1, source_target_pairs={{1,0},{2,1},{3,2},{4,3},{5,4},{6,5},{7,6},{8,7},{9,8},{10,9},{11,1... | collective-permute-start | bytes 1179656 | tf_op jit(solution)/shard_map/ppermute | solution.py:109
  4.4 10.0 %collective-permute-start = (f32[12,8,8,128]{3,2,1,0:T(8,128)}, f32[12,8,8,128]{3,2,1,0:T(8,128)S(1)}, u32[]{:S(2)}, u32[]{:S(2)}) collective-permute-start(f32[12,8,8,128]{3,2,1,0:T(8,128)} %shard_map.77), channel_id=1, source_target_pairs={{0,1},{1,2},{2,3},{3,4},{4,5},{5,6},{6,7},{7,8},{8,9},{9,10},{10,1... | collective-permute-start | bytes 1179656 | tf_op jit(solution)/shard_map/ppermute | solution.py:108
  15.5 31.2 %copy-start = (f32[12,8,24,128]{3,2,1,0:T(8,128)}, f32[12,8,24,128]{3,2,1,0:T(8,128)S(1)}, u32[]{:S(2)}) copy-start(f32[12,8,24,128]{3,2,1,0:T(8,128)S(1)} %pad_maximum_fusion.mid_ref) | copy-start | bytes 3538948
  15.5 21.5 %collective-permute-start.3 = (f32[12,8,24,128]{3,2,1,0:T(8,128)S(1)}, f32[12,8,24,128]{3,2,1,0:T(8,128)S(1)}, u32[]{:S(2)}, u32[]{:S(2)}) collective-permute-start(f32[12,8,24,128]{3,2,1,0:T(8,128)S(1)} %pad_maximum_fusion.mid_ref), channel_id=1, source_target_pairs={{32,0},{64,32},{96,64},{128,96},{160,128},{192,160},{224,192},{256... | collective-permute-start | bytes 3538952 | tf_op jit(solution)/shard_map/ppermute | solution.py:302
  31.6 15.1 %collective-permute-start.2 = (f32[12,8,24,128]{3,2,1,0:T(8,128)S(1)}, f32[12,8,24,128]{3,2,1,0:T(8,128)S(1)}, u32[]{:S(2)}, u32[]{:S(2)}) collective-permute-start(f32[12,8,24,128]{3,2,1,0:T(8,128)S(1)} %pad_maximum_fusion.mid_ref), channel_id=1, source_target_pairs={{0,32},{32,64},{64,96},{96,128},{128,160},{160,192},{192,224},{224... | collective-permute-start | bytes 3538952 | tf_op jit(solution)/shard_map/ppermute | solution.py:301
  37.0 9.7 %copy-start.1 = (f32[12,8,24,128]{3,2,1,0:T(8,128)}, f32[12,8,24,128]{3,2,1,0:T(8,128)S(1)}, u32[]{:S(2)}) copy-start(f32[12,8,24,128]{3,2,1,0:T(8,128)S(1)} %collective-permute-done.3.above_ref) | copy-start | bytes 3538948
  46.7 1.0 %copy-start.2 = (f32[12,8,24,128]{3,2,1,0:T(8,128)}, f32[12,8,24,128]{3,2,1,0:T(8,128)S(1)}, u32[]{:S(2)}) copy-start(f32[12,8,24,128]{3,2,1,0:T(8,128)S(1)} %collective-permute-done.2.below_ref) | copy-start | bytes 3538948

commit v7 on v6

--- a/solution.py
+++ b/solution.py
@@ -135,9 +135,11 @@
     return z_backward, z_forward
 
 
-def substeps_kernel(below_ref, mid_ref, above_ref, vel_out, strs_out, vbuf, sbuf, ext_ref):
-    piece = mid_ref.shape[1]
-    rows, cols, depth = 3 * piece, mid_ref.shape[2], mid_ref.shape[3]
+def substeps_kernel(*refs):
+    d_below, x_below, y_below, own, y_above, d_above, x_above = refs[:7]
+    vel_out, strs_out, vbuf, sbuf, ext_ref = refs[7:]
+    piece, side, depth = own.shape[1], own.shape[2], own.shape[3]
+    rows, cols = 3 * piece, 3 * side
     ny = vel_out.shape[2]
     nx = vel_out.shape[1]
     halo = (rows - nx) // 2
@@ -151,14 +153,27 @@
             buf[c, :, YOFF + cols :, :] = zero_y2
             buf[c, 0:1, :, :] = zero_x
             buf[c, rows + 1 : rows + 2, :, :] = zero_x
-    for k, src in enumerate((below_ref, mid_ref, above_ref)):
-        at = 1 + k * piece
+    placed = (
+        (d_below, 0, 0, 0),
+        (d_below, 0, 2, side),
+        (x_below, 0, 1, 0),
+        (y_below, 1, 0, 0),
+        (own, 1, 1, 0),
+        (y_above, 1, 2, 0),
+        (d_above, 2, 0, 0),
+        (d_above, 2, 2, side),
+        (x_above, 2, 1, 0),
+    )
+    for src, xb, yb, yfrom in placed:
+        at = 1 + xb * piece
+        yat = yb * side
+        yin = slice(yfrom, yfrom + side)
         for c in range(3):
-            vbuf[c, at : at + piece, YOFF : YOFF + cols, :] = src[c]
+            vbuf[c, at : at + piece, YOFF + yat : YOFF + yat + side, :] = src[c, :, yin, :]
         for c in range(6):
-            sbuf[c, at : at + piece, YOFF : YOFF + cols, :] = src[3 + c]
+            sbuf[c, at : at + piece, YOFF + yat : YOFF + yat + side, :] = src[3 + c, :, yin, :]
         for c in range(3):
-            ext_ref[9 + c, at - 1 : at - 1 + piece, :, :] = src[9 + c]
+            ext_ref[9 + c, at - 1 : at - 1 + piece, yat : yat + side, :] = src[9 + c, :, yin, :]
     z_backward, z_forward = lane_shifts((1, cols, depth))
     ys = pl.ds(YOFF, cols)
     ym = pl.ds(YOFF - 1, cols)
@@ -249,9 +264,9 @@
         strs_out[c] = sbuf[c, xs, yc, :]
 
 
-def substeps(below, mid, above, nx, ny):
-    fields, piece, cols, depth = mid.shape
-    rows = 3 * piece
+def substeps(pieces, nx, ny):
+    fields, piece, side, depth = pieces[3].shape
+    rows, cols = 3 * piece, 3 * side
     return pl.pallas_call(
         substeps_kernel,
         out_shape=(
@@ -264,7 +279,7 @@
             pltpu.VMEM((fields, rows, cols, depth), jnp.float32),
         ],
         interpret=INTERPRET,
-    )(below, mid, above)
+    )(*pieces)
 
 
 def pack_kernel(e_ref, v_ref, s_ref, b_ref, l_ref, m_ref, out_ref):
@@ -296,11 +311,19 @@
 def per_device(velocity, stress, buoyancy, lame_lambda, lame_mu, rate_exponent):
     nx, ny = velocity.shape[1], velocity.shape[2]
     block = pack(velocity, stress, buoyancy, lame_lambda, lame_mu, rate_exponent)
-    block = with_blocks(block, "gy", 2)
-    count = lax.axis_size("gx")
-    below = lax.ppermute(block, "gx", [(i, i + 1) for i in range(count - 1)])
-    above = lax.ppermute(block, "gx", [(i + 1, i) for i in range(count - 1)])
-    return substeps(below, block, above, nx, ny)
+    count_x, count_y = lax.axis_size("gx"), lax.axis_size("gy")
+    up_x = [(i, i + 1) for i in range(count_x - 1)]
+    down_x = [(i + 1, i) for i in range(count_x - 1)]
+    y_below = lax.ppermute(block, "gy", [(i, i + 1) for i in range(count_y - 1)])
+    y_above = lax.ppermute(block, "gy", [(i + 1, i) for i in range(count_y - 1)])
+    x_below = lax.ppermute(block, "gx", up_x)
+    x_above = lax.ppermute(block, "gx", down_x)
+    y_below, y_above, x_below, x_above = lax.optimization_barrier((y_below, y_above, x_below, x_above))
+    y_pair = jnp.concatenate([y_below, y_above], axis=2)
+    d_below = lax.ppermute(y_pair, "gx", up_x)
+    d_above = lax.ppermute(y_pair, "gx", down_x)
+    pieces = (d_below, x_below, y_below, block, y_above, d_above, x_above)
+    return substeps(pieces, nx, ny)
 
 
 def solution(mesh):

time: 56.4 us -> 59.1 us (1.048)
  starting transfers between devices: 24.4 us -> 28.8 us
  waiting for transfers between devices: 18.1 us -> 16.8 us
  other arithmetic: 1.08 us -> 0 us
  local copies, waits for them, and re-layouts: 1.03 us -> 1.66 us
    ppermute x4 -> x6, starting transfers between devices: 24.4 us -> 28.8 us  [the longest x1 16 us: per_device(): x_above = lax.ppermute(block, 'gx', down_x)]
    ppermute x4 -> x6, waiting for transfers between devices: 18.1 us -> 16.8 us  [the longest x1 7.73 us: per_device(): d_above = lax.ppermute(y_pair, 'gx', down_x)]
    concatenate x1 -> x0, other arithmetic: 1.08 us -> none  [with_blocks(): return jnp.concatenate([from_below, cells, from_above], axis=dim)]
    unnamed x6 -> x13, local copies, waits for them, and re-layouts: 1.03 us -> 1.63 us
  transfers between devices with their start and end apart: 4 -> 6, of which waited for: 4 -> 4; matrix products, arithmetic and copies ran while one was open for 0% -> 0% of each run, Pallas kernels for 0% -> 0%
where the time goes in v7:
time: 59.1 us; the launch traced here: 58.5 us
  starting transfers between devices  28.8 us (49%)
  waiting for transfers between devices  16.8 us (28%)
  Pallas kernels  9.84 us (17%)
  local copies, waits for them, and re-layouts  1.66 us (3%)
  between operations  1.39 us (2%)
    ppermute x1, starting transfers between devices, per_device(): x_above = lax.ppermute(block, 'gx', down_x)  16 us
    pallas_call x1, Pallas kernels, substeps(): pl.pallas_call(substeps_kernel, out_shape=(jax.ShapeDtypeStruct((3, nx, n...  8.05 us
    ppermute x1, waiting for transfers between devices, per_device(): d_above = lax.ppermute(y_pair, 'gx', down_x)  7.73 us
    ppermute x1, waiting for transfers between devices, per_device(): lax.ppermute(block, 'gy', [(i + 1, i) for i in range(count_y - 1)])  6.9 us
    ppermute x1, starting transfers between devices, per_device(): lax.ppermute(block, 'gy', [(i, i + 1) for i in range(count_y - 1)])  4.01 us
    ppermute x1, starting transfers between devices, per_device(): d_above = lax.ppermute(y_pair, 'gx', down_x)  3.56 us
    ppermute x1, starting transfers between devices, per_device(): d_below = lax.ppermute(y_pair, 'gx', up_x)  2 us
    ppermute x1, starting transfers between devices, per_device(): x_below = lax.ppermute(block, 'gx', up_x)  1.92 us
  transfers between devices with their start and end apart: 6, of which 4 were waited for; matrix products, arithmetic and copies ran while one was open for 0% of the time, Pallas kernels for 0%

profile of v7, /device:TPU:1, one launch (start us, length us, event | category | flops | bytes accessed | tf_op | source)
XLA Modules:
  0.0 58.5 jit_solution(2257564391769294865)
XLA Ops:
  1.3 1.8 %shard_map.77.refs_3_ = f32[12,8,8,128]{3,2,1,0:T(8,128)} custom-call(s32[1,1]{1,0:T(1,128)S(6)} %copy.9.e_ref, f32[3,8,8,128]{3,2,1,0:T(8,128)} %v_ref.1, f32[6,8,8,128]{3,2,1,0:T(8,128)} %s_ref.1, f32[8,8,128]{2,1,0:T(8,128)} %b_ref.1, f32[8,8,128]{2,1,0:T(8,128)} %l_ref.1, f32[8,8,128]{2,1,0:T(8,128)} %m_ref.1), custom_call_target="tpu_custom_call" | custom-call | tf_op jit(solution)/shard_map/pallas_call | solution.py:302
  3.1 16.0 %collective-permute-start.3 = (f32[12,8,8,128]{3,2,1,0:T(8,128)}, f32[12,8,8,128]{3,2,1,0:T(8,128)S(1)}, u32[]{:S(2)}, u32[]{:S(2)}) collective-permute-start(f32[12,8,8,128]{3,2,1,0:T(8,128)} %shard_map.77.refs_3_), channel_id=1, source_target_pairs={{32,0},{64,32},{96,64},{128,96},{160,128},{192,160},{224,192},{256... | collective-permute-start | bytes 1179656 | tf_op jit(solution)/shard_map/ppermute | solution.py:320
  19.1 1.9 %collective-permute-start.2 = (f32[12,8,8,128]{3,2,1,0:T(8,128)}, f32[12,8,8,128]{3,2,1,0:T(8,128)S(1)}, u32[]{:S(2)}, u32[]{:S(2)}) collective-permute-start(f32[12,8,8,128]{3,2,1,0:T(8,128)} %shard_map.77.refs_3_), channel_id=1, source_target_pairs={{0,32},{32,64},{64,96},{96,128},{128,160},{160,192},{192,224},{224... | collective-permute-start | bytes 1179656 | tf_op jit(solution)/shard_map/ppermute | solution.py:319
  21.0 1.3 %collective-permute-start.1 = (f32[12,8,8,128]{3,2,1,0:T(8,128)}, f32[12,8,8,128]{3,2,1,0:T(8,128)S(1)}, u32[]{:S(2)}, u32[]{:S(2)}) collective-permute-start(f32[12,8,8,128]{3,2,1,0:T(8,128)} %shard_map.77.refs_3_), channel_id=1, source_target_pairs={{1,0},{2,1},{3,2},{4,3},{5,4},{6,5},{7,6},{8,7},{9,8},{10,9},{11,1... | collective-permute-start | bytes 1179656 | tf_op jit(solution)/shard_map/ppermute | solution.py:318
  22.3 4.0 %collective-permute-start = (f32[12,8,8,128]{3,2,1,0:T(8,128)}, f32[12,8,8,128]{3,2,1,0:T(8,128)S(1)}, u32[]{:S(2)}, u32[]{:S(2)}) collective-permute-start(f32[12,8,8,128]{3,2,1,0:T(8,128)} %shard_map.77.refs_3_), channel_id=1, source_target_pairs={{0,1},{1,2},{2,3},{3,4},{4,5},{5,6},{6,7},{7,8},{8,9},{9,10},{10,1... | collective-permute-start | bytes 1179656 | tf_op jit(solution)/shard_map/ppermute | solution.py:317
  26.3 0.0 collective-permute-done.3.refs_6_
  26.3 0.0 copy-start.4
  26.3 0.0 collective-permute-done.2.refs_1_
  26.4 0.0 copy-start.5
  26.4 6.9 %collective-permute-done.1.refs_4_ = f32[12,8,8,128]{3,2,1,0:T(8,128)S(1)} collective-permute-done((f32[12,8,8,128]{3,2,1,0:T(8,128)}, f32[12,8,8,128]{3,2,1,0:T(8,128)S(1)}, u32[]{:S(2)}, u32[]{:S(2)}) %collective-permute-start.1) | collective-permute-done | bytes 393248 | tf_op jit(solution)/shard_map/ppermute | solution.py:318
  33.3 0.0 copy-start
  33.3 1.0 %collective-permute-done.refs_2_ = f32[12,8,8,128]{3,2,1,0:T(8,128)S(1)} collective-permute-done((f32[12,8,8,128]{3,2,1,0:T(8,128)}, f32[12,8,8,128]{3,2,1,0:T(8,128)S(1)}, u32[]{:S(2)}, u32[]{:S(2)}) %collective-permute-start) | collective-permute-done | bytes 393248 | tf_op jit(solution)/shard_map/ppermute | solution.py:317
  34.3 0.0 copy-start.1
  34.3 0.0 copy-done
  34.3 0.7 %copy-done.1 = f32[12,8,8,128]{3,2,1,0:T(8,128)} copy-done((f32[12,8,8,128]{3,2,1,0:T(8,128)}, f32[12,8,8,128]{3,2,1,0:T(8,128)S(1)}, u32[]{:S(2)}) %copy-start.1) | copy-done | bytes 393240
  35.1 3.6 %collective-permute-start.5 = (f32[12,8,16,128]{3,2,1,0:T(8,128)S(1)}, f32[12,8,16,128]{3,2,1,0:T(8,128)S(1)}, u32[]{:S(2)}, u32[]{:S(2)}) collective-permute-start(f32[12,8,16,128]{3,2,1,0:T(8,128)S(1)} %constant_dynamic-update-slice_fusion), channel_id=1, source_target_pairs={{32,0},{64,32},{96,64},{128,96},{160,128},{192,160},{224,192},{256... | collective-permute-start | bytes 2359304 | tf_op jit(solution)/shard_map/ppermute | solution.py:324
  38.6 2.0 %collective-permute-start.4 = (f32[12,8,16,128]{3,2,1,0:T(8,128)S(1)}, f32[12,8,16,128]{3,2,1,0:T(8,128)S(1)}, u32[]{:S(2)}, u32[]{:S(2)}) collective-permute-start(f32[12,8,16,128]{3,2,1,0:T(8,128)S(1)} %constant_dynamic-update-slice_fusion), channel_id=1, source_target_pairs={{0,32},{32,64},{64,96},{96,128},{128,160},{160,192},{192,224},{224... | collective-permute-start | bytes 2359304 | tf_op jit(solution)/shard_map/ppermute | solution.py:323
  40.6 7.7 %collective-permute-done.5.refs_5_ = f32[12,8,16,128]{3,2,1,0:T(8,128)S(1)} collective-permute-done((f32[12,8,16,128]{3,2,1,0:T(8,128)S(1)}, f32[12,8,16,128]{3,2,1,0:T(8,128)S(1)}, u32[]{:S(2)}, u32[]{:S(2)}) %collective-permute-start.5) | collective-permute-done | bytes 786464 | tf_op jit(solution)/shard_map/ppermute | solution.py:324
  48.4 0.0 copy-start.2
  48.4 1.2 %collective-permute-done.4.refs_0_ = f32[12,8,16,128]{3,2,1,0:T(8,128)S(1)} collective-permute-done((f32[12,8,16,128]{3,2,1,0:T(8,128)S(1)}, f32[12,8,16,128]{3,2,1,0:T(8,128)S(1)}, u32[]{:S(2)}, u32[]{:S(2)}) %collective-permute-start.4) | collective-permute-done | bytes 786464 | tf_op jit(solution)/shard_map/ppermute | solution.py:323
  49.5 0.0 copy-done.4
  49.5 0.0 copy-done.5
  49.5 0.0 copy-done.2
  49.6 0.0 copy-start.3
  49.6 0.9 %copy-done.3 = f32[12,8,16,128]{3,2,1,0:T(8,128)} copy-done((f32[12,8,16,128]{3,2,1,0:T(8,128)}, f32[12,8,16,128]{3,2,1,0:T(8,128)S(1)}, u32[]{:S(2)}) %copy-start.3) | copy-done | bytes 786456
  50.4 8.1 %shard_map.78 = (f32[3,8,8,128]{3,2,1,0:T(8,128)}, f32[6,8,8,128]{3,2,1,0:T(8,128)}) custom-call(f32[12,8,16,128]{3,2,1,0:T(8,128)} %copy-done.3, f32[12,8,8,128]{3,2,1,0:T(8,128)} %copy-done.5, f32[12,8,8,128]{3,2,1,0:T(8,128)} %copy-done.1, f32[12,8,8,128]{3,2,1,0:T(8,128)} %shard_map.77.refs_3_, f32[12,8,8,128]{3,2,1,0:T(8,128)} %copy-done, ...), custom_call_target="tpu_custom_call" | custom-call | tf_op jit(solution)/shard_map/pallas_call | solution.py:270
  (2 shorter events, 0.1 us)
Async XLA Ops:
  3.1 23.3 %collective-permute-start.3 = (f32[12,8,8,128]{3,2,1,0:T(8,128)}, f32[12,8,8,128]{3,2,1,0:T(8,128)S(1)}, u32[]{:S(2)}, u32[]{:S(2)}) collective-permute-start(f32[12,8,8,128]{3,2,1,0:T(8,128)} %shard_map.77.refs_3_), channel_id=1, source_target_pairs={{32,0},{64,32},{96,64},{128,96},{160,128},{192,160},{224,192},{256... | collective-permute-start | bytes 1179656 | tf_op jit(solution)/shard_map/ppermute | solution.py:320
  19.1 7.3 %collective-permute-start.2 = (f32[12,8,8,128]{3,2,1,0:T(8,128)}, f32[12,8,8,128]{3,2,1,0:T(8,128)S(1)}, u32[]{:S(2)}, u32[]{:S(2)}) collective-permute-start(f32[12,8,8,128]{3,2,1,0:T(8,128)} %shard_map.77.refs_3_), channel_id=1, source_target_pairs={{0,32},{32,64},{64,96},{96,128},{128,160},{160,192},{192,224},{224... | collective-permute-start | bytes 1179656 | tf_op jit(solution)/shard_map/ppermute | solution.py:319
  21.0 12.3 %collective-permute-start.1 = (f32[12,8,8,128]{3,2,1,0:T(8,128)}, f32[12,8,8,128]{3,2,1,0:T(8,128)S(1)}, u32[]{:S(2)}, u32[]{:S(2)}) collective-permute-start(f32[12,8,8,128]{3,2,1,0:T(8,128)} %shard_map.77.refs_3_), channel_id=1, source_target_pairs={{1,0},{2,1},{3,2},{4,3},{5,4},{6,5},{7,6},{8,7},{9,8},{10,9},{11,1... | collective-permute-start | bytes 1179656 | tf_op jit(solution)/shard_map/ppermute | solution.py:318
  22.3 12.0 %collective-permute-start = (f32[12,8,8,128]{3,2,1,0:T(8,128)}, f32[12,8,8,128]{3,2,1,0:T(8,128)S(1)}, u32[]{:S(2)}, u32[]{:S(2)}) collective-permute-start(f32[12,8,8,128]{3,2,1,0:T(8,128)} %shard_map.77.refs_3_), channel_id=1, source_target_pairs={{0,1},{1,2},{2,3},{3,4},{4,5},{5,6},{6,7},{7,8},{8,9},{9,10},{10,1... | collective-permute-start | bytes 1179656 | tf_op jit(solution)/shard_map/ppermute | solution.py:317
  26.3 23.2 %copy-start.4 = (f32[12,8,8,128]{3,2,1,0:T(8,128)}, f32[12,8,8,128]{3,2,1,0:T(8,128)S(1)}, u32[]{:S(2)}) copy-start(f32[12,8,8,128]{3,2,1,0:T(8,128)S(1)} %collective-permute-done.3.refs_6_) | copy-start | bytes 1179652
  26.4 23.2 %copy-start.5 = (f32[12,8,8,128]{3,2,1,0:T(8,128)}, f32[12,8,8,128]{3,2,1,0:T(8,128)S(1)}, u32[]{:S(2)}) copy-start(f32[12,8,8,128]{3,2,1,0:T(8,128)S(1)} %collective-permute-done.2.refs_1_) | copy-start | bytes 1179652
  33.3 1.0 %copy-start = (f32[12,8,8,128]{3,2,1,0:T(8,128)}, f32[12,8,8,128]{3,2,1,0:T(8,128)S(1)}, u32[]{:S(2)}) copy-start(f32[12,8,8,128]{3,2,1,0:T(8,128)S(1)} %collective-permute-done.1.refs_4_) | copy-start | bytes 1179652
  34.3 0.7 %copy-start.1 = (f32[12,8,8,128]{3,2,1,0:T(8,128)}, f32[12,8,8,128]{3,2,1,0:T(8,128)S(1)}, u32[]{:S(2)}) copy-start(f32[12,8,8,128]{3,2,1,0:T(8,128)S(1)} %collective-permute-done.refs_2_) | copy-start | bytes 1179652
  35.1 13.3 %collective-permute-start.5 = (f32[12,8,16,128]{3,2,1,0:T(8,128)S(1)}, f32[12,8,16,128]{3,2,1,0:T(8,128)S(1)}, u32[]{:S(2)}, u32[]{:S(2)}) collective-permute-start(f32[12,8,16,128]{3,2,1,0:T(8,128)S(1)} %constant_dynamic-update-slice_fusion), channel_id=1, source_target_pairs={{32,0},{64,32},{96,64},{128,96},{160,128},{192,160},{224,192},{256... | collective-permute-start | bytes 2359304 | tf_op jit(solution)/shard_map/ppermute | solution.py:324
  38.6 10.9 %collective-permute-start.4 = (f32[12,8,16,128]{3,2,1,0:T(8,128)S(1)}, f32[12,8,16,128]{3,2,1,0:T(8,128)S(1)}, u32[]{:S(2)}, u32[]{:S(2)}) collective-permute-start(f32[12,8,16,128]{3,2,1,0:T(8,128)S(1)} %constant_dynamic-update-slice_fusion), channel_id=1, source_target_pairs={{0,32},{32,64},{64,96},{96,128},{128,160},{160,192},{192,224},{224... | collective-permute-start | bytes 2359304 | tf_op jit(solution)/shard_map/ppermute | solution.py:323
  48.4 1.2 %copy-start.2 = (f32[12,8,16,128]{3,2,1,0:T(8,128)}, f32[12,8,16,128]{3,2,1,0:T(8,128)S(1)}, u32[]{:S(2)}) copy-start(f32[12,8,16,128]{3,2,1,0:T(8,128)S(1)} %collective-permute-done.5.refs_5_) | copy-start | bytes 2359300
  49.6 0.9 %copy-start.3 = (f32[12,8,16,128]{3,2,1,0:T(8,128)}, f32[12,8,16,128]{3,2,1,0:T(8,128)S(1)}, u32[]{:S(2)}) copy-start(f32[12,8,16,128]{3,2,1,0:T(8,128)S(1)} %collective-permute-done.4.refs_0_) | copy-start | bytes 2359300

commit v8 on v6

--- a/solution.py
+++ b/solution.py
@@ -115,22 +115,17 @@
 
 
 def lane_shifts(shape):
-    lane = lax.broadcasted_iota(jnp.int32, shape, len(shape) - 1)
+    axis = len(shape) - 1
     width = shape[-1]
-    from_below = pltpu.roll(lane, 1, len(shape) - 1) == (lane + (width - 1)) % width
+    lane = lax.broadcasted_iota(jnp.int32, shape, axis)
     first = lane == 0
     last = lane == width - 1
-    axis = len(shape) - 1
 
     def z_backward(f):
-        one, back = pltpu.roll(f, 1, axis), pltpu.roll(f, width - 1, axis)
-        prev = jnp.where(first, 0.0, jnp.where(from_below, one, back))
-        return f - prev
+        return f - jnp.where(first, 0.0, pltpu.roll(f, 1, axis))
 
     def z_forward(f):
-        one, back = pltpu.roll(f, 1, axis), pltpu.roll(f, width - 1, axis)
-        nxt = jnp.where(last, 0.0, jnp.where(from_below, back, one))
-        return nxt - f
+        return jnp.where(last, 0.0, pltpu.roll(f, width - 1, axis)) - f
 
     return z_backward, z_forward
 

time: 56.4 us -> 55.6 us (0.986)
  Pallas kernels: 9.87 us -> 9.09 us
    pallas_call x1, Pallas kernels: 8.07 us -> 7.29 us  [substeps(): pl.pallas_call(substeps_kernel, out_shape=(jax.ShapeDtypeStruct((3, nx, n...]
where the time goes in v8:
time: 55.6 us; the launch traced here: 55 us
  starting transfers between devices  24.4 us (44%)
  waiting for transfers between devices  18.1 us (33%)
  Pallas kernels  9.09 us (16%)
  between operations  1.33 us (2%)
  other arithmetic  1.08 us (2%)
  local copies, waits for them, and re-layouts  1.03 us (2%)
    ppermute x1, starting transfers between devices, per_device(): above = lax.ppermute(block, 'gx', [(i + 1, i) for i in range(count - 1)])  16.2 us
    ppermute x1, waiting for transfers between devices, per_device(): below = lax.ppermute(block, 'gx', [(i, i + 1) for i in range(count - 1)])  9.72 us
    pallas_call x1, Pallas kernels, substeps(): pl.pallas_call(substeps_kernel, out_shape=(jax.ShapeDtypeStruct((3, nx, n...  7.29 us
    ppermute x1, starting transfers between devices, with_blocks(): lax.ppermute(cells, axis, [(i, i + 1) for i in range(count - 1)])  5.01 us
    ppermute x1, waiting for transfers between devices, with_blocks(): lax.ppermute(cells, axis, [(i + 1, i) for i in range(count - 1)])  3.41 us
    ppermute x1, waiting for transfers between devices, per_device(): above = lax.ppermute(block, 'gx', [(i + 1, i) for i in range(count - 1)])  3.4 us
    ppermute x1, starting transfers between devices, per_device(): below = lax.ppermute(block, 'gx', [(i, i + 1) for i in range(count - 1)])  1.92 us
    pallas_call x1, Pallas kernels, pack(): pl.pallas_call(pack_kernel, out_shape=jax.ShapeDtypeStruct((12, nx, ny, d...  1.8 us
  transfers between devices with their start and end apart: 4, of which 4 were waited for; matrix products, arithmetic and copies ran while one was open for 0% of the time, Pallas kernels for 0%

profile of v8, /device:TPU:1, one launch (start us, length us, event | category | flops | bytes accessed | tf_op | source)
XLA Modules:
  0.0 55.0 jit_solution(10761974477986988767)
XLA Ops:
  1.3 1.8 %shard_map.77 = f32[12,8,8,128]{3,2,1,0:T(8,128)} custom-call(s32[1,1]{1,0:T(1,128)S(6)} %copy.8.e_ref, f32[3,8,8,128]{3,2,1,0:T(8,128)} %v_ref.1, f32[6,8,8,128]{3,2,1,0:T(8,128)} %s_ref.1, f32[8,8,128]{2,1,0:T(8,128)} %b_ref.1, f32[8,8,128]{2,1,0:T(8,128)} %l_ref.1, f32[8,8,128]{2,1,0:T(8,128)} %m_ref.1), custom_call_target="tpu_custom_call" | custom-call | tf_op jit(solution)/shard_map/pallas_call | solution.py:282
  3.1 1.3 %collective-permute-start.1 = (f32[12,8,8,128]{3,2,1,0:T(8,128)}, f32[12,8,8,128]{3,2,1,0:T(8,128)S(1)}, u32[]{:S(2)}, u32[]{:S(2)}) collective-permute-start(f32[12,8,8,128]{3,2,1,0:T(8,128)} %shard_map.77), channel_id=1, source_target_pairs={{1,0},{2,1},{3,2},{4,3},{5,4},{6,5},{7,6},{8,7},{9,8},{10,9},{11,1... | collective-permute-start | bytes 1179656 | tf_op jit(solution)/shard_map/ppermute | solution.py:109
  4.4 5.0 %collective-permute-start = (f32[12,8,8,128]{3,2,1,0:T(8,128)}, f32[12,8,8,128]{3,2,1,0:T(8,128)S(1)}, u32[]{:S(2)}, u32[]{:S(2)}) collective-permute-start(f32[12,8,8,128]{3,2,1,0:T(8,128)} %shard_map.77), channel_id=1, source_target_pairs={{0,1},{1,2},{2,3},{3,4},{4,5},{5,6},{6,7},{7,8},{8,9},{9,10},{10,1... | collective-permute-start | bytes 1179656 | tf_op jit(solution)/shard_map/ppermute | solution.py:108
  9.4 3.4 %collective-permute-done.1 = f32[12,8,8,128]{3,2,1,0:T(8,128)S(1)} collective-permute-done((f32[12,8,8,128]{3,2,1,0:T(8,128)}, f32[12,8,8,128]{3,2,1,0:T(8,128)S(1)}, u32[]{:S(2)}, u32[]{:S(2)}) %collective-permute-start.1) | collective-permute-done | bytes 393248 | tf_op jit(solution)/shard_map/ppermute | solution.py:109
  12.8 1.6 %collective-permute-done = f32[12,8,8,128]{3,2,1,0:T(8,128)S(1)} collective-permute-done((f32[12,8,8,128]{3,2,1,0:T(8,128)}, f32[12,8,8,128]{3,2,1,0:T(8,128)S(1)}, u32[]{:S(2)}, u32[]{:S(2)}) %collective-permute-start) | collective-permute-done | bytes 393248 | tf_op jit(solution)/shard_map/ppermute | solution.py:108
  14.4 1.1 %pad_maximum_fusion.mid_ref = f32[12,8,24,128]{3,2,1,0:T(8,128)S(1)} fusion(f32[12,8,8,128]{3,2,1,0:T(8,128)S(1)} %collective-permute-done.1, f32[12,8,8,128]{3,2,1,0:T(8,128)} %shard_map.77, f32[12,8,8,128]{3,2,1,0:T(8,128)S(1)} %collective-permute-done), kind=kLoop, calls=%fused_computation | loop fusion | flops 589824 | bytes 2359296 | tf_op jit(solution)/shard_map/concatenate | solution.py:110
  15.5 0.0 copy-start
  15.5 16.2 %collective-permute-start.3 = (f32[12,8,24,128]{3,2,1,0:T(8,128)S(1)}, f32[12,8,24,128]{3,2,1,0:T(8,128)S(1)}, u32[]{:S(2)}, u32[]{:S(2)}) collective-permute-start(f32[12,8,24,128]{3,2,1,0:T(8,128)S(1)} %pad_maximum_fusion.mid_ref), channel_id=1, source_target_pairs={{32,0},{64,32},{96,64},{128,96},{160,128},{192,160},{224,192},{256... | collective-permute-start | bytes 3538952 | tf_op jit(solution)/shard_map/ppermute | solution.py:297
  31.6 1.9 %collective-permute-start.2 = (f32[12,8,24,128]{3,2,1,0:T(8,128)S(1)}, f32[12,8,24,128]{3,2,1,0:T(8,128)S(1)}, u32[]{:S(2)}, u32[]{:S(2)}) collective-permute-start(f32[12,8,24,128]{3,2,1,0:T(8,128)S(1)} %pad_maximum_fusion.mid_ref), channel_id=1, source_target_pairs={{0,32},{32,64},{64,96},{96,128},{128,160},{160,192},{192,224},{224... | collective-permute-start | bytes 3538952 | tf_op jit(solution)/shard_map/ppermute | solution.py:296
  33.6 3.4 %collective-permute-done.3.above_ref = f32[12,8,24,128]{3,2,1,0:T(8,128)S(1)} collective-permute-done((f32[12,8,24,128]{3,2,1,0:T(8,128)S(1)}, f32[12,8,24,128]{3,2,1,0:T(8,128)S(1)}, u32[]{:S(2)}, u32[]{:S(2)}) %collective-permute-start.3) | collective-permute-done | bytes 1179680 | tf_op jit(solution)/shard_map/ppermute | solution.py:297
  37.0 0.0 copy-start.1
  37.0 9.7 %collective-permute-done.2.below_ref = f32[12,8,24,128]{3,2,1,0:T(8,128)S(1)} collective-permute-done((f32[12,8,24,128]{3,2,1,0:T(8,128)S(1)}, f32[12,8,24,128]{3,2,1,0:T(8,128)S(1)}, u32[]{:S(2)}, u32[]{:S(2)}) %collective-permute-start.2) | collective-permute-done | bytes 1179680 | tf_op jit(solution)/shard_map/ppermute | solution.py:296
  46.7 0.0 copy-done
  46.7 0.0 copy-done.1
  46.7 0.0 copy-start.2
  46.7 1.0 %copy-done.2 = f32[12,8,24,128]{3,2,1,0:T(8,128)} copy-done((f32[12,8,24,128]{3,2,1,0:T(8,128)}, f32[12,8,24,128]{3,2,1,0:T(8,128)S(1)}, u32[]{:S(2)}) %copy-start.2) | copy-done | bytes 1179672
  47.7 7.3 %shard_map.78 = (f32[3,8,8,128]{3,2,1,0:T(8,128)}, f32[6,8,8,128]{3,2,1,0:T(8,128)}) custom-call(f32[12,8,24,128]{3,2,1,0:T(8,128)} %copy-done.2, f32[12,8,24,128]{3,2,1,0:T(8,128)} %copy-done, f32[12,8,24,128]{3,2,1,0:T(8,128)} %copy-done.1), custom_call_target="tpu_custom_call" | custom-call | tf_op jit(solution)/shard_map/pallas_call | solution.py:250
Async XLA Ops:
  3.1 9.7 %collective-permute-start.1 = (f32[12,8,8,128]{3,2,1,0:T(8,128)}, f32[12,8,8,128]{3,2,1,0:T(8,128)S(1)}, u32[]{:S(2)}, u32[]{:S(2)}) collective-permute-start(f32[12,8,8,128]{3,2,1,0:T(8,128)} %shard_map.77), channel_id=1, source_target_pairs={{1,0},{2,1},{3,2},{4,3},{5,4},{6,5},{7,6},{8,7},{9,8},{10,9},{11,1... | collective-permute-start | bytes 1179656 | tf_op jit(solution)/shard_map/ppermute | solution.py:109
  4.4 10.0 %collective-permute-start = (f32[12,8,8,128]{3,2,1,0:T(8,128)}, f32[12,8,8,128]{3,2,1,0:T(8,128)S(1)}, u32[]{:S(2)}, u32[]{:S(2)}) collective-permute-start(f32[12,8,8,128]{3,2,1,0:T(8,128)} %shard_map.77), channel_id=1, source_target_pairs={{0,1},{1,2},{2,3},{3,4},{4,5},{5,6},{6,7},{7,8},{8,9},{9,10},{10,1... | collective-permute-start | bytes 1179656 | tf_op jit(solution)/shard_map/ppermute | solution.py:108
  15.5 31.2 %copy-start = (f32[12,8,24,128]{3,2,1,0:T(8,128)}, f32[12,8,24,128]{3,2,1,0:T(8,128)S(1)}, u32[]{:S(2)}) copy-start(f32[12,8,24,128]{3,2,1,0:T(8,128)S(1)} %pad_maximum_fusion.mid_ref) | copy-start | bytes 3538948
  15.5 21.5 %collective-permute-start.3 = (f32[12,8,24,128]{3,2,1,0:T(8,128)S(1)}, f32[12,8,24,128]{3,2,1,0:T(8,128)S(1)}, u32[]{:S(2)}, u32[]{:S(2)}) collective-permute-start(f32[12,8,24,128]{3,2,1,0:T(8,128)S(1)} %pad_maximum_fusion.mid_ref), channel_id=1, source_target_pairs={{32,0},{64,32},{96,64},{128,96},{160,128},{192,160},{224,192},{256... | collective-permute-start | bytes 3538952 | tf_op jit(solution)/shard_map/ppermute | solution.py:297
  31.6 15.1 %collective-permute-start.2 = (f32[12,8,24,128]{3,2,1,0:T(8,128)S(1)}, f32[12,8,24,128]{3,2,1,0:T(8,128)S(1)}, u32[]{:S(2)}, u32[]{:S(2)}) collective-permute-start(f32[12,8,24,128]{3,2,1,0:T(8,128)S(1)} %pad_maximum_fusion.mid_ref), channel_id=1, source_target_pairs={{0,32},{32,64},{64,96},{96,128},{128,160},{160,192},{192,224},{224... | collective-permute-start | bytes 3538952 | tf_op jit(solution)/shard_map/ppermute | solution.py:296
  37.0 9.7 %copy-start.1 = (f32[12,8,24,128]{3,2,1,0:T(8,128)}, f32[12,8,24,128]{3,2,1,0:T(8,128)S(1)}, u32[]{:S(2)}) copy-start(f32[12,8,24,128]{3,2,1,0:T(8,128)S(1)} %collective-permute-done.3.above_ref) | copy-start | bytes 3538948
  46.7 1.0 %copy-start.2 = (f32[12,8,24,128]{3,2,1,0:T(8,128)}, f32[12,8,24,128]{3,2,1,0:T(8,128)S(1)}, u32[]{:S(2)}) copy-start(f32[12,8,24,128]{3,2,1,0:T(8,128)S(1)} %collective-permute-done.2.below_ref) | copy-start | bytes 3538948

commit v9 on v8

--- a/solution.py
+++ b/solution.py
@@ -130,30 +130,36 @@
     return z_backward, z_forward
 
 
-def substeps_kernel(below_ref, mid_ref, above_ref, vel_out, strs_out, vbuf, sbuf, ext_ref):
+def substeps_kernel(below_ref, mid_ref, above_ref, vel_out, strs_out, vbuf, sbuf, cbuf, sems):
     piece = mid_ref.shape[1]
     rows, cols, depth = 3 * piece, mid_ref.shape[2], mid_ref.shape[3]
     ny = vel_out.shape[2]
     nx = vel_out.shape[1]
     halo = (rows - nx) // 2
     pad_rows = vbuf.shape[2] - cols - YOFF
+    copies = []
+    for k, src in enumerate((below_ref, mid_ref, above_ref)):
+        at = 1 + k * piece
+        targets = (
+            (src.at[0:3], vbuf.at[:, at : at + piece, YOFF : YOFF + cols, :]),
+            (src.at[3:9], sbuf.at[:, at : at + piece, YOFF : YOFF + cols, :]),
+            (src.at[9:12], cbuf.at[:, at - 1 : at - 1 + piece, :, :]),
+        )
+        for src_view, dst_view in targets:
+            copy = pltpu.make_async_copy(src_view, dst_view, sems.at[len(copies)])
+            copy.start()
+            copies.append(copy)
     zero_y = jnp.zeros((vbuf.shape[1], YOFF, depth), jnp.float32)
     zero_y2 = jnp.zeros((vbuf.shape[1], pad_rows, depth), jnp.float32)
-    zero_x = jnp.zeros((1, vbuf.shape[2], depth), jnp.float32)
+    zero_x = jnp.zeros((1, cols, depth), jnp.float32)
     for buf, count in ((vbuf, 3), (sbuf, 6)):
         for c in range(count):
             buf[c, :, 0:YOFF, :] = zero_y
             buf[c, :, YOFF + cols :, :] = zero_y2
-            buf[c, 0:1, :, :] = zero_x
-            buf[c, rows + 1 : rows + 2, :, :] = zero_x
-    for k, src in enumerate((below_ref, mid_ref, above_ref)):
-        at = 1 + k * piece
-        for c in range(3):
-            vbuf[c, at : at + piece, YOFF : YOFF + cols, :] = src[c]
-        for c in range(6):
-            sbuf[c, at : at + piece, YOFF : YOFF + cols, :] = src[3 + c]
-        for c in range(3):
-            ext_ref[9 + c, at - 1 : at - 1 + piece, :, :] = src[9 + c]
+            buf[c, 0:1, YOFF : YOFF + cols, :] = zero_x
+            buf[c, rows + 1 : rows + 2, YOFF : YOFF + cols, :] = zero_x
+    for copy in copies:
+        copy.wait()
     z_backward, z_forward = lane_shifts((1, cols, depth))
     ys = pl.ds(YOFF, cols)
     ym = pl.ds(YOFF - 1, cols)
@@ -163,7 +169,7 @@
         if sub == 3:
             return None
         field = 10 if sub == 1 else 11
-        return ext_ref[field, pl.ds(r, 1), :, :] < 0.0
+        return cbuf[field - 9, pl.ds(r, 1), :, :] < 0.0
 
     def keep(active, fresh, old):
         return fresh if active is None else jnp.where(active, fresh, old)
@@ -190,7 +196,7 @@
                 force_x = sxx_px - sxx_c + (sxy_c - sxy_my) + z_backward(sxz_c)
                 force_y = sxy_c - sxy_mx + (syy_py - syy_c) + z_backward(syz_c)
                 force_z = sxz_c - sxz_mx + (syz_c - syz_my) + z_forward(szz_c)
-                push = ext_ref[9, pl.ds(r, 1), :, :]
+                push = cbuf[0, pl.ds(r, 1), :, :]
                 active = mask_of(sub, r)
                 for c, force in enumerate((force_x, force_y, force_z)):
                     old = vbuf[c, pl.ds(b, 1), ys, :]
@@ -217,8 +223,8 @@
                 shear_xz = z_forward(vx_c) + (vz_px - vz_c)
                 shear_yz = z_forward(vy_c) + (vz_py - vz_c)
                 trace_sum = strain_x + strain_y + strain_z
-                lam = jnp.abs(ext_ref[10, pl.ds(r, 1), :, :])
-                shear = jnp.abs(ext_ref[11, pl.ds(r, 1), :, :])
+                lam = jnp.abs(cbuf[1, pl.ds(r, 1), :, :])
+                shear = jnp.abs(cbuf[2, pl.ds(r, 1), :, :])
                 two_shear = 2.0 * shear
                 adds = (
                     lam * trace_sum + two_shear * strain_x,
@@ -256,8 +262,10 @@
         scratch_shapes=[
             pltpu.VMEM((3, rows + 2, cols + 2 * YOFF, depth), jnp.float32),
             pltpu.VMEM((6, rows + 2, cols + 2 * YOFF, depth), jnp.float32),
-            pltpu.VMEM((fields, rows, cols, depth), jnp.float32),
+            pltpu.VMEM((fields - 9, rows, cols, depth), jnp.float32),
+            pltpu.SemaphoreType.DMA((9,)),
         ],
+        in_specs=[pl.BlockSpec(memory_space=pl.ANY)] * 3,
         interpret=INTERPRET,
     )(below, mid, above)
 

time: 55.6 us -> 55.5 us (level)
  no operation moved by 1% of the time
where the time goes in v9:
time: 55.5 us; the launch traced here: 54.9 us
  starting transfers between devices  24.4 us (44%)
  waiting for transfers between devices  18.1 us (33%)
  Pallas kernels  8.92 us (16%)
  between operations  1.33 us (2%)
  other arithmetic  1.08 us (2%)
  local copies, waits for them, and re-layouts  1.03 us (2%)
    ppermute x1, starting transfers between devices, per_device(): above = lax.ppermute(block, 'gx', [(i + 1, i) for i in range(count - 1)])  16.2 us
    ppermute x1, waiting for transfers between devices, per_device(): below = lax.ppermute(block, 'gx', [(i, i + 1) for i in range(count - 1)])  9.72 us
    pallas_call x1, Pallas kernels, substeps(): pl.pallas_call(substeps_kernel, out_shape=(jax.ShapeDtypeStruct((3, nx, n...  7.12 us
    ppermute x1, starting transfers between devices, with_blocks(): lax.ppermute(cells, axis, [(i, i + 1) for i in range(count - 1)])  5.01 us
    ppermute x1, waiting for transfers between devices, with_blocks(): lax.ppermute(cells, axis, [(i + 1, i) for i in range(count - 1)])  3.41 us
    ppermute x1, waiting for transfers between devices, per_device(): above = lax.ppermute(block, 'gx', [(i + 1, i) for i in range(count - 1)])  3.4 us
    ppermute x1, starting transfers between devices, per_device(): below = lax.ppermute(block, 'gx', [(i, i + 1) for i in range(count - 1)])  1.92 us
    pallas_call x1, Pallas kernels, pack(): pl.pallas_call(pack_kernel, out_shape=jax.ShapeDtypeStruct((12, nx, ny, d...  1.8 us
  transfers between devices with their start and end apart: 4, of which 4 were waited for; matrix products, arithmetic and copies ran while one was open for 0% of the time, Pallas kernels for 0%

profile of v9, /device:TPU:1, one launch (start us, length us, event | category | flops | bytes accessed | tf_op | source)
XLA Modules:
  0.0 54.9 jit_solution(17661250708495666676)
XLA Ops:
  1.3 1.8 %shard_map.77 = f32[12,8,8,128]{3,2,1,0:T(8,128)} custom-call(s32[1,1]{1,0:T(1,128)S(6)} %copy.8.e_ref, f32[3,8,8,128]{3,2,1,0:T(8,128)} %v_ref.1, f32[6,8,8,128]{3,2,1,0:T(8,128)} %s_ref.1, f32[8,8,128]{2,1,0:T(8,128)} %b_ref.1, f32[8,8,128]{2,1,0:T(8,128)} %l_ref.1, f32[8,8,128]{2,1,0:T(8,128)} %m_ref.1), custom_call_target="tpu_custom_call" | custom-call | tf_op jit(solution)/shard_map/pallas_call | solution.py:290
  3.1 1.3 %collective-permute-start.1 = (f32[12,8,8,128]{3,2,1,0:T(8,128)}, f32[12,8,8,128]{3,2,1,0:T(8,128)S(1)}, u32[]{:S(2)}, u32[]{:S(2)}) collective-permute-start(f32[12,8,8,128]{3,2,1,0:T(8,128)} %shard_map.77), channel_id=1, source_target_pairs={{1,0},{2,1},{3,2},{4,3},{5,4},{6,5},{7,6},{8,7},{9,8},{10,9},{11,1... | collective-permute-start | bytes 1179656 | tf_op jit(solution)/shard_map/ppermute | solution.py:109
  4.4 5.0 %collective-permute-start = (f32[12,8,8,128]{3,2,1,0:T(8,128)}, f32[12,8,8,128]{3,2,1,0:T(8,128)S(1)}, u32[]{:S(2)}, u32[]{:S(2)}) collective-permute-start(f32[12,8,8,128]{3,2,1,0:T(8,128)} %shard_map.77), channel_id=1, source_target_pairs={{0,1},{1,2},{2,3},{3,4},{4,5},{5,6},{6,7},{7,8},{8,9},{9,10},{10,1... | collective-permute-start | bytes 1179656 | tf_op jit(solution)/shard_map/ppermute | solution.py:108
  9.4 3.4 %collective-permute-done.1 = f32[12,8,8,128]{3,2,1,0:T(8,128)S(1)} collective-permute-done((f32[12,8,8,128]{3,2,1,0:T(8,128)}, f32[12,8,8,128]{3,2,1,0:T(8,128)S(1)}, u32[]{:S(2)}, u32[]{:S(2)}) %collective-permute-start.1) | collective-permute-done | bytes 393248 | tf_op jit(solution)/shard_map/ppermute | solution.py:109
  12.8 1.6 %collective-permute-done = f32[12,8,8,128]{3,2,1,0:T(8,128)S(1)} collective-permute-done((f32[12,8,8,128]{3,2,1,0:T(8,128)}, f32[12,8,8,128]{3,2,1,0:T(8,128)S(1)}, u32[]{:S(2)}, u32[]{:S(2)}) %collective-permute-start) | collective-permute-done | bytes 393248 | tf_op jit(solution)/shard_map/ppermute | solution.py:108
  14.4 1.1 %pad_maximum_fusion.mid_ref = f32[12,8,24,128]{3,2,1,0:T(8,128)S(1)} fusion(f32[12,8,8,128]{3,2,1,0:T(8,128)S(1)} %collective-permute-done.1, f32[12,8,8,128]{3,2,1,0:T(8,128)} %shard_map.77, f32[12,8,8,128]{3,2,1,0:T(8,128)S(1)} %collective-permute-done), kind=kLoop, calls=%fused_computation | loop fusion | flops 589824 | bytes 2359296 | tf_op jit(solution)/shard_map/concatenate | solution.py:110
  15.5 0.0 copy-start
  15.5 16.2 %collective-permute-start.3 = (f32[12,8,24,128]{3,2,1,0:T(8,128)S(1)}, f32[12,8,24,128]{3,2,1,0:T(8,128)S(1)}, u32[]{:S(2)}, u32[]{:S(2)}) collective-permute-start(f32[12,8,24,128]{3,2,1,0:T(8,128)S(1)} %pad_maximum_fusion.mid_ref), channel_id=1, source_target_pairs={{32,0},{64,32},{96,64},{128,96},{160,128},{192,160},{224,192},{256... | collective-permute-start | bytes 3538952 | tf_op jit(solution)/shard_map/ppermute | solution.py:305
  31.6 1.9 %collective-permute-start.2 = (f32[12,8,24,128]{3,2,1,0:T(8,128)S(1)}, f32[12,8,24,128]{3,2,1,0:T(8,128)S(1)}, u32[]{:S(2)}, u32[]{:S(2)}) collective-permute-start(f32[12,8,24,128]{3,2,1,0:T(8,128)S(1)} %pad_maximum_fusion.mid_ref), channel_id=1, source_target_pairs={{0,32},{32,64},{64,96},{96,128},{128,160},{160,192},{192,224},{224... | collective-permute-start | bytes 3538952 | tf_op jit(solution)/shard_map/ppermute | solution.py:304
  33.6 3.4 %collective-permute-done.3.above_ref = f32[12,8,24,128]{3,2,1,0:T(8,128)S(1)} collective-permute-done((f32[12,8,24,128]{3,2,1,0:T(8,128)S(1)}, f32[12,8,24,128]{3,2,1,0:T(8,128)S(1)}, u32[]{:S(2)}, u32[]{:S(2)}) %collective-permute-start.3) | collective-permute-done | bytes 1179680 | tf_op jit(solution)/shard_map/ppermute | solution.py:305
  37.0 0.0 copy-start.1
  37.0 9.7 %collective-permute-done.2.below_ref = f32[12,8,24,128]{3,2,1,0:T(8,128)S(1)} collective-permute-done((f32[12,8,24,128]{3,2,1,0:T(8,128)S(1)}, f32[12,8,24,128]{3,2,1,0:T(8,128)S(1)}, u32[]{:S(2)}, u32[]{:S(2)}) %collective-permute-start.2) | collective-permute-done | bytes 1179680 | tf_op jit(solution)/shard_map/ppermute | solution.py:304
  46.7 0.0 copy-done
  46.7 0.0 copy-done.1
  46.7 0.0 copy-start.2
  46.7 1.0 %copy-done.2 = f32[12,8,24,128]{3,2,1,0:T(8,128)} copy-done((f32[12,8,24,128]{3,2,1,0:T(8,128)}, f32[12,8,24,128]{3,2,1,0:T(8,128)S(1)}, u32[]{:S(2)}) %copy-start.2) | copy-done | bytes 1179672
  47.7 7.1 %shard_map.78 = (f32[3,8,8,128]{3,2,1,0:T(8,128)}, f32[6,8,8,128]{3,2,1,0:T(8,128)}) custom-call(f32[12,8,24,128]{3,2,1,0:T(8,128)} %copy-done.2, f32[12,8,24,128]{3,2,1,0:T(8,128)} %copy-done, f32[12,8,24,128]{3,2,1,0:T(8,128)} %copy-done.1), custom_call_target="tpu_custom_call" | custom-call | tf_op jit(solution)/shard_map/pallas_call | solution.py:256
Async XLA Ops:
  3.1 9.7 %collective-permute-start.1 = (f32[12,8,8,128]{3,2,1,0:T(8,128)}, f32[12,8,8,128]{3,2,1,0:T(8,128)S(1)}, u32[]{:S(2)}, u32[]{:S(2)}) collective-permute-start(f32[12,8,8,128]{3,2,1,0:T(8,128)} %shard_map.77), channel_id=1, source_target_pairs={{1,0},{2,1},{3,2},{4,3},{5,4},{6,5},{7,6},{8,7},{9,8},{10,9},{11,1... | collective-permute-start | bytes 1179656 | tf_op jit(solution)/shard_map/ppermute | solution.py:109
  4.4 10.0 %collective-permute-start = (f32[12,8,8,128]{3,2,1,0:T(8,128)}, f32[12,8,8,128]{3,2,1,0:T(8,128)S(1)}, u32[]{:S(2)}, u32[]{:S(2)}) collective-permute-start(f32[12,8,8,128]{3,2,1,0:T(8,128)} %shard_map.77), channel_id=1, source_target_pairs={{0,1},{1,2},{2,3},{3,4},{4,5},{5,6},{6,7},{7,8},{8,9},{9,10},{10,1... | collective-permute-start | bytes 1179656 | tf_op jit(solution)/shard_map/ppermute | solution.py:108
  15.5 31.2 %copy-start = (f32[12,8,24,128]{3,2,1,0:T(8,128)}, f32[12,8,24,128]{3,2,1,0:T(8,128)S(1)}, u32[]{:S(2)}) copy-start(f32[12,8,24,128]{3,2,1,0:T(8,128)S(1)} %pad_maximum_fusion.mid_ref) | copy-start | bytes 3538948
  15.5 21.5 %collective-permute-start.3 = (f32[12,8,24,128]{3,2,1,0:T(8,128)S(1)}, f32[12,8,24,128]{3,2,1,0:T(8,128)S(1)}, u32[]{:S(2)}, u32[]{:S(2)}) collective-permute-start(f32[12,8,24,128]{3,2,1,0:T(8,128)S(1)} %pad_maximum_fusion.mid_ref), channel_id=1, source_target_pairs={{32,0},{64,32},{96,64},{128,96},{160,128},{192,160},{224,192},{256... | collective-permute-start | bytes 3538952 | tf_op jit(solution)/shard_map/ppermute | solution.py:305
  31.6 15.1 %collective-permute-start.2 = (f32[12,8,24,128]{3,2,1,0:T(8,128)S(1)}, f32[12,8,24,128]{3,2,1,0:T(8,128)S(1)}, u32[]{:S(2)}, u32[]{:S(2)}) collective-permute-start(f32[12,8,24,128]{3,2,1,0:T(8,128)S(1)} %pad_maximum_fusion.mid_ref), channel_id=1, source_target_pairs={{0,32},{32,64},{64,96},{96,128},{128,160},{160,192},{192,224},{224... | collective-permute-start | bytes 3538952 | tf_op jit(solution)/shard_map/ppermute | solution.py:304
  37.0 9.7 %copy-start.1 = (f32[12,8,24,128]{3,2,1,0:T(8,128)}, f32[12,8,24,128]{3,2,1,0:T(8,128)S(1)}, u32[]{:S(2)}) copy-start(f32[12,8,24,128]{3,2,1,0:T(8,128)S(1)} %collective-permute-done.3.above_ref) | copy-start | bytes 3538948
  46.7 1.0 %copy-start.2 = (f32[12,8,24,128]{3,2,1,0:T(8,128)}, f32[12,8,24,128]{3,2,1,0:T(8,128)S(1)}, u32[]{:S(2)}) copy-start(f32[12,8,24,128]{3,2,1,0:T(8,128)S(1)} %collective-permute-done.2.below_ref) | copy-start | bytes 3538948

commit v10 on v9

--- a/solution.py
+++ b/solution.py
@@ -240,7 +240,7 @@
                     sbuf[c, pl.ds(b, 1), ys, :] = keep(active, old + add, old)
                 return carry
 
-            lax.fori_loop(lo, hi, strs_row, 0, unroll=True)
+            lax.fori_loop(lo + 1, hi - 1, strs_row, 0, unroll=True)
 
     xs = slice(halo + 1, halo + 1 + nx)
     yc = slice(YOFF + halo, YOFF + halo + ny)

time: 55.5 us -> 55.2 us (level)
  no operation moved by 1% of the time
where the time goes in v10:
time: 55.2 us; the launch traced here: 54.5 us
  starting transfers between devices  24.4 us (44%)
  waiting for transfers between devices  18.1 us (33%)
  Pallas kernels  8.62 us (16%)
  between operations  1.33 us (2%)
  other arithmetic  1.08 us (2%)
  local copies, waits for them, and re-layouts  1.03 us (2%)
    ppermute x1, starting transfers between devices, per_device(): above = lax.ppermute(block, 'gx', [(i + 1, i) for i in range(count - 1)])  16.2 us
    ppermute x1, waiting for transfers between devices, per_device(): below = lax.ppermute(block, 'gx', [(i, i + 1) for i in range(count - 1)])  9.72 us
    pallas_call x1, Pallas kernels, substeps(): pl.pallas_call(substeps_kernel, out_shape=(jax.ShapeDtypeStruct((3, nx, n...  6.82 us
    ppermute x1, starting transfers between devices, with_blocks(): lax.ppermute(cells, axis, [(i, i + 1) for i in range(count - 1)])  5.01 us
    ppermute x1, waiting for transfers between devices, with_blocks(): lax.ppermute(cells, axis, [(i + 1, i) for i in range(count - 1)])  3.41 us
    ppermute x1, waiting for transfers between devices, per_device(): above = lax.ppermute(block, 'gx', [(i + 1, i) for i in range(count - 1)])  3.4 us
    ppermute x1, starting transfers between devices, per_device(): below = lax.ppermute(block, 'gx', [(i, i + 1) for i in range(count - 1)])  1.92 us
    pallas_call x1, Pallas kernels, pack(): pl.pallas_call(pack_kernel, out_shape=jax.ShapeDtypeStruct((12, nx, ny, d...  1.8 us
  transfers between devices with their start and end apart: 4, of which 4 were waited for; matrix products, arithmetic and copies ran while one was open for 0% of the time, Pallas kernels for 0%

profile of v10, /device:TPU:1, one launch (start us, length us, event | category | flops | bytes accessed | tf_op | source)
XLA Modules:
  0.0 54.5 jit_solution(2067635904568259260)
XLA Ops:
  1.3 1.8 %shard_map.77 = f32[12,8,8,128]{3,2,1,0:T(8,128)} custom-call(s32[1,1]{1,0:T(1,128)S(6)} %copy.8.e_ref, f32[3,8,8,128]{3,2,1,0:T(8,128)} %v_ref.1, f32[6,8,8,128]{3,2,1,0:T(8,128)} %s_ref.1, f32[8,8,128]{2,1,0:T(8,128)} %b_ref.1, f32[8,8,128]{2,1,0:T(8,128)} %l_ref.1, f32[8,8,128]{2,1,0:T(8,128)} %m_ref.1), custom_call_target="tpu_custom_call" | custom-call | tf_op jit(solution)/shard_map/pallas_call | solution.py:290
  3.1 1.3 %collective-permute-start.1 = (f32[12,8,8,128]{3,2,1,0:T(8,128)}, f32[12,8,8,128]{3,2,1,0:T(8,128)S(1)}, u32[]{:S(2)}, u32[]{:S(2)}) collective-permute-start(f32[12,8,8,128]{3,2,1,0:T(8,128)} %shard_map.77), channel_id=1, source_target_pairs={{1,0},{2,1},{3,2},{4,3},{5,4},{6,5},{7,6},{8,7},{9,8},{10,9},{11,1... | collective-permute-start | bytes 1179656 | tf_op jit(solution)/shard_map/ppermute | solution.py:109
  4.4 5.0 %collective-permute-start = (f32[12,8,8,128]{3,2,1,0:T(8,128)}, f32[12,8,8,128]{3,2,1,0:T(8,128)S(1)}, u32[]{:S(2)}, u32[]{:S(2)}) collective-permute-start(f32[12,8,8,128]{3,2,1,0:T(8,128)} %shard_map.77), channel_id=1, source_target_pairs={{0,1},{1,2},{2,3},{3,4},{4,5},{5,6},{6,7},{7,8},{8,9},{9,10},{10,1... | collective-permute-start | bytes 1179656 | tf_op jit(solution)/shard_map/ppermute | solution.py:108
  9.4 3.4 %collective-permute-done.1 = f32[12,8,8,128]{3,2,1,0:T(8,128)S(1)} collective-permute-done((f32[12,8,8,128]{3,2,1,0:T(8,128)}, f32[12,8,8,128]{3,2,1,0:T(8,128)S(1)}, u32[]{:S(2)}, u32[]{:S(2)}) %collective-permute-start.1) | collective-permute-done | bytes 393248 | tf_op jit(solution)/shard_map/ppermute | solution.py:109
  12.8 1.6 %collective-permute-done = f32[12,8,8,128]{3,2,1,0:T(8,128)S(1)} collective-permute-done((f32[12,8,8,128]{3,2,1,0:T(8,128)}, f32[12,8,8,128]{3,2,1,0:T(8,128)S(1)}, u32[]{:S(2)}, u32[]{:S(2)}) %collective-permute-start) | collective-permute-done | bytes 393248 | tf_op jit(solution)/shard_map/ppermute | solution.py:108
  14.4 1.1 %pad_maximum_fusion.mid_ref = f32[12,8,24,128]{3,2,1,0:T(8,128)S(1)} fusion(f32[12,8,8,128]{3,2,1,0:T(8,128)S(1)} %collective-permute-done.1, f32[12,8,8,128]{3,2,1,0:T(8,128)} %shard_map.77, f32[12,8,8,128]{3,2,1,0:T(8,128)S(1)} %collective-permute-done), kind=kLoop, calls=%fused_computation | loop fusion | flops 589824 | bytes 2359296 | tf_op jit(solution)/shard_map/concatenate | solution.py:110
  15.5 0.0 copy-start
  15.5 16.2 %collective-permute-start.3 = (f32[12,8,24,128]{3,2,1,0:T(8,128)S(1)}, f32[12,8,24,128]{3,2,1,0:T(8,128)S(1)}, u32[]{:S(2)}, u32[]{:S(2)}) collective-permute-start(f32[12,8,24,128]{3,2,1,0:T(8,128)S(1)} %pad_maximum_fusion.mid_ref), channel_id=1, source_target_pairs={{32,0},{64,32},{96,64},{128,96},{160,128},{192,160},{224,192},{256... | collective-permute-start | bytes 3538952 | tf_op jit(solution)/shard_map/ppermute | solution.py:305
  31.6 1.9 %collective-permute-start.2 = (f32[12,8,24,128]{3,2,1,0:T(8,128)S(1)}, f32[12,8,24,128]{3,2,1,0:T(8,128)S(1)}, u32[]{:S(2)}, u32[]{:S(2)}) collective-permute-start(f32[12,8,24,128]{3,2,1,0:T(8,128)S(1)} %pad_maximum_fusion.mid_ref), channel_id=1, source_target_pairs={{0,32},{32,64},{64,96},{96,128},{128,160},{160,192},{192,224},{224... | collective-permute-start | bytes 3538952 | tf_op jit(solution)/shard_map/ppermute | solution.py:304
  33.6 3.4 %collective-permute-done.3.above_ref = f32[12,8,24,128]{3,2,1,0:T(8,128)S(1)} collective-permute-done((f32[12,8,24,128]{3,2,1,0:T(8,128)S(1)}, f32[12,8,24,128]{3,2,1,0:T(8,128)S(1)}, u32[]{:S(2)}, u32[]{:S(2)}) %collective-permute-start.3) | collective-permute-done | bytes 1179680 | tf_op jit(solution)/shard_map/ppermute | solution.py:305
  37.0 0.0 copy-start.1
  37.0 9.7 %collective-permute-done.2.below_ref = f32[12,8,24,128]{3,2,1,0:T(8,128)S(1)} collective-permute-done((f32[12,8,24,128]{3,2,1,0:T(8,128)S(1)}, f32[12,8,24,128]{3,2,1,0:T(8,128)S(1)}, u32[]{:S(2)}, u32[]{:S(2)}) %collective-permute-start.2) | collective-permute-done | bytes 1179680 | tf_op jit(solution)/shard_map/ppermute | solution.py:304
  46.7 0.0 copy-done
  46.7 0.0 copy-done.1
  46.7 0.0 copy-start.2
  46.7 1.0 %copy-done.2 = f32[12,8,24,128]{3,2,1,0:T(8,128)} copy-done((f32[12,8,24,128]{3,2,1,0:T(8,128)}, f32[12,8,24,128]{3,2,1,0:T(8,128)S(1)}, u32[]{:S(2)}) %copy-start.2) | copy-done | bytes 1179672
  47.7 6.8 %shard_map.78 = (f32[3,8,8,128]{3,2,1,0:T(8,128)}, f32[6,8,8,128]{3,2,1,0:T(8,128)}) custom-call(f32[12,8,24,128]{3,2,1,0:T(8,128)} %copy-done.2, f32[12,8,24,128]{3,2,1,0:T(8,128)} %copy-done, f32[12,8,24,128]{3,2,1,0:T(8,128)} %copy-done.1), custom_call_target="tpu_custom_call" | custom-call | tf_op jit(solution)/shard_map/pallas_call | solution.py:256
Async XLA Ops:
  3.1 9.7 %collective-permute-start.1 = (f32[12,8,8,128]{3,2,1,0:T(8,128)}, f32[12,8,8,128]{3,2,1,0:T(8,128)S(1)}, u32[]{:S(2)}, u32[]{:S(2)}) collective-permute-start(f32[12,8,8,128]{3,2,1,0:T(8,128)} %shard_map.77), channel_id=1, source_target_pairs={{1,0},{2,1},{3,2},{4,3},{5,4},{6,5},{7,6},{8,7},{9,8},{10,9},{11,1... | collective-permute-start | bytes 1179656 | tf_op jit(solution)/shard_map/ppermute | solution.py:109
  4.4 10.0 %collective-permute-start = (f32[12,8,8,128]{3,2,1,0:T(8,128)}, f32[12,8,8,128]{3,2,1,0:T(8,128)S(1)}, u32[]{:S(2)}, u32[]{:S(2)}) collective-permute-start(f32[12,8,8,128]{3,2,1,0:T(8,128)} %shard_map.77), channel_id=1, source_target_pairs={{0,1},{1,2},{2,3},{3,4},{4,5},{5,6},{6,7},{7,8},{8,9},{9,10},{10,1... | collective-permute-start | bytes 1179656 | tf_op jit(solution)/shard_map/ppermute | solution.py:108
  15.5 31.2 %copy-start = (f32[12,8,24,128]{3,2,1,0:T(8,128)}, f32[12,8,24,128]{3,2,1,0:T(8,128)S(1)}, u32[]{:S(2)}) copy-start(f32[12,8,24,128]{3,2,1,0:T(8,128)S(1)} %pad_maximum_fusion.mid_ref) | copy-start | bytes 3538948
  15.5 21.5 %collective-permute-start.3 = (f32[12,8,24,128]{3,2,1,0:T(8,128)S(1)}, f32[12,8,24,128]{3,2,1,0:T(8,128)S(1)}, u32[]{:S(2)}, u32[]{:S(2)}) collective-permute-start(f32[12,8,24,128]{3,2,1,0:T(8,128)S(1)} %pad_maximum_fusion.mid_ref), channel_id=1, source_target_pairs={{32,0},{64,32},{96,64},{128,96},{160,128},{192,160},{224,192},{256... | collective-permute-start | bytes 3538952 | tf_op jit(solution)/shard_map/ppermute | solution.py:305
  31.6 15.1 %collective-permute-start.2 = (f32[12,8,24,128]{3,2,1,0:T(8,128)S(1)}, f32[12,8,24,128]{3,2,1,0:T(8,128)S(1)}, u32[]{:S(2)}, u32[]{:S(2)}) collective-permute-start(f32[12,8,24,128]{3,2,1,0:T(8,128)S(1)} %pad_maximum_fusion.mid_ref), channel_id=1, source_target_pairs={{0,32},{32,64},{64,96},{96,128},{128,160},{160,192},{192,224},{224... | collective-permute-start | bytes 3538952 | tf_op jit(solution)/shard_map/ppermute | solution.py:304
  37.0 9.7 %copy-start.1 = (f32[12,8,24,128]{3,2,1,0:T(8,128)}, f32[12,8,24,128]{3,2,1,0:T(8,128)S(1)}, u32[]{:S(2)}) copy-start(f32[12,8,24,128]{3,2,1,0:T(8,128)S(1)} %collective-permute-done.3.above_ref) | copy-start | bytes 3538948
  46.7 1.0 %copy-start.2 = (f32[12,8,24,128]{3,2,1,0:T(8,128)}, f32[12,8,24,128]{3,2,1,0:T(8,128)S(1)}, u32[]{:S(2)}) copy-start(f32[12,8,24,128]{3,2,1,0:T(8,128)S(1)} %collective-permute-done.2.below_ref) | copy-start | bytes 3538948

commit v11 on v10

--- a/solution.py
+++ b/solution.py
@@ -179,7 +179,7 @@
             t = step * SUBSTEPS + sub
             lo, hi = t + 1, rows + 1 - t
 
-            def vel_row(b, carry, sub=sub):
+            def vel_row(b, carry, sub=sub, comps=(0, 1, 2)):
                 r = b - 1
                 sxx_c = sbuf[0, pl.ds(b, 1), ys, :]
                 sxx_px = sbuf[0, pl.ds(b + 1, 1), ys, :]
@@ -199,11 +199,15 @@
                 push = cbuf[0, pl.ds(r, 1), :, :]
                 active = mask_of(sub, r)
                 for c, force in enumerate((force_x, force_y, force_z)):
+                    if c not in comps:
+                        continue
                     old = vbuf[c, pl.ds(b, 1), ys, :]
                     vbuf[c, pl.ds(b, 1), ys, :] = keep(active, old + push * force, old)
                 return carry
 
-            lax.fori_loop(lo, hi, vel_row, 0, unroll=True)
+            vel_row(lo, 0, comps=(0,))
+            lax.fori_loop(lo + 1, hi - 1, vel_row, 0, unroll=True)
+            vel_row(hi - 1, 0, comps=(1, 2))
 
             def strs_row(b, carry, sub=sub):
                 r = b - 1

time: 55.2 us -> 55.1 us (level)
  no operation moved by 1% of the time
where the time goes in v11:
time: 55.1 us; the launch traced here: 54.4 us
  starting transfers between devices  24.4 us (44%)
  waiting for transfers between devices  18.1 us (33%)
  Pallas kernels  8.51 us (15%)
  between operations  1.33 us (2%)
  other arithmetic  1.08 us (2%)
  local copies, waits for them, and re-layouts  1.03 us (2%)
    ppermute x1, starting transfers between devices, per_device(): above = lax.ppermute(block, 'gx', [(i + 1, i) for i in range(count - 1)])  16.2 us
    ppermute x1, waiting for transfers between devices, per_device(): below = lax.ppermute(block, 'gx', [(i, i + 1) for i in range(count - 1)])  9.72 us
    pallas_call x1, Pallas kernels, substeps(): pl.pallas_call(substeps_kernel, out_shape=(jax.ShapeDtypeStruct((3, nx, n...  6.71 us
    ppermute x1, starting transfers between devices, with_blocks(): lax.ppermute(cells, axis, [(i, i + 1) for i in range(count - 1)])  5.01 us
    ppermute x1, waiting for transfers between devices, with_blocks(): lax.ppermute(cells, axis, [(i + 1, i) for i in range(count - 1)])  3.41 us
    ppermute x1, waiting for transfers between devices, per_device(): above = lax.ppermute(block, 'gx', [(i + 1, i) for i in range(count - 1)])  3.4 us
    ppermute x1, starting transfers between devices, per_device(): below = lax.ppermute(block, 'gx', [(i, i + 1) for i in range(count - 1)])  1.92 us
    pallas_call x1, Pallas kernels, pack(): pl.pallas_call(pack_kernel, out_shape=jax.ShapeDtypeStruct((12, nx, ny, d...  1.8 us
  transfers between devices with their start and end apart: 4, of which 4 were waited for; matrix products, arithmetic and copies ran while one was open for 0% of the time, Pallas kernels for 0%

profile of v11, /device:TPU:1, one launch (start us, length us, event | category | flops | bytes accessed | tf_op | source)
XLA Modules:
  0.0 54.4 jit_solution(16414911253560588944)
XLA Ops:
  1.3 1.8 %shard_map.77 = f32[12,8,8,128]{3,2,1,0:T(8,128)} custom-call(s32[1,1]{1,0:T(1,128)S(6)} %copy.8.e_ref, f32[3,8,8,128]{3,2,1,0:T(8,128)} %v_ref.1, f32[6,8,8,128]{3,2,1,0:T(8,128)} %s_ref.1, f32[8,8,128]{2,1,0:T(8,128)} %b_ref.1, f32[8,8,128]{2,1,0:T(8,128)} %l_ref.1, f32[8,8,128]{2,1,0:T(8,128)} %m_ref.1), custom_call_target="tpu_custom_call" | custom-call | tf_op jit(solution)/shard_map/pallas_call | solution.py:294
  3.1 1.3 %collective-permute-start.1 = (f32[12,8,8,128]{3,2,1,0:T(8,128)}, f32[12,8,8,128]{3,2,1,0:T(8,128)S(1)}, u32[]{:S(2)}, u32[]{:S(2)}) collective-permute-start(f32[12,8,8,128]{3,2,1,0:T(8,128)} %shard_map.77), channel_id=1, source_target_pairs={{1,0},{2,1},{3,2},{4,3},{5,4},{6,5},{7,6},{8,7},{9,8},{10,9},{11,1... | collective-permute-start | bytes 1179656 | tf_op jit(solution)/shard_map/ppermute | solution.py:109
  4.4 5.0 %collective-permute-start = (f32[12,8,8,128]{3,2,1,0:T(8,128)}, f32[12,8,8,128]{3,2,1,0:T(8,128)S(1)}, u32[]{:S(2)}, u32[]{:S(2)}) collective-permute-start(f32[12,8,8,128]{3,2,1,0:T(8,128)} %shard_map.77), channel_id=1, source_target_pairs={{0,1},{1,2},{2,3},{3,4},{4,5},{5,6},{6,7},{7,8},{8,9},{9,10},{10,1... | collective-permute-start | bytes 1179656 | tf_op jit(solution)/shard_map/ppermute | solution.py:108
  9.4 3.4 %collective-permute-done.1 = f32[12,8,8,128]{3,2,1,0:T(8,128)S(1)} collective-permute-done((f32[12,8,8,128]{3,2,1,0:T(8,128)}, f32[12,8,8,128]{3,2,1,0:T(8,128)S(1)}, u32[]{:S(2)}, u32[]{:S(2)}) %collective-permute-start.1) | collective-permute-done | bytes 393248 | tf_op jit(solution)/shard_map/ppermute | solution.py:109
  12.8 1.6 %collective-permute-done = f32[12,8,8,128]{3,2,1,0:T(8,128)S(1)} collective-permute-done((f32[12,8,8,128]{3,2,1,0:T(8,128)}, f32[12,8,8,128]{3,2,1,0:T(8,128)S(1)}, u32[]{:S(2)}, u32[]{:S(2)}) %collective-permute-start) | collective-permute-done | bytes 393248 | tf_op jit(solution)/shard_map/ppermute | solution.py:108
  14.4 1.1 %pad_maximum_fusion.mid_ref = f32[12,8,24,128]{3,2,1,0:T(8,128)S(1)} fusion(f32[12,8,8,128]{3,2,1,0:T(8,128)S(1)} %collective-permute-done.1, f32[12,8,8,128]{3,2,1,0:T(8,128)} %shard_map.77, f32[12,8,8,128]{3,2,1,0:T(8,128)S(1)} %collective-permute-done), kind=kLoop, calls=%fused_computation | loop fusion | flops 589824 | bytes 2359296 | tf_op jit(solution)/shard_map/concatenate | solution.py:110
  15.5 0.0 copy-start
  15.5 16.2 %collective-permute-start.3 = (f32[12,8,24,128]{3,2,1,0:T(8,128)S(1)}, f32[12,8,24,128]{3,2,1,0:T(8,128)S(1)}, u32[]{:S(2)}, u32[]{:S(2)}) collective-permute-start(f32[12,8,24,128]{3,2,1,0:T(8,128)S(1)} %pad_maximum_fusion.mid_ref), channel_id=1, source_target_pairs={{32,0},{64,32},{96,64},{128,96},{160,128},{192,160},{224,192},{256... | collective-permute-start | bytes 3538952 | tf_op jit(solution)/shard_map/ppermute | solution.py:309
  31.6 1.9 %collective-permute-start.2 = (f32[12,8,24,128]{3,2,1,0:T(8,128)S(1)}, f32[12,8,24,128]{3,2,1,0:T(8,128)S(1)}, u32[]{:S(2)}, u32[]{:S(2)}) collective-permute-start(f32[12,8,24,128]{3,2,1,0:T(8,128)S(1)} %pad_maximum_fusion.mid_ref), channel_id=1, source_target_pairs={{0,32},{32,64},{64,96},{96,128},{128,160},{160,192},{192,224},{224... | collective-permute-start | bytes 3538952 | tf_op jit(solution)/shard_map/ppermute | solution.py:308
  33.6 3.4 %collective-permute-done.3.above_ref = f32[12,8,24,128]{3,2,1,0:T(8,128)S(1)} collective-permute-done((f32[12,8,24,128]{3,2,1,0:T(8,128)S(1)}, f32[12,8,24,128]{3,2,1,0:T(8,128)S(1)}, u32[]{:S(2)}, u32[]{:S(2)}) %collective-permute-start.3) | collective-permute-done | bytes 1179680 | tf_op jit(solution)/shard_map/ppermute | solution.py:309
  37.0 0.0 copy-start.1
  37.0 9.7 %collective-permute-done.2.below_ref = f32[12,8,24,128]{3,2,1,0:T(8,128)S(1)} collective-permute-done((f32[12,8,24,128]{3,2,1,0:T(8,128)S(1)}, f32[12,8,24,128]{3,2,1,0:T(8,128)S(1)}, u32[]{:S(2)}, u32[]{:S(2)}) %collective-permute-start.2) | collective-permute-done | bytes 1179680 | tf_op jit(solution)/shard_map/ppermute | solution.py:308
  46.7 0.0 copy-done
  46.7 0.0 copy-done.1
  46.7 0.0 copy-start.2
  46.7 1.0 %copy-done.2 = f32[12,8,24,128]{3,2,1,0:T(8,128)} copy-done((f32[12,8,24,128]{3,2,1,0:T(8,128)}, f32[12,8,24,128]{3,2,1,0:T(8,128)S(1)}, u32[]{:S(2)}) %copy-start.2) | copy-done | bytes 1179672
  47.7 6.7 %shard_map.78 = (f32[3,8,8,128]{3,2,1,0:T(8,128)}, f32[6,8,8,128]{3,2,1,0:T(8,128)}) custom-call(f32[12,8,24,128]{3,2,1,0:T(8,128)} %copy-done.2, f32[12,8,24,128]{3,2,1,0:T(8,128)} %copy-done, f32[12,8,24,128]{3,2,1,0:T(8,128)} %copy-done.1), custom_call_target="tpu_custom_call" | custom-call | tf_op jit(solution)/shard_map/pallas_call | solution.py:260
Async XLA Ops:
  3.1 9.7 %collective-permute-start.1 = (f32[12,8,8,128]{3,2,1,0:T(8,128)}, f32[12,8,8,128]{3,2,1,0:T(8,128)S(1)}, u32[]{:S(2)}, u32[]{:S(2)}) collective-permute-start(f32[12,8,8,128]{3,2,1,0:T(8,128)} %shard_map.77), channel_id=1, source_target_pairs={{1,0},{2,1},{3,2},{4,3},{5,4},{6,5},{7,6},{8,7},{9,8},{10,9},{11,1... | collective-permute-start | bytes 1179656 | tf_op jit(solution)/shard_map/ppermute | solution.py:109
  4.4 10.0 %collective-permute-start = (f32[12,8,8,128]{3,2,1,0:T(8,128)}, f32[12,8,8,128]{3,2,1,0:T(8,128)S(1)}, u32[]{:S(2)}, u32[]{:S(2)}) collective-permute-start(f32[12,8,8,128]{3,2,1,0:T(8,128)} %shard_map.77), channel_id=1, source_target_pairs={{0,1},{1,2},{2,3},{3,4},{4,5},{5,6},{6,7},{7,8},{8,9},{9,10},{10,1... | collective-permute-start | bytes 1179656 | tf_op jit(solution)/shard_map/ppermute | solution.py:108
  15.5 31.2 %copy-start = (f32[12,8,24,128]{3,2,1,0:T(8,128)}, f32[12,8,24,128]{3,2,1,0:T(8,128)S(1)}, u32[]{:S(2)}) copy-start(f32[12,8,24,128]{3,2,1,0:T(8,128)S(1)} %pad_maximum_fusion.mid_ref) | copy-start | bytes 3538948
  15.5 21.5 %collective-permute-start.3 = (f32[12,8,24,128]{3,2,1,0:T(8,128)S(1)}, f32[12,8,24,128]{3,2,1,0:T(8,128)S(1)}, u32[]{:S(2)}, u32[]{:S(2)}) collective-permute-start(f32[12,8,24,128]{3,2,1,0:T(8,128)S(1)} %pad_maximum_fusion.mid_ref), channel_id=1, source_target_pairs={{32,0},{64,32},{96,64},{128,96},{160,128},{192,160},{224,192},{256... | collective-permute-start | bytes 3538952 | tf_op jit(solution)/shard_map/ppermute | solution.py:309
  31.6 15.1 %collective-permute-start.2 = (f32[12,8,24,128]{3,2,1,0:T(8,128)S(1)}, f32[12,8,24,128]{3,2,1,0:T(8,128)S(1)}, u32[]{:S(2)}, u32[]{:S(2)}) collective-permute-start(f32[12,8,24,128]{3,2,1,0:T(8,128)S(1)} %pad_maximum_fusion.mid_ref), channel_id=1, source_target_pairs={{0,32},{32,64},{64,96},{96,128},{128,160},{160,192},{192,224},{224... | collective-permute-start | bytes 3538952 | tf_op jit(solution)/shard_map/ppermute | solution.py:308
  37.0 9.7 %copy-start.1 = (f32[12,8,24,128]{3,2,1,0:T(8,128)}, f32[12,8,24,128]{3,2,1,0:T(8,128)S(1)}, u32[]{:S(2)}) copy-start(f32[12,8,24,128]{3,2,1,0:T(8,128)S(1)} %collective-permute-done.3.above_ref) | copy-start | bytes 3538948
  46.7 1.0 %copy-start.2 = (f32[12,8,24,128]{3,2,1,0:T(8,128)}, f32[12,8,24,128]{3,2,1,0:T(8,128)S(1)}, u32[]{:S(2)}) copy-start(f32[12,8,24,128]{3,2,1,0:T(8,128)S(1)} %collective-permute-done.2.below_ref) | copy-start | bytes 3538948
